TPU v7x, 32 devices: a whole 2x2x4 slice. The times are simulated.
32 devices in a mesh: dp: 4 (over y, x), expert: 8 (over z, core).
Axes of the slice: x: 2, y: 2, z: 4, core: 2. Of those that a mesh axis runs over, the one named last changes fastest.
Arguments:
- hidden: bfloat16 [32, 2048], P(('dp', 'expert')), may hold values from -6 to 6
- attn_gain: float32 [2048], replicated, may hold values from 0.25 to 1.75
- query_weight: bfloat16 [3072, 2048], P('expert'), may hold values from -0.125 to 0.125
- latent_down: bfloat16 [2048, 576], replicated, may hold values from -0.125 to 0.125
- latent_up: bfloat16 [512, 4096], P(None, 'expert'), may hold values from -0.25 to 0.25
- out_weight: bfloat16 [2048, 2048], P('expert'), may hold values from -0.125 to 0.125
- latent_pool: bfloat16 [128, 32, 576], P('dp'), may hold values from -1000 to 1000
- page_table: int32 [32, 16], replicated, may hold values from -1 to 127, as said below
- page_counts: int32 [32], replicated, may hold values from 1 to 16, as said below
- ffn_gain: float32 [2048], replicated, may hold values from 0.25 to 1.75
- expert_ids: int32 [32, 6], replicated, may hold values from 0 to 23, all different within a row; in each aligned block of 32 rows (0 to 31, 32 to 63, ...) at most 16 rows name the same one
- expert_gates: float32 [32, 6], replicated, may hold values from 0.05 to 0.6
- old_place: int32 [8, 4], replicated, may hold values from 0 to 23, as said below
- new_place: int32 [8, 4], replicated, may hold values from 0 to 23, as said below
- expert_gate_up: bfloat16 [32, 2, 1408, 2048], P('expert', None, None, 'dp'), as said below
- expert_down: bfloat16 [32, 1408, 2048], P('expert', None, 'dp'), as said below
- shared_gate_up: bfloat16 [2, 2816, 2048], P(None, None, 'dp'), may hold values from -0.125 to 0.125
- shared_down: bfloat16 [2816, 2048], P(None, 'dp'), may hold values from -0.109375 to 0.109375
Outputs:
- layer_out: bfloat16 [32, 2048], P(('dp', 'expert'))
- moved_gate_up: bfloat16 [32, 2, 1408, 2048], P('expert', None, None, 'dp')
- moved_down: bfloat16 [32, 1408, 2048], P('expert', None, 'dp')
Inputs may be any that keep to these rules, and one draw needn't show every extreme that they name: `page_counts`: each request's count of cached pages; exactly one request has 16. `page_table`: row t names page_counts[t] pages of the pool, no page named twice in the table; its other entries are -1. Page p lies on dp index p // 32. `expert_ids`: no expert is named by more than 16 tokens in all; some expert by exactly 16. `old_place`: row i holds the experts of the slots on expert index i, slot s of row i being global slot i * 4 + s; every expert is held by one slot or more. `new_place`: equal to old_place except in exactly one slot of each row, which names another expert. `expert_gate_up`: slots that hold the same expert under old_place hold equal weights. `expert_down`: slots that hold the same expert under old_place hold equal weights.
All inputs are finite; a program needn't handle non-finite values.
Results may differ from a plain program's by a relative error of at most 0.02.
Values may be sent and summed in bfloat16 or wider, within the bound.
No kernel may reach another device: no remote copies, remote signals or barrier semaphores. Data moves between devices by JAX's collectives and lax.ppermute only.
A program may use at most 128 MiB of HBM per device.

v0:
```python
import math

import jax
import jax.numpy as jnp
from jax import lax
from jax.sharding import PartitionSpec as P

NOPE = 128
ROPE = 64
VHEAD = 128
LATENT = 512
EXP_DEV = 3
PAGE = 32


EPSILON = 1e-06
ROPE_BASE = 50000.0
MASKED_SCORE = -1e30
HIGHEST = lax.Precision.HIGHEST


def rms_plain(values):
    mean_square = jnp.mean(values * values, axis=-1, keepdims=True)
    return values * lax.rsqrt(mean_square + EPSILON)


def rms_norm(values, norm_gain):
    return rms_plain(values) * norm_gain


def rotary(values, position):
    half_width = values.shape[-1] // 2
    exponent = jnp.arange(half_width).astype(jnp.float32) * (2.0 / values.shape[-1])
    frequency = jnp.exp(-exponent * math.log(ROPE_BASE))
    angles = position[..., None] * frequency
    cosine = jnp.cos(angles)
    sine_part = jnp.sin(angles)
    first_half = values[..., :half_width]
    second = values[..., half_width:]
    return jnp.concatenate(
        [first_half * cosine - second * sine_part, second * cosine + first_half * sine_part],
        axis=-1,
    )


def gather_rows(rows):
    by_expert = lax.all_gather(rows, "expert", axis=0, tiled=True)
    return lax.all_gather(by_expert, "dp", axis=0, tiled=True)


def pick_rows(table, rows):
    return jnp.stack([lax.dynamic_index_in_dim(table, rows[k], 0, False) for k in range(rows.shape[0])])


def pick_slots(gate_up, down, picks):
    return jnp.concatenate([pick_rows(gate_up, picks), pick_rows(down, picks)[:, None]], axis=1)


def spread_slots(chosen, ex_count):
    count, parts, ff_width, col_width = chosen.shape
    pieces = chosen.reshape(count, parts, ex_count, ff_width // ex_count, col_width)
    spread = lax.all_to_all(pieces, "expert", split_axis=2, concat_axis=0, tiled=True)
    return spread.reshape(ex_count * count, parts, ff_width // ex_count, col_width)


def scatter_sum(values, axis):
    count = lax.axis_size(axis)
    share = values.shape[0] // count
    gathered = lax.all_gather(values, axis, axis=0, tiled=False)
    mine = lax.dynamic_slice_in_dim(gathered, lax.axis_index(axis) * share, share, 1)
    return jnp.sum(mine, axis=0)


def sum_over(values, axis):
    return jnp.sum(lax.all_gather(values, axis, axis=0, tiled=False), axis=0)


def migrate_start(expert_gate_up, expert_down, old_place, new_place, ex_index):
    rows, slots_local = old_place.shape
    slots = rows * slots_local
    ex_count = rows
    ff_width = expert_gate_up.shape[2]
    changed = old_place != new_place
    moved_slot = jnp.argmax(changed, axis=1)
    wanted = jnp.take_along_axis(new_place, moved_slot[:, None], axis=1)[:, 0]
    hit = old_place.reshape(-1)[None, :] == wanted[:, None]
    first = jnp.argmax(hit, axis=1).astype(jnp.int32)
    last = (slots - 1 - jnp.argmax(hit[:, ::-1], axis=1)).astype(jnp.int32)
    slot_ids = jnp.arange(slots, dtype=jnp.int32)

    def needed_of(src):
        needed = jnp.any(src[:, None] == slot_ids[None, :], axis=0).reshape(rows, slots_local)
        return needed, jnp.max(jnp.sum(needed.astype(jnp.int32), axis=1))

    need_first, load_first = needed_of(first)
    need_last, load_last = needed_of(last)
    use_last = load_last < load_first
    source = jnp.where(use_last, last, first)
    needed = jnp.where(use_last, need_last, need_first)
    load = jnp.minimum(load_first, load_last)
    rank = jnp.cumsum(needed.astype(jnp.int32), axis=1) - 1
    local_ids = jnp.arange(slots_local, dtype=jnp.int32)
    picks = jnp.stack(
        [jnp.argmax(needed & (rank == k), axis=1).astype(jnp.int32) for k in range(slots_local)],
        axis=1,
    )
    my_picks = picks[ex_index]
    src_dev = source // slots_local
    src_rank = rank.reshape(-1)[source]
    fast = min(2, slots_local)
    chosen = [pick_slots(expert_gate_up, expert_down, my_picks[k:k + 1]) for k in range(fast)]
    return chosen, (my_picks, src_dev, src_rank, load, moved_slot[ex_index])


def migrate_route(spread, plan, expert_gate_up, expert_down):
    my_picks, src_dev, src_rank, load, my_moved = plan
    ex_count = src_dev.shape[0]
    slots_local = expert_gate_up.shape[0]
    fast = len(spread)
    stacked = jnp.concatenate(spread, axis=0)
    out_a = pick_rows(stacked, jnp.minimum(src_rank, fast - 1) * ex_count + src_dev)
    if slots_local > fast:
        rest = slots_local - fast

        def extra():
            spread_b = spread_slots(pick_slots(expert_gate_up, expert_down, my_picks[fast:]), ex_count)
            out_b = pick_rows(spread_b, src_dev * rest + jnp.clip(src_rank - fast, 0, rest - 1))
            return jnp.where((src_rank < fast)[:, None, None, None], out_a, out_b)

        out_a = lax.cond(load > fast, extra, lambda: out_a)
    return out_a


def deliver(outgoing):
    return lax.all_to_all(outgoing, "expert", split_axis=0, concat_axis=2, tiled=True)


def local(
    hidden,
    attn_gain,
    query_weight,
    latent_down,
    latent_up,
    out_weight,
    latent_pool,
    page_table,
    page_counts,
    ffn_gain,
    expert_ids,
    expert_gates,
    old_place,
    new_place,
    expert_gate_up,
    expert_down,
    shared_gate_up,
    shared_down,
):
    dp_count = lax.axis_size("dp")
    ex_count = lax.axis_size("expert")
    dp_index = lax.axis_index("dp")
    ex_index = lax.axis_index("expert")
    req_local = hidden.shape[0]
    group_rows = req_local * ex_count
    requests = page_counts.shape[0]
    head_local = query_weight.shape[0] // (NOPE + ROPE)
    score_scale = (NOPE + ROPE) ** (-0.5)
    group_start = dp_index * group_rows
    chosen, plan = migrate_start(expert_gate_up, expert_down, old_place, new_place, ex_index)
    everyone = gather_rows(hidden)
    everyone, chosen = lax.optimization_barrier((everyone, chosen))
    spread = [spread_slots(part, ex_count) for part in chosen]
    normed = rms_norm(everyone.astype(jnp.float32), attn_gain).astype(jnp.bfloat16)
    queries = jnp.einsum(
        "td,qd->tq", normed, query_weight, preferred_element_type=jnp.float32
    ).reshape(requests, head_local, NOPE + ROPE)
    position = (page_counts * PAGE).astype(jnp.float32)
    query_rope = rotary(queries[..., NOPE:], position[:, None]).astype(jnp.bfloat16)
    up_table = latent_up.reshape(LATENT, head_local, NOPE + VHEAD)
    query_latent = jnp.einsum(
        "thn,lhn->thl",
        queries[..., :NOPE],
        up_table[..., :NOPE].astype(jnp.float32),
        precision=HIGHEST,
    ).astype(jnp.bfloat16)
    pages_local = latent_pool.shape[0]
    pool_total = pages_local * dp_count
    flat_pages = page_table.reshape(-1)
    flat_owner = jnp.repeat(jnp.arange(requests, dtype=jnp.int32), page_table.shape[1])
    target = jnp.where(flat_pages >= 0, flat_pages, pool_total)
    owner_all = jnp.full((pool_total,), -1, jnp.int32).at[target].set(flat_owner, mode="drop")
    page_owner = lax.dynamic_slice_in_dim(owner_all, dp_index * pages_local, pages_local)
    page_used = page_owner >= 0
    owner_safe = jnp.maximum(page_owner, 0)
    page_latent = latent_pool[..., :LATENT]
    page_rope = latent_pool[..., LATENT:]
    scores = jnp.einsum(
        "phl,pkl->phk", query_latent[owner_safe], page_latent, preferred_element_type=jnp.float32
    )
    scores = (
        scores
        + jnp.einsum(
            "phr,pkr->phk", query_rope[owner_safe], page_rope, preferred_element_type=jnp.float32
        )
    ) * score_scale
    raw_max = jnp.max(scores, axis=2)
    weights = jnp.exp(scores - raw_max[..., None])
    page_total = jnp.sum(weights, axis=2)
    page_mix = jnp.einsum(
        "phk,pkl->phl",
        weights.astype(jnp.bfloat16),
        page_latent,
        preferred_element_type=jnp.float32,
    )
    page_max = jnp.where(page_used[:, None], raw_max, MASKED_SCORE)
    member = page_owner[None, :] == jnp.arange(requests, dtype=jnp.int32)[:, None]
    req_max = jnp.max(jnp.where(member[:, :, None], page_max[None], MASKED_SCORE), axis=1)
    rescale = jnp.where(page_used[:, None], jnp.exp(page_max - req_max[owner_safe]), 0.0)
    member_float = member.astype(jnp.float32)
    req_total = jnp.dot(member_float, page_total * rescale, precision=HIGHEST)
    req_mix = jnp.einsum(
        "rp,phl->rhl", member_float, page_mix * rescale[..., None], precision=HIGHEST
    )
    packed = jnp.concatenate([req_mix, req_max[..., None], req_total[..., None]], axis=-1)
    gathered = lax.all_gather(packed, "dp", axis=0, tiled=False)
    gathered = lax.dynamic_slice_in_dim(gathered, group_start, group_rows, 1)
    each_max = gathered[..., LATENT]
    part_max = jnp.max(each_max, axis=0)
    each_weight = jnp.exp(each_max - part_max[None])
    part_total = jnp.sum(gathered[..., LATENT + 1] * each_weight, axis=0)
    part_mix = jnp.sum(gathered[..., :LATENT] * each_weight[..., None], axis=0)
    own_normed = lax.dynamic_slice_in_dim(normed, group_start, group_rows, 0)
    own_position = lax.dynamic_slice_in_dim(position, group_start, group_rows, 0)
    fresh_latent = jnp.dot(own_normed, latent_down, preferred_element_type=jnp.float32)
    new_latent = rms_plain(fresh_latent[:, :LATENT]).astype(jnp.bfloat16)
    new_rope = rotary(fresh_latent[:, LATENT:], own_position).astype(jnp.bfloat16)
    own_query = lax.dynamic_slice_in_dim(query_latent, group_start, group_rows, 0)
    own_rope_query = lax.dynamic_slice_in_dim(query_rope, group_start, group_rows, 0)
    own_score = jnp.einsum("thl,tl->th", own_query, new_latent, preferred_element_type=jnp.float32)
    own_score = (
        own_score
        + jnp.einsum("thr,tr->th", own_rope_query, new_rope, preferred_element_type=jnp.float32)
    ) * score_scale
    highest = jnp.maximum(part_max, own_score)
    kept_part = jnp.exp(part_max - highest)
    own_weight = jnp.exp(own_score - highest)
    denominator = part_total * kept_part + own_weight
    numerator = (
        part_mix * kept_part[..., None]
        + own_weight[..., None] * new_latent.astype(jnp.float32)[:, None, :]
    )
    attended = (numerator / denominator[..., None]).astype(jnp.bfloat16)
    heads_out = jnp.einsum(
        "thl,lhv->thv", attended, up_table[..., NOPE:], preferred_element_type=jnp.float32
    )
    heads_out = heads_out.astype(jnp.bfloat16).reshape(group_rows, head_local * VHEAD)
    partial_value = jnp.dot(heads_out, out_weight, preferred_element_type=jnp.float32)
    partial_value, spread = lax.optimization_barrier((partial_value, spread))
    attn_out = scatter_sum(partial_value, "expert")
    residual = hidden.astype(jnp.float32) + attn_out
    normed_ffn = rms_norm(residual, ffn_gain).astype(jnp.bfloat16)
    slots_local = expert_gate_up.shape[0]
    ff_width = expert_gate_up.shape[2]
    col_width = expert_gate_up.shape[3]
    every_row = gather_rows(normed_ffn)
    outgoing = migrate_route(spread, plan, expert_gate_up, expert_down)
    every_row, outgoing = lax.optimization_barrier((every_row, outgoing))
    unit = (every_row[0, 0].astype(jnp.float32) * 0.0 + 1.0).astype(expert_gate_up.dtype)
    base_gate_up = expert_gate_up * unit
    base_down = expert_down * unit
    arrived = deliver(outgoing)
    my_columns = lax.dynamic_slice_in_dim(every_row, dp_index * col_width, col_width, 1)
    by_group = my_columns.reshape(dp_count, ex_count, req_local, col_width).transpose(1, 0, 2, 3)
    ffn_rows = by_group.reshape(requests, col_width)
    column_rows = lax.dynamic_index_in_dim(by_group, ex_index, 0, keepdims=False).reshape(
        dp_count * req_local, col_width
    )
    top_count = expert_ids.shape[1]
    experts_count = EXP_DEV * ex_count
    ids_order = (
        expert_ids.reshape(dp_count, ex_count, req_local, top_count)
        .transpose(1, 0, 2, 3)
        .reshape(requests, top_count)
    )
    gates_order = (
        expert_gates.reshape(dp_count, ex_count, req_local, top_count)
        .transpose(1, 0, 2, 3)
        .reshape(requests, top_count)
    )
    old_flat = old_place.reshape(-1)
    holds_map = old_flat[None, :] == jnp.arange(experts_count, dtype=jnp.int32)[:, None]
    holder = jnp.argmax(holds_map, axis=1)
    slot_of = holder[ids_order.reshape(-1)]
    capacity = 2 * requests * top_count // experts_count
    local_slot = slot_of - ex_index * slots_local
    slot_hot = local_slot[:, None] == jnp.arange(slots_local, dtype=jnp.int32)[None, :]
    slot_rank = jnp.cumsum(slot_hot.astype(jnp.int32), axis=0) - 1
    position_in = jnp.where(slot_hot, slot_rank, capacity)
    route_hot = (
        position_in[:, :, None] == jnp.arange(capacity, dtype=jnp.int32)[None, None, :]
    ).astype(jnp.float32)
    route_hot = route_hot.reshape(requests, top_count, slots_local, capacity)
    dispatch = jnp.sum(route_hot, axis=1).astype(jnp.bfloat16)
    combine = jnp.sum(route_hot * gates_order[:, :, None, None], axis=1)
    slot_inputs = jnp.einsum(
        "tsc,td->scd", dispatch, ffn_rows, preferred_element_type=jnp.float32
    ).astype(jnp.bfloat16)
    routed_part = jnp.einsum(
        "scd,sgfd->sgcf", slot_inputs, expert_gate_up, preferred_element_type=jnp.float32
    )
    shared_part = jnp.einsum(
        "td,gfd->gtf", column_rows, shared_gate_up, preferred_element_type=jnp.float32
    )
    routed_sum, shared_sum = sum_over(routed_part, "dp"), sum_over(shared_part, "dp")
    activated = (jax.nn.silu(routed_sum[:, 0]) * routed_sum[:, 1]).astype(jnp.bfloat16)
    slot_out = jnp.einsum(
        "scf,sfd->scd", activated, expert_down, preferred_element_type=jnp.float32
    )
    routed = jnp.einsum("tsc,scd->td", combine, slot_out, precision=HIGHEST)
    shared_act = (jax.nn.silu(shared_sum[0]) * shared_sum[1]).astype(jnp.bfloat16)
    shared_term = jnp.dot(shared_act, shared_down, preferred_element_type=jnp.float32)
    routed, arrived = lax.optimization_barrier((routed, arrived))
    moe_rows = scatter_sum(routed, "expert")
    moe_part = lax.all_to_all(moe_rows + shared_term, "dp", split_axis=0, concat_axis=1, tiled=True)
    layer_out = (residual + moe_part).astype(jnp.bfloat16)
    my_moved = plan[-1]
    moved_gate_up = lax.dynamic_update_index_in_dim(base_gate_up, arrived[0, :2], my_moved, 0)
    moved_down = lax.dynamic_update_index_in_dim(base_down, arrived[0, 2], my_moved, 0)
    return (layer_out, moved_gate_up, moved_down)


def solution(mesh):
    in_specs = (
        P(("dp", "expert"), None),
        P(),
        P("expert", None),
        P(),
        P(None, "expert"),
        P("expert", None),
        P("dp", None, None),
        P(),
        P(),
        P(),
        P(),
        P(),
        P(),
        P(),
        P("expert", None, None, "dp"),
        P("expert", None, "dp"),
        P(None, None, "dp"),
        P(None, "dp"),
    )
    out_specs = (P(("dp", "expert"), None), P("expert", None, None, "dp"), P("expert", None, "dp"))
    return jax.shard_map(local, mesh=mesh, in_specs=in_specs, out_specs=out_specs, check_vma=False)
```

profile of v0, /device:TPU:0, one launch (start us, length us, event | category | flops | bytes accessed | tf_op | source)
XLA Modules:
  0.0 450.5 jit_solution(3862399786021227322)
XLA Ops:
  7.2 0.9 copy.148
  8.2 1.2 iota_reduce_fusion.7
  9.5 1.3 gather_fusion.4
  21.4 15.9 %all-gather.5 = bf16[8,1,2048]{2,1,0:T(2,128)(2,1)S(1)} all-gather(bf16[1,1,2048]{2,1,0:T(2,128)(2,1)} %bitcast.260), channel_id=1, replica_groups=mesh['dp'=4,'expert'=8] {'expert'}, dimensions={0}, use_global_device_ids=true | all-gather | bytes 36864 | tf_op jit(solution)/shard_map/all_gather | solution.py:47
  37.3 8.5 %all_gather.43 = bf16[32,2048]{1,0:T(8,128)(2,1)S(1)} all-gather(bf16[8,2048]{1,0:T(8,128)(2,1)S(1)} %bitcast.258), channel_id=1, replica_groups=mesh['dp'=4,'expert'=8] {'dp'}, dimensions={0}, use_global_device_ids=true | all-gather | bytes 163840 | tf_op jit(solution)/shard_map/all_gather | solution.py:48
  47.0 2.0 dynamic-slice_bitcast_fusion
  49.1 3.1 constant_dynamic-slice_fusion.8
  52.5 2.4 pad_maximum_fusion.4
  55.0 2.3 copy.161
  57.3 4.8 %all-to-all-start.1 = ((bf16[1,3,8,176,512]{4,3,1,0,2:T(8,128)(2,1)}), bf16[1,3,8,176,512]{4,3,1,0,2:T(8,128)(2,1)}, u32[]{:S(2)}, u32[]{:S(2)}) async-start(bf16[1,3,8,176,512]{4,3,1,0,2:T(8,128)(2,1)} %copy.161), calls=%async_computation.1 | async-start | bytes 8650752 | tf_op jit(solution)/shard_map/all_to_all | solution.py:62
  76.2 1.3 copy.150
  77.5 4.8 %copy.162 = bf16[1,3,8,176,512]{4,3,1,0,2:T(8,128)(2,1)} copy(bf16[1,3,8,176,512]{4,3,2,1,0:T(8,128)(2,1)} %bitcast.246) | data formatting | bytes 8650752 | tf_op jit(solution)/shard_map/reshape | solution.py:61
  82.4 76.6 %all-to-all-done.1 = bf16[1,3,8,176,512]{4,3,1,0,2:T(8,128)(2,1)} async-done(((bf16[1,3,8,176,512]{4,3,1,0,2:T(8,128)(2,1)}), bf16[1,3,8,176,512]{4,3,1,0,2:T(8,128)(2,1)}, u32[]{:S(2)}, u32[]{:S(2)}) %all-to-all-start.1) | async-done | bytes 4325408 | tf_op jit(solution)/shard_map/all_to_all | solution.py:62
  159.0 4.6 %all-to-all-start.2 = ((bf16[1,3,8,176,512]{4,3,1,0,2:T(8,128)(2,1)}), bf16[1,3,8,176,512]{4,3,1,0,2:T(8,128)(2,1)}, u32[]{:S(2)}, u32[]{:S(2)}) async-start(bf16[1,3,8,176,512]{4,3,1,0,2:T(8,128)(2,1)} %copy.162), calls=%async_computation.2 | async-start | bytes 8650752 | tf_op jit(solution)/shard_map/all_to_all | solution.py:62
  164.4 2.0 fusion.92
  168.3 2.4 scatter_custom_fusion
  173.3 1.6 fusion.5
  174.9 1.3 fusion.91
  178.4 1.5 convolution_multiply_fusion
  180.3 11.6 %all-gather = f32[128,2,514]{2,0,1:T(8,128)S(1)} all-gather(f32[32,2,514]{2,0,1:T(8,128)S(1)} %pad_maximum_fusion.5), channel_id=2, replica_groups=mesh['dp'=4,'expert'=8] {'dp'}, dimensions={0}, use_global_device_ids=true | all-gather | bytes 657920 | tf_op jit(solution)/shard_map/all_gather | solution.py:224
  192.5 2.5 copy.185
  196.6 3.0 multiply_reduce_fusion
  200.7 2.4 fusion.25
  210.4 1.8 fusion.7
  212.2 48.2 %all-to-all-done.2 = bf16[1,3,8,176,512]{4,3,1,0,2:T(8,128)(2,1)} async-done(((bf16[1,3,8,176,512]{4,3,1,0,2:T(8,128)(2,1)}), bf16[1,3,8,176,512]{4,3,1,0,2:T(8,128)(2,1)}, u32[]{:S(2)}, u32[]{:S(2)}) %all-to-all-start.2) | async-done | bytes 4325408 | tf_op jit(solution)/shard_map/all_to_all | solution.py:62
  260.4 15.1 %all-gather.1 = f32[64,2048]{1,0:T(8,128)S(1)} all-gather(f32[8,2048]{1,0:T(8,128)S(1)} %fusion.7), channel_id=3, replica_groups=mesh['dp'=4,'expert'=8] {'expert'}, dimensions={0}, use_global_device_ids=true | all-gather | bytes 589824 | tf_op jit(solution)/shard_map/all_gather | solution.py:69
  277.0 14.0 %all-gather.6 = bf16[8,1,2048]{2,1,0:T(2,128)(2,1)S(1)} all-gather(bf16[1,1,2048]{2,1,0:T(2,128)(2,1)S(1)} %convert_bitcast_fusion), channel_id=1, replica_groups=mesh['dp'=4,'expert'=8] {'expert'}, dimensions={0}, use_global_device_ids=true | all-gather | bytes 36864 | tf_op jit(solution)/shard_map/all_gather | solution.py:47
  291.0 8.4 %all_gather.49 = bf16[32,2048]{1,0:T(8,128)(2,1)S(1)} all-gather(bf16[8,2048]{1,0:T(8,128)(2,1)S(1)} %bitcast.259), channel_id=1, replica_groups=mesh['dp'=4,'expert'=8] {'dp'}, dimensions={0}, use_global_device_ids=true | all-gather | bytes 163840 | tf_op jit(solution)/shard_map/all_gather | solution.py:48
  299.4 2.5 constant_dynamic-update-slice_fusion.1
  301.9 2.8 constant_dynamic-update-slice_fusion
  311.6 4.6 %all-to-all-start.3 = ((bf16[8,3,176,512]{3,2,1,0:T(8,128)(2,1)}), bf16[8,3,176,512]{3,2,1,0:T(8,128)(2,1)}, u32[]{:S(2)}, u32[]{:S(2)}) async-start(bf16[8,3,176,512]{3,2,1,0:T(8,128)(2,1)} %get-tuple-element.195), calls=%async_computation.3 | async-start | bytes 8650752 | tf_op jit(solution)/shard_map/all_to_all | solution.py:135
  318.2 4.3 compare_select_fusion.3
  322.6 10.5 %select_subtract_fusion = s32[192]{0:T(256)S(1)} fusion(pred[192]{0:T(512)(128)(4,1)S(1)} %get-tuple-element.116, pred[192]{0:T(512)(128)(4,1)S(1)} %get-tuple-element.115, pred[192]{0:T(512)(128)(4,1)S(1)} %get-tuple-element.114, pred[192]{0:T(512)(128)(4,1)S(1)} %get-tuple-element.113, pred[192]{0:T(512)(128)(4,1)S(1)} %get-tuple-element.112, ...), kind=kLoop, calls=%fused_computation.225 | loop fusion | flops 3456 | bytes 4872 | tf_op jit(solution)/shard_map/sub | solution.py:294
  333.2 1.2 reduce-window.6
  335.4 6.9 %convolution_bitcast_fusion.1 = f32[4,2,16,1408]{3,2,1,0:T(8,128)} fusion(bf16[4,2,1408,512]{3,2,1,0:T(8,128)(2,1)} %param.34, bf16[32,512,1]{1,0,2:T(8,128)(2,1)S(1)} %reshape.551, bf16[32,4,16]{0,2,1:T(8,128)(2,1)S(1)} %get-tuple-element.98), kind=kOutput, calls=%fused_computation.30 | convolution fusion | flops 186679296 | bytes 12292096 | tf_op jit(solution)/shard_map/scd,sgfd->sgcf/dot_general | solution.py:307
  345.4 4.2 convolution_bitcast_fusion
  349.6 11.9 %all-gather.4 = f32[8,4,2816]{2,1,0:T(4,128)S(1)} all-gather(f32[2,4,2816]{2,1,0:T(4,128)S(1)} %convolution_bitcast_fusion), channel_id=6, replica_groups=mesh['dp'=4,'expert'=8] {'dp'}, dimensions={0}, use_global_device_ids=true | all-gather | bytes 450560 | tf_op jit(solution)/shard_map/all_gather | solution.py:75
  362.3 5.5 %broadcast_multiply_fusion.1 = bf16[4,1408,512]{2,1,0:T(8,128)(2,1)} fusion(bf16[4,1408,512]{2,1,0:T(8,128)(2,1)} %param.35, bf16[]{:T(256)} %bitcast.114), kind=kLoop, calls=%fused_computation.28 | loop fusion | flops 2883584 | bytes 11534338 | tf_op jit(solution)/shard_map/mul | solution.py:269
  367.8 9.9 %broadcast_multiply_fusion = bf16[4,2,1408,512]{3,2,1,0:T(8,128)(2,1)} fusion(bf16[4,2,1408,512]{3,2,1,0:T(8,128)(2,1)} %param.34, bf16[]{:T(256)} %bitcast.114), kind=kLoop, calls=%fused_computation.24 | loop fusion | flops 5767168 | bytes 23068674 | tf_op jit(solution)/shard_map/mul | solution.py:268
  377.7 9.8 %all-gather.9.cloned.1.call-done = f32[16,2,16,1408]{3,2,1,0:T(8,128)} async-done(((f32[4,2,16,1408]{3,2,1,0:T(8,128)}), f32[16,2,16,1408]{3,2,1,0:T(8,128)}) %all-gather.9.cloned.1.call-update) | async-done | bytes 2883600 | tf_op jit(solution)/shard_map/all_gather | solution.py:75
  387.5 2.9 reduce_sum.140
  390.4 3.7 fusion.17
  394.4 18.5 %all-to-all-done.3 = bf16[8,3,176,512]{3,2,1,0:T(8,128)(2,1)} async-done(((bf16[8,3,176,512]{3,2,1,0:T(8,128)(2,1)}), bf16[8,3,176,512]{3,2,1,0:T(8,128)(2,1)}, u32[]{:S(2)}, u32[]{:S(2)}) %all-to-all-start.3) | async-done | bytes 4325408 | tf_op jit(solution)/shard_map/all_to_all | solution.py:135
  413.0 4.6 %copy.171 = bf16[1,3,8,176,512]{4,3,2,1,0:T(8,128)(2,1)} copy(bf16[1,3,8,176,512]{4,3,1,2,0:T(8,128)(2,1)} %bitcast.105) | data formatting | bytes 8650752 | tf_op jit(solution)/shard_map/all_to_all | solution.py:135
  417.6 14.9 %all-gather.3 = f32[256,512]{1,0:T(8,128)S(1)} all-gather(f32[32,512]{1,0:T(8,128)S(1)} %convolution_bitcast_fusion.2), channel_id=5, replica_groups=mesh['dp'=4,'expert'=8] {'expert'}, dimensions={0}, use_global_device_ids=true | all-gather | bytes 589824 | tf_op jit(solution)/shard_map/all_gather | solution.py:69
  433.6 3.2 all-to-all-start.4
  436.9 3.6 slice_dynamic-update-slice_fusion
  440.5 2.6 bitcast_dynamic-update-slice_fusion
  (190 shorter events, 37.5 us)
Async XLA Ops:
  7.2 425.4 %copy-start = (bf16[2816,512]{1,0:T(8,128)(2,1)S(1)}, bf16[2816,512]{1,0:T(8,128)(2,1)}, u32[]{:S(2)}) copy-start(bf16[2816,512]{1,0:T(8,128)(2,1)} %param.37) | copy-start | bytes 8650756
  8.2 4.3 copy-start.12
  9.4 7.5 %copy-start.20 = (s32[8]{0:T(128)}, s32[8]{0:T(128)S(1)}, u32[]{:S(2)}) copy-start(s32[8]{0:T(128)S(1)} %get-tuple-element.44) | copy-start | bytes 100
  57.3 18.0 %copy-start.15 = (s32[32,6]{0,1:T(8,128)S(1)}, s32[32,6]{0,1:T(8,128)}, u32[]{:S(2)}) copy-start(s32[32,6]{0,1:T(8,128)} %param.30) | copy-start | bytes 2308
  57.3 101.7 %all-to-all-start.1 = ((bf16[1,3,8,176,512]{4,3,1,0,2:T(8,128)(2,1)}), bf16[1,3,8,176,512]{4,3,1,0,2:T(8,128)(2,1)}, u32[]{:S(2)}, u32[]{:S(2)}) async-start(bf16[1,3,8,176,512]{4,3,1,0,2:T(8,128)(2,1)} %copy.161), calls=%async_computation.1 | async-start | bytes 8650752 | tf_op jit(solution)/shard_map/all_to_all | solution.py:62
  64.1 11.2 %copy-start.18 = (s32[8]{0:T(128)}, s32[8]{0:T(128)S(1)}, u32[]{:S(2)}) copy-start(s32[8]{0:T(128)S(1)} %gather_fusion.3) | copy-start | bytes 100
  77.5 89.0 %copy-start.2 = (bf16[512,512]{0,1:T(8,128)(2,1)}, bf16[512,512]{0,1:T(8,128)(2,1)S(1)}, u32[]{:S(2)}) copy-start(bf16[512,512]{0,1:T(8,128)(2,1)S(1)} %copy.150) | copy-start | bytes 1572868
  82.4 81.2 %copy-start.10 = (f32[2048]{0:T(1024)S(1)}, f32[2048]{0:T(1024)}, u32[]{:S(2)}) copy-start(f32[2048]{0:T(1024)} %param.21) | copy-start | bytes 24580
  159.0 101.4 %all-to-all-start.2 = ((bf16[1,3,8,176,512]{4,3,1,0,2:T(8,128)(2,1)}), bf16[1,3,8,176,512]{4,3,1,0,2:T(8,128)(2,1)}, u32[]{:S(2)}, u32[]{:S(2)}) async-start(bf16[1,3,8,176,512]{4,3,1,0,2:T(8,128)(2,1)} %copy.162), calls=%async_computation.2 | async-start | bytes 8650752 | tf_op jit(solution)/shard_map/all_to_all | solution.py:62
  163.7 0.7 copy-start.3
  166.7 0.6 copy-start.4
  171.6 8.6 %copy-start.17 = (f32[32]{0:T(128)}, f32[32]{0:T(128)S(1)}, u32[]{:S(2)}) copy-start(f32[32]{0:T(128)S(1)} %multiply_exponential_fusion) | copy-start | bytes 388
  172.5 0.7 copy-start.6
  172.5 3.9 copy-start.8
  195.0 80.6 %copy-start.5 = (bf16[1,2048]{1,0:T(2,128)(2,1)S(1)}, bf16[1,2048]{1,0:T(2,128)(2,1)}, u32[]{:S(2)}) copy-start(bf16[1,2048]{1,0:T(2,128)(2,1)} %param.20) | copy-start | bytes 12292
  195.7 8.3 %copy-start.7 = (bf16[32,2,32]{2,1,0:T(2,128)(2,1)S(1)}, bf16[32,2,32]{2,1,0:T(2,128)(2,1)}, u32[]{:S(2)}) copy-start(bf16[32,2,32]{2,1,0:T(2,128)(2,1)} %copy-done.6) | copy-start | bytes 12292
  195.7 8.3 %copy-start.9 = (bf16[32,2,32]{2,1,0:T(2,128)(2,1)S(1)}, bf16[32,2,32]{2,1,0:T(2,128)(2,1)}, u32[]{:S(2)}) copy-start(bf16[32,2,32]{2,1,0:T(2,128)(2,1)} %copy-done.8) | copy-start | bytes 12292
  195.7 81.3 %copy-start.11 = (f32[2048]{0:T(1024)S(1)}, f32[2048]{0:T(1024)}, u32[]{:S(2)}) copy-start(f32[2048]{0:T(1024)} %param.29) | copy-start | bytes 24580
  304.7 6.8 %copy-start.19 = (s32[8]{0:T(128)S(1)}, s32[8]{0:T(128)}, u32[]{:S(2)}) copy-start(s32[8]{0:T(128)} %copy-done.18) | copy-start | bytes 100
  304.7 6.8 %copy-start.22 = (s32[8]{0:T(128)S(1)}, s32[8]{0:T(128)}, u32[]{:S(2)}) copy-start(s32[8]{0:T(128)} %get-tuple-element.118) | copy-start | bytes 100
  311.5 4.6 %copy-start.13 = (s32[32]{0:T(128)S(1)}, s32[32]{0:T(128)}, u32[]{:S(2)}) copy-start(s32[32]{0:T(128)} %copy-done.12) | copy-start | bytes 388
  311.5 6.7 %copy-start.14 = (s32[192,1]{0,1:T(1,128)S(1)}, s32[192,1]{0,1:T(1,128)}, u32[]{:S(2)}) copy-start(s32[192,1]{0,1:T(1,128)} %reshape_reshape.3) | copy-start | bytes 2308
  311.6 23.5 %copy-start.16 = (f32[32,6]{0,1:T(8,128)S(1)}, f32[32,6]{0,1:T(8,128)}, u32[]{:S(2)}) copy-start(f32[32,6]{0,1:T(8,128)} %param.31) | copy-start | bytes 2308
  311.6 101.4 %all-to-all-start.3 = ((bf16[8,3,176,512]{3,2,1,0:T(8,128)(2,1)}), bf16[8,3,176,512]{3,2,1,0:T(8,128)(2,1)}, u32[]{:S(2)}, u32[]{:S(2)}) async-start(bf16[8,3,176,512]{3,2,1,0:T(8,128)(2,1)} %get-tuple-element.195), calls=%async_computation.3 | async-start | bytes 8650752 | tf_op jit(solution)/shard_map/all_to_all | solution.py:135
  316.1 71.4 %all-gather.9.cloned.1.call-start = ((), (), s32[]{:S(2)}) async-start(), calls=%async_computation.5 | async-start | bytes 3604480 | tf_op jit(solution)/shard_map/all_gather | solution.py:75
  335.4 6.9 %copy-start.21 = (s32[8]{0:T(128)S(1)}, s32[8]{0:T(128)}, u32[]{:S(2)}) copy-start(s32[8]{0:T(128)} %copy-done.20) | copy-start | bytes 100
  433.6 9.4 %all-to-all-start.4 = ((f32[4,1,512]{2,1,0:T(1,128)}), f32[4,1,512]{2,1,0:T(1,128)S(1)}, u32[]{:S(2)}, u32[]{:S(2)}) async-start(f32[4,1,512]{2,1,0:T(1,128)} %copy.172), calls=%async_computation.4 | async-start | bytes 16384 | tf_op jit(solution)/shard_map/all_to_all | solution.py:323
Sparse Core Ops, SparseCore 0:
  342.5 45.0 all-gather.8
where the time goes:
time: 453 us; the launch traced here: 450 us
  waiting for transfers between devices  153 us (34%)
  blocking collectives  100 us (22%)
  local copies, waits for them, and re-layouts  59.6 us (13%)
  other arithmetic  54 us (12%)
  between operations  39.3 us (9%)
  matrix products  27 us (6%)
  starting transfers between devices  17.2 us (4%)
    all_to_all x2, waiting for transfers between devices, spread_slots(): lax.all_to_all(pieces, 'expert', split_axis=2, concat_axis=0, tiled=True)  125 us
    all_gather x2, blocking collectives, scatter_sum(): gathered = lax.all_gather(values, axis, axis=0, tiled=False)  30 us
    all_gather x2, blocking collectives, gather_rows(): by_expert = lax.all_gather(rows, 'expert', axis=0, tiled=True)  29.8 us
    all_to_all x1, waiting for transfers between devices, deliver(): lax.all_to_all(outgoing, 'expert', split_axis=0, concat_axis=2, tiled=True)  18.5 us
    unnamed x62, local copies, waits for them, and re-layouts  17.1 us
    all_gather x2, blocking collectives, gather_rows(): return lax.all_gather(by_expert, 'dp', axis=0, tiled=True)  16.9 us
    all_gather x1, blocking collectives, sum_over(): return jnp.sum(lax.all_gather(values, axis, axis=0, tiled=False), axis=0)  11.9 us
    all_gather x1, blocking collectives, local(): gathered = lax.all_gather(packed, 'dp', axis=0, tiled=False)  11.6 us
  transfers between devices with their start and end apart: 5, of which 4 were waited for; matrix products, arithmetic and copies ran while one was open for 22% of the time, Pallas kernels for 0%

commit v1 on v0

--- a/solution.py
+++ b/solution.py
@@ -108,7 +108,7 @@
     src_dev = source // slots_local
     src_rank = rank.reshape(-1)[source]
     fast = min(2, slots_local)
-    chosen = [pick_slots(expert_gate_up, expert_down, my_picks[k:k + 1]) for k in range(fast)]
+    chosen = pick_slots(expert_gate_up, expert_down, my_picks[:fast])
     return chosen, (my_picks, src_dev, src_rank, load, moved_slot[ex_index])
 
 
@@ -116,9 +116,8 @@
     my_picks, src_dev, src_rank, load, my_moved = plan
     ex_count = src_dev.shape[0]
     slots_local = expert_gate_up.shape[0]
-    fast = len(spread)
-    stacked = jnp.concatenate(spread, axis=0)
-    out_a = pick_rows(stacked, jnp.minimum(src_rank, fast - 1) * ex_count + src_dev)
+    fast = spread.shape[0] // ex_count
+    out_a = pick_rows(spread, src_dev * fast + jnp.minimum(src_rank, fast - 1))
     if slots_local > fast:
         rest = slots_local - fast
 
@@ -168,7 +167,7 @@
     chosen, plan = migrate_start(expert_gate_up, expert_down, old_place, new_place, ex_index)
     everyone = gather_rows(hidden)
     everyone, chosen = lax.optimization_barrier((everyone, chosen))
-    spread = [spread_slots(part, ex_count) for part in chosen]
+    spread = spread_slots(chosen, ex_count)
     normed = rms_norm(everyone.astype(jnp.float32), attn_gain).astype(jnp.bfloat16)
     queries = jnp.einsum(
         "td,qd->tq", normed, query_weight, preferred_element_type=jnp.float32
@@ -255,13 +254,15 @@
     heads_out = heads_out.astype(jnp.bfloat16).reshape(group_rows, head_local * VHEAD)
     partial_value = jnp.dot(heads_out, out_weight, preferred_element_type=jnp.float32)
     partial_value, spread = lax.optimization_barrier((partial_value, spread))
-    attn_out = scatter_sum(partial_value, "expert")
-    residual = hidden.astype(jnp.float32) + attn_out
-    normed_ffn = rms_norm(residual, ffn_gain).astype(jnp.bfloat16)
+    attn_group = jnp.sum(lax.all_gather(partial_value, "expert", axis=0, tiled=False), axis=0)
+    group_hidden = lax.dynamic_slice_in_dim(everyone, group_start, group_rows, 0)
+    group_residual = group_hidden.astype(jnp.float32) + attn_group
+    residual = lax.dynamic_slice_in_dim(group_residual, ex_index * req_local, req_local, 0)
+    normed_group = rms_norm(group_residual, ffn_gain).astype(jnp.bfloat16)
     slots_local = expert_gate_up.shape[0]
     ff_width = expert_gate_up.shape[2]
     col_width = expert_gate_up.shape[3]
-    every_row = gather_rows(normed_ffn)
+    every_row = lax.all_gather(normed_group, "dp", axis=0, tiled=True)
     outgoing = migrate_route(spread, plan, expert_gate_up, expert_down)
     every_row, outgoing = lax.optimization_barrier((every_row, outgoing))
     unit = (every_row[0, 0].astype(jnp.float32) * 0.0 + 1.0).astype(expert_gate_up.dtype)

time: 453 us -> 440 us (0.971)
  waiting for transfers between devices: 153 us -> 126 us
  local copies, waits for them, and re-layouts: 59.6 us -> 78.4 us
  blocking collectives: 100 us -> 86.3 us
  other arithmetic: 54 us -> 64.1 us
    all_to_all x2 -> x1, waiting for transfers between devices: 125 us -> 97.9 us  [spread_slots(): lax.all_to_all(pieces, 'expert', split_axis=2, concat_axis=0, tiled=True)]
    all_gather x0 -> x2, blocking collectives: none -> 23.5 us  [the longest x1 14.9 us: local(): lax.all_gather(partial_value, 'expert', axis=0, tiled=False)]
    all_gather x2 -> x1, blocking collectives: 30 us -> 14.9 us  [scatter_sum(): gathered = lax.all_gather(values, axis, axis=0, tiled=False)]
    all_gather x2 -> x1, blocking collectives: 29.8 us -> 15.9 us  [gather_rows(): by_expert = lax.all_gather(rows, 'expert', axis=0, tiled=True)]
    all_gather x2 -> x1, blocking collectives: 16.9 us -> 8.47 us  [gather_rows(): return lax.all_gather(by_expert, 'dp', axis=0, tiled=True)]
    unnamed x62 -> x74, local copies, waits for them, and re-layouts: 17.1 us -> 25.3 us
    all_to_all x2 -> x1, starting transfers between devices: 9.36 us -> 5.1 us  [spread_slots(): lax.all_to_all(pieces, 'expert', split_axis=2, concat_axis=0, tiled=True)]
  transfers between devices with their start and end apart: 5 -> 4, of which waited for: 4 -> 3; matrix products, arithmetic and copies ran while one was open for 22% -> 27% of each run, Pallas kernels for 0% -> 0%
where the time goes in v1:
time: 440 us; the launch traced here: 437 us
  waiting for transfers between devices  126 us (29%)
  blocking collectives  86.3 us (20%)
  local copies, waits for them, and re-layouts  78.4 us (18%)
  other arithmetic  64.1 us (15%)
  between operations  38.1 us (9%)
  matrix products  30.9 us (7%)
  starting transfers between devices  13 us (3%)
    all_to_all x1, waiting for transfers between devices, spread_slots(): lax.all_to_all(pieces, 'expert', split_axis=2, concat_axis=0, tiled=True)  97.9 us
    unnamed x74, local copies, waits for them, and re-layouts  25.3 us
    all_to_all x1, waiting for transfers between devices, deliver(): lax.all_to_all(outgoing, 'expert', split_axis=0, concat_axis=2, tiled=True)  18.2 us
    all_gather x1, blocking collectives, gather_rows(): by_expert = lax.all_gather(rows, 'expert', axis=0, tiled=True)  15.9 us
    all_gather x1, blocking collectives, local(): lax.all_gather(partial_value, 'expert', axis=0, tiled=False)  14.9 us
    all_gather x1, blocking collectives, scatter_sum(): gathered = lax.all_gather(values, axis, axis=0, tiled=False)  14.9 us
    all_gather x1, blocking collectives, sum_over(): return jnp.sum(lax.all_gather(values, axis, axis=0, tiled=False), axis=0)  11.9 us
    all_gather x1, blocking collectives, local(): gathered = lax.all_gather(packed, 'dp', axis=0, tiled=False)  11.6 us
  transfers between devices with their start and end apart: 4, of which 3 were waited for; matrix products, arithmetic and copies ran while one was open for 27% of the time, Pallas kernels for 0%

profile of v1, /device:TPU:0, one launch (start us, length us, event | category | flops | bytes accessed | tf_op | source)
XLA Modules:
  0.0 436.7 jit_solution(2396777572764559732)
XLA Ops:
  21.8 15.9 %all-gather.5 = bf16[8,1,2048]{2,1,0:T(2,128)(2,1)S(1)} all-gather(bf16[1,1,2048]{2,1,0:T(2,128)(2,1)} %bitcast.250), channel_id=1, replica_groups=mesh['dp'=4,'expert'=8] {'expert'}, dimensions={0}, use_global_device_ids=true | all-gather | bytes 36864 | tf_op jit(solution)/shard_map/all_gather | solution.py:47
  37.7 8.5 %all_gather.40 = bf16[32,2048]{1,0:T(8,128)(2,1)S(1)} all-gather(bf16[8,2048]{1,0:T(8,128)(2,1)S(1)} %bitcast.244), channel_id=1, replica_groups=mesh['dp'=4,'expert'=8] {'dp'}, dimensions={0}, use_global_device_ids=true | all-gather | bytes 163840 | tf_op jit(solution)/shard_map/all_gather | solution.py:48
  47.3 2.0 constant_dynamic-slice_fusion.9
  49.3 3.1 constant_dynamic-slice_fusion.11
  52.7 3.9 pad_maximum_fusion.3
  56.5 7.6 %copy.193 = bf16[2,3,8,176,512]{4,3,1,0,2:T(8,128)(2,1)} copy(bf16[2,3,8,176,512]{4,3,2,1,0:T(8,128)(2,1)} %bitcast.231) | data formatting | bytes 17301504 | tf_op jit(solution)/shard_map/reshape | solution.py:61
  64.1 5.1 %all-to-all-start.1 = ((bf16[2,3,8,176,512]{4,3,1,0,2:T(8,128)(2,1)}), bf16[2,3,8,176,512]{4,3,1,0,2:T(8,128)(2,1)}, u32[]{:S(2)}, u32[]{:S(2)}) async-start(bf16[2,3,8,176,512]{4,3,1,0,2:T(8,128)(2,1)} %copy.193), calls=%async_computation.1 | async-start | bytes 17301504 | tf_op jit(solution)/shard_map/all_to_all | solution.py:62
  85.4 2.6 fusion.92
  88.0 1.5 reshape.365
  94.6 2.6 scatter_custom_fusion
  98.4 2.1 gather_fusion
  104.8 1.6 fusion.5
  106.5 1.9 fusion.91
  121.4 1.6 convolution_multiply_fusion
  124.8 11.6 %all-gather = f32[128,2,514]{2,0,1:T(8,128)S(1)} all-gather(f32[32,2,514]{2,0,1:T(8,128)S(1)} %pad_maximum_fusion.4), channel_id=2, replica_groups=mesh['dp'=4,'expert'=8] {'dp'}, dimensions={0}, use_global_device_ids=true | all-gather | bytes 657920 | tf_op jit(solution)/shard_map/all_gather | solution.py:223
  137.8 2.5 copy.215
  140.3 1.5 fusion.84
  142.6 3.0 multiply_reduce_fusion
  147.3 2.4 fusion.25
  159.0 1.8 fusion.7
  160.8 97.9 %all-to-all-done.1 = bf16[2,3,8,176,512]{4,3,1,0,2:T(8,128)(2,1)} async-done(((bf16[2,3,8,176,512]{4,3,1,0,2:T(8,128)(2,1)}), bf16[2,3,8,176,512]{4,3,1,0,2:T(8,128)(2,1)}, u32[]{:S(2)}, u32[]{:S(2)}) %all-to-all-start.1) | async-done | bytes 8650784 | tf_op jit(solution)/shard_map/all_to_all | solution.py:62
  258.7 14.9 %all-gather.1 = f32[64,2048]{1,0:T(8,128)S(1)} all-gather(f32[8,2048]{1,0:T(8,128)S(1)} %fusion.7), channel_id=3, replica_groups=mesh['dp'=4,'expert'=8] {'expert'}, dimensions={0}, use_global_device_ids=true | all-gather | bytes 589824 | tf_op jit(solution)/shard_map/all_gather | solution.py:257
  273.9 8.6 %all_gather.45 = bf16[32,2048]{1,0:T(8,128)(2,1)S(1)} all-gather(bf16[8,2048]{1,0:T(8,128)(2,1)S(1)} %multiply_convert_fusion), channel_id=1, replica_groups=mesh['dp'=4,'expert'=8] {'dp'}, dimensions={0}, use_global_device_ids=true | all-gather | bytes 163840 | tf_op jit(solution)/shard_map/all_gather | solution.py:265
  282.6 1.9 dynamic-slice_dynamic-update-slice_fusion.15
  284.5 1.9 dynamic-slice_dynamic-update-slice_fusion.14
  286.4 1.9 dynamic-slice_dynamic-update-slice_fusion.13
  288.3 1.9 dynamic-slice_dynamic-update-slice_fusion.12
  290.2 1.9 dynamic-slice_dynamic-update-slice_fusion.11
  292.1 1.9 dynamic-slice_dynamic-update-slice_fusion.10
  293.9 1.9 dynamic-slice_dynamic-update-slice_fusion.9
  295.8 1.9 dynamic-slice_dynamic-update-slice_fusion.8
  297.8 4.6 %all-to-all-start.2 = ((bf16[8,3,176,512]{3,2,1,0:T(8,128)(2,1)}), bf16[8,3,176,512]{3,2,1,0:T(8,128)(2,1)}, u32[]{:S(2)}, u32[]{:S(2)}) async-start(bf16[8,3,176,512]{3,2,1,0:T(8,128)(2,1)} %get-tuple-element.199), calls=%async_computation.2 | async-start | bytes 8650752 | tf_op jit(solution)/shard_map/all_to_all | solution.py:134
  304.5 4.5 %compare_select_fusion.3 = (s32[192,1]{0,1:T(1,128)S(1)}, s32[192,1]{0,1:T(1,128)S(1)}) fusion(s32[]{:T(128)} %bitcast.69, s32[]{:T(128)} %bitcast.70, s32[]{:T(128)} %bitcast.71, s32[]{:T(128)} %bitcast.72, s32[]{:T(128)} %bitcast.73, s32[]{:T(128)} %bitcast.75, s32[]{:T(128)} %bitcast.74, s32[192,1]{0,1:T(1,128)S(1)} %copy-done.20), kind=kLoop, calls=%fused_computation.194 | loop fusion | flops 2880 | bytes 2332 | tf_op jit(solution)/shard_map/gather | solution.py:293
  309.0 10.7 %select_subtract_fusion = s32[192]{0:T(256)S(1)} fusion(pred[192]{0:T(512)(128)(4,1)S(1)} %get-tuple-element.118, pred[192]{0:T(512)(128)(4,1)S(1)} %get-tuple-element.117, pred[192]{0:T(512)(128)(4,1)S(1)} %get-tuple-element.116, pred[192]{0:T(512)(128)(4,1)S(1)} %get-tuple-element.115, pred[192]{0:T(512)(128)(4,1)S(1)} %get-tuple-element.114, ...), kind=kLoop, calls=%fused_computation.222 | loop fusion | flops 3456 | bytes 4872 | tf_op jit(solution)/shard_map/sub | solution.py:295
  322.0 6.9 %convolution_bitcast_fusion.1 = f32[4,2,16,1408]{3,2,1,0:T(8,128)} fusion(bf16[4,2,1408,512]{3,2,1,0:T(8,128)(2,1)} %param.34, bf16[32,512,1]{1,0,2:T(8,128)(2,1)S(1)} %reshape.537, bf16[32,4,16]{0,2,1:T(8,128)(2,1)S(1)} %get-tuple-element.100), kind=kOutput, calls=%fused_computation.30 | convolution fusion | flops 186679296 | bytes 12292096 | tf_op jit(solution)/shard_map/scd,sgfd->sgcf/dot_general | solution.py:308
  332.0 4.2 convolution_bitcast_fusion
  336.2 11.9 %all-gather.4 = f32[8,4,2816]{2,1,0:T(4,128)S(1)} all-gather(f32[2,4,2816]{2,1,0:T(4,128)S(1)} %convolution_bitcast_fusion), channel_id=6, replica_groups=mesh['dp'=4,'expert'=8] {'dp'}, dimensions={0}, use_global_device_ids=true | all-gather | bytes 450560 | tf_op jit(solution)/shard_map/all_gather | solution.py:75
  348.8 5.5 %broadcast_multiply_fusion.1 = bf16[4,1408,512]{2,1,0:T(8,128)(2,1)} fusion(bf16[4,1408,512]{2,1,0:T(8,128)(2,1)} %param.35, bf16[]{:T(256)} %bitcast.107), kind=kLoop, calls=%fused_computation.28 | loop fusion | flops 2883584 | bytes 11534338 | tf_op jit(solution)/shard_map/mul | solution.py:270
  354.4 9.9 %broadcast_multiply_fusion = bf16[4,2,1408,512]{3,2,1,0:T(8,128)(2,1)} fusion(bf16[4,2,1408,512]{3,2,1,0:T(8,128)(2,1)} %param.34, bf16[]{:T(256)} %bitcast.107), kind=kLoop, calls=%fused_computation.25 | loop fusion | flops 5767168 | bytes 23068674 | tf_op jit(solution)/shard_map/mul | solution.py:269
  364.3 9.8 %all-gather.8.cloned.1.call-done = f32[16,2,16,1408]{3,2,1,0:T(8,128)} async-done(((f32[4,2,16,1408]{3,2,1,0:T(8,128)}), f32[16,2,16,1408]{3,2,1,0:T(8,128)}) %all-gather.8.cloned.1.call-update) | async-done | bytes 2883600 | tf_op jit(solution)/shard_map/all_gather | solution.py:75
  374.1 2.9 reduce_sum.137
  377.0 3.7 fusion.17
  381.0 18.2 %all-to-all-done.2 = bf16[8,3,176,512]{3,2,1,0:T(8,128)(2,1)} async-done(((bf16[8,3,176,512]{3,2,1,0:T(8,128)(2,1)}), bf16[8,3,176,512]{3,2,1,0:T(8,128)(2,1)}, u32[]{:S(2)}, u32[]{:S(2)}) %all-to-all-start.2) | async-done | bytes 4325408 | tf_op jit(solution)/shard_map/all_to_all | solution.py:134
  399.2 4.6 %copy.202 = bf16[1,3,8,176,512]{4,3,2,1,0:T(8,128)(2,1)} copy(bf16[1,3,8,176,512]{4,3,1,2,0:T(8,128)(2,1)} %bitcast.98) | data formatting | bytes 8650752 | tf_op jit(solution)/shard_map/all_to_all | solution.py:134
  403.8 14.9 %all-gather.3 = f32[256,512]{1,0:T(8,128)S(1)} all-gather(f32[32,512]{1,0:T(8,128)S(1)} %convolution_bitcast_fusion.2), channel_id=5, replica_groups=mesh['dp'=4,'expert'=8] {'expert'}, dimensions={0}, use_global_device_ids=true | all-gather | bytes 589824 | tf_op jit(solution)/shard_map/all_gather | solution.py:69
  419.9 3.2 all-to-all-start.3
  423.1 3.6 slice_dynamic-update-slice_fusion
  426.7 2.6 bitcast_dynamic-update-slice_fusion
  (198 shorter events, 57.7 us)
Async XLA Ops:
  7.2 411.6 %copy-start = (bf16[2816,512]{1,0:T(8,128)(2,1)S(1)}, bf16[2816,512]{1,0:T(8,128)(2,1)}, u32[]{:S(2)}) copy-start(bf16[2816,512]{1,0:T(8,128)(2,1)} %param.37) | copy-start | bytes 8650756
  8.2 4.3 copy-start.18
  9.4 6.9 %copy-start.27 = (s32[8]{0:T(128)}, s32[8]{0:T(128)S(1)}, u32[]{:S(2)}) copy-start(s32[8]{0:T(128)S(1)} %get-tuple-element.42) | copy-start | bytes 100
  18.3 0.6 copy-start.12
  64.1 18.2 %copy-start.21 = (s32[32,6]{0,1:T(8,128)S(1)}, s32[32,6]{0,1:T(8,128)}, u32[]{:S(2)}) copy-start(s32[32,6]{0,1:T(8,128)} %param.30) | copy-start | bytes 2308
  64.1 20.5 %copy-start.15 = (f32[2048]{0:T(1024)S(1)}, f32[2048]{0:T(1024)}, u32[]{:S(2)}) copy-start(f32[2048]{0:T(1024)} %param.21) | copy-start | bytes 24580
  64.1 194.6 %all-to-all-start.1 = ((bf16[2,3,8,176,512]{4,3,1,0,2:T(8,128)(2,1)}), bf16[2,3,8,176,512]{4,3,1,0,2:T(8,128)(2,1)}, u32[]{:S(2)}, u32[]{:S(2)}) async-start(bf16[2,3,8,176,512]{4,3,1,0,2:T(8,128)(2,1)} %copy.193), calls=%async_computation.1 | async-start | bytes 17301504 | tf_op jit(solution)/shard_map/all_to_all | solution.py:62
  71.3 11.1 %copy-start.24 = (s32[8]{0:T(128)}, s32[8]{0:T(128)S(1)}, u32[]{:S(2)}) copy-start(s32[8]{0:T(128)S(1)} %gather_fusion.3) | copy-start | bytes 100
  84.5 55.8 %copy-start.2 = (bf16[512,512]{0,1:T(8,128)(2,1)}, bf16[512,512]{0,1:T(8,128)(2,1)S(1)}, u32[]{:S(2)}) copy-start(bf16[512,512]{0,1:T(8,128)(2,1)S(1)} %copy.182) | copy-start | bytes 1572868
  84.8 0.6 copy-start.4
  90.5 0.6 copy-start.5
  97.8 0.6 copy-start.14
  98.4 4.4 %copy-start.17 = (s32[1024]{0:T(1024)}, s32[1024]{0:T(1024)S(1)}, u32[]{:S(2)}) copy-start(s32[1024]{0:T(1024)S(1)} %pad_clamp_fusion.1) | copy-start | bytes 12292
  100.6 0.8 copy-start.23
  101.3 0.6 copy-start.26
  102.8 0.6 copy-start.7
  102.8 0.6 copy-start.9
  108.3 0.6 copy-start.6
  136.3 0.8 copy-start.3
  136.3 14.3 %copy-start.8 = (bf16[32,2,32]{2,1,0:T(2,128)(2,1)S(1)}, bf16[32,2,32]{2,1,0:T(2,128)(2,1)}, u32[]{:S(2)}) copy-start(bf16[32,2,32]{2,1,0:T(2,128)(2,1)} %copy-done.7) | copy-start | bytes 12292
  141.9 0.6 copy-start.11
  142.0 0.6 copy-start.10
  146.4 127.4 %copy-start.16 = (f32[2048]{0:T(1024)S(1)}, f32[2048]{0:T(1024)}, u32[]{:S(2)}) copy-start(f32[2048]{0:T(1024)} %param.29) | copy-start | bytes 24580
  282.6 15.2 %copy-start.13 = (s32[1,4]{0,1:T(4,128)S(1)}, s32[1,4]{0,1:T(4,128)}, u32[]{:S(2)}) copy-start(s32[1,4]{0,1:T(4,128)} %copy-done.12) | copy-start | bytes 52
  282.6 15.2 %copy-start.25 = (s32[8]{0:T(128)S(1)}, s32[8]{0:T(128)}, u32[]{:S(2)}) copy-start(s32[8]{0:T(128)} %copy-done.24) | copy-start | bytes 100
  282.6 15.2 %copy-start.29 = (s32[8]{0:T(128)S(1)}, s32[8]{0:T(128)}, u32[]{:S(2)}) copy-start(s32[8]{0:T(128)} %get-tuple-element.120) | copy-start | bytes 100
  297.8 4.7 %copy-start.19 = (s32[32]{0:T(128)S(1)}, s32[32]{0:T(128)}, u32[]{:S(2)}) copy-start(s32[32]{0:T(128)} %copy-done.18) | copy-start | bytes 388
  297.8 6.7 %copy-start.20 = (s32[192,1]{0,1:T(1,128)S(1)}, s32[192,1]{0,1:T(1,128)}, u32[]{:S(2)}) copy-start(s32[192,1]{0,1:T(1,128)} %reshape_reshape.3) | copy-start | bytes 2308
  297.8 23.8 %copy-start.22 = (f32[32,6]{0,1:T(8,128)S(1)}, f32[32,6]{0,1:T(8,128)}, u32[]{:S(2)}) copy-start(f32[32,6]{0,1:T(8,128)} %param.31) | copy-start | bytes 2308
  297.8 101.4 %all-to-all-start.2 = ((bf16[8,3,176,512]{3,2,1,0:T(8,128)(2,1)}), bf16[8,3,176,512]{3,2,1,0:T(8,128)(2,1)}, u32[]{:S(2)}, u32[]{:S(2)}) async-start(bf16[8,3,176,512]{3,2,1,0:T(8,128)(2,1)} %get-tuple-element.199), calls=%async_computation.2 | async-start | bytes 8650752 | tf_op jit(solution)/shard_map/all_to_all | solution.py:134
  302.4 71.7 %all-gather.8.cloned.1.call-start = ((), (), s32[]{:S(2)}) async-start(), calls=%async_computation.4 | async-start | bytes 3604480 | tf_op jit(solution)/shard_map/all_gather | solution.py:75
  322.0 6.9 %copy-start.28 = (s32[8]{0:T(128)S(1)}, s32[8]{0:T(128)}, u32[]{:S(2)}) copy-start(s32[8]{0:T(128)} %copy-done.27) | copy-start | bytes 100
  419.9 9.4 %all-to-all-start.3 = ((f32[4,1,512]{2,1,0:T(1,128)}), f32[4,1,512]{2,1,0:T(1,128)S(1)}, u32[]{:S(2)}, u32[]{:S(2)}) async-start(f32[4,1,512]{2,1,0:T(1,128)} %copy.203), calls=%async_computation.3 | async-start | bytes 16384 | tf_op jit(solution)/shard_map/all_to_all | solution.py:324
Sparse Core Ops, SparseCore 0:
  329.0 45.0 all-gather.7

commit v2 on v1

--- a/solution.py
+++ b/solution.py
@@ -59,7 +59,8 @@
 def spread_slots(chosen, ex_count):
     count, parts, ff_width, col_width = chosen.shape
     pieces = chosen.reshape(count, parts, ex_count, ff_width // ex_count, col_width)
-    spread = lax.all_to_all(pieces, "expert", split_axis=2, concat_axis=0, tiled=True)
+    pieces = pieces.transpose(2, 0, 1, 3, 4)
+    spread = lax.all_to_all(pieces, "expert", split_axis=0, concat_axis=0, tiled=True)
     return spread.reshape(ex_count * count, parts, ff_width // ex_count, col_width)
 
 
@@ -262,9 +263,9 @@
     slots_local = expert_gate_up.shape[0]
     ff_width = expert_gate_up.shape[2]
     col_width = expert_gate_up.shape[3]
+    outgoing = migrate_route(spread, plan, expert_gate_up, expert_down)
+    normed_group, outgoing = lax.optimization_barrier((normed_group, outgoing))
     every_row = lax.all_gather(normed_group, "dp", axis=0, tiled=True)
-    outgoing = migrate_route(spread, plan, expert_gate_up, expert_down)
-    every_row, outgoing = lax.optimization_barrier((every_row, outgoing))
     unit = (every_row[0, 0].astype(jnp.float32) * 0.0 + 1.0).astype(expert_gate_up.dtype)
     base_gate_up = expert_gate_up * unit
     base_down = expert_down * unit
@@ -320,8 +321,14 @@
     shared_act = (jax.nn.silu(shared_sum[0]) * shared_sum[1]).astype(jnp.bfloat16)
     shared_term = jnp.dot(shared_act, shared_down, preferred_element_type=jnp.float32)
     routed, arrived = lax.optimization_barrier((routed, arrived))
-    moe_rows = scatter_sum(routed, "expert")
-    moe_part = lax.all_to_all(moe_rows + shared_term, "dp", split_axis=0, concat_axis=1, tiled=True)
+    shared_at = ex_index * dp_count * req_local
+    own_block = lax.dynamic_slice_in_dim(routed, shared_at, dp_count * req_local, 0) + shared_term
+    routed = lax.dynamic_update_slice_in_dim(routed, own_block, shared_at, 0)
+    by_token = routed.reshape(ex_count, dp_count, req_local, col_width).transpose(1, 0, 2, 3)
+    by_token = by_token.reshape(requests, col_width)
+    received = lax.all_to_all(by_token, ("dp", "expert"), split_axis=0, concat_axis=0, tiled=True)
+    moe_cols = jnp.sum(received.reshape(dp_count, ex_count, req_local, col_width), axis=1)
+    moe_part = moe_cols.transpose(1, 0, 2).reshape(req_local, dp_count * col_width)
     layer_out = (residual + moe_part).astype(jnp.bfloat16)
     my_moved = plan[-1]
     moved_gate_up = lax.dynamic_update_index_in_dim(base_gate_up, arrived[0, :2], my_moved, 0)

time: 440 us -> 418 us (0.950)
  blocking collectives: 86.3 us -> 70.8 us
  waiting for transfers between devices: 126 us -> 119 us
    all_gather x1 -> x0, blocking collectives: 14.9 us -> none  [scatter_sum(): gathered = lax.all_gather(values, axis, axis=0, tiled=False)]
    all_to_all x1, waiting for transfers between devices: 18.2 us -> 10.2 us  [deliver(): lax.all_to_all(outgoing, 'expert', split_axis=0, concat_axis=2, tiled=True)]
    unnamed x74 -> x75, local copies, waits for them, and re-layouts: 25.3 us -> 25.9 us
  transfers between devices with their start and end apart: 4 -> 4, of which waited for: 3 -> 4; matrix products, arithmetic and copies ran while one was open for 27% -> 29% of each run, Pallas kernels for 0% -> 0%
where the time goes in v2:
time: 418 us; the launch traced here: 415 us
  waiting for transfers between devices  119 us (28%)
  local copies, waits for them, and re-layouts  79.3 us (19%)
  blocking collectives  70.8 us (17%)
  other arithmetic  64.1 us (15%)
  between operations  38.1 us (9%)
  matrix products  31 us (7%)
  starting transfers between devices  12.3 us (3%)
    all_to_all x1, waiting for transfers between devices, spread_slots(): lax.all_to_all(pieces, 'expert', split_axis=0, concat_axis=0, tiled=True)  98 us
    unnamed x75, local copies, waits for them, and re-layouts  25.9 us
    all_gather x1, blocking collectives, gather_rows(): by_expert = lax.all_gather(rows, 'expert', axis=0, tiled=True)  15.9 us
    all_gather x1, blocking collectives, local(): lax.all_gather(partial_value, 'expert', axis=0, tiled=False)  15.1 us
    all_gather x1, blocking collectives, local(): gathered = lax.all_gather(packed, 'dp', axis=0, tiled=False)  11.6 us
    all_gather x1, blocking collectives, sum_over(): return jnp.sum(lax.all_gather(values, axis, axis=0, tiled=False), axis=0)  11.4 us
    sub x1, other arithmetic, local(): local_slot = slot_of - ex_index * slots_local  10.7 us
    all_to_all x1, waiting for transfers between devices, deliver(): lax.all_to_all(outgoing, 'expert', split_axis=0, concat_axis=2, tiled=True)  10.2 us
  transfers between devices with their start and end apart: 4, of which 4 were waited for; matrix products, arithmetic and copies ran while one was open for 29% of the time, Pallas kernels for 0%

profile of v2, /device:TPU:0, one launch (start us, length us, event | category | flops | bytes accessed | tf_op | source)
XLA Modules:
  0.0 414.9 jit_solution(12615380756412562912)
XLA Ops:
  21.8 15.9 %all-gather.4 = bf16[8,1,2048]{2,1,0:T(2,128)(2,1)S(1)} all-gather(bf16[1,1,2048]{2,1,0:T(2,128)(2,1)} %bitcast.255), channel_id=1, replica_groups=mesh['dp'=4,'expert'=8] {'expert'}, dimensions={0}, use_global_device_ids=true | all-gather | bytes 36864 | tf_op jit(solution)/shard_map/all_gather | solution.py:47
  37.7 8.5 %all_gather.34 = bf16[32,2048]{1,0:T(8,128)(2,1)S(1)} all-gather(bf16[8,2048]{1,0:T(8,128)(2,1)S(1)} %bitcast.248), channel_id=1, replica_groups=mesh['dp'=4,'expert'=8] {'dp'}, dimensions={0}, use_global_device_ids=true | all-gather | bytes 163840 | tf_op jit(solution)/shard_map/all_gather | solution.py:48
  47.3 2.1 constant_dynamic-slice_fusion.9
  49.5 3.1 constant_dynamic-slice_fusion.11
  52.8 3.9 pad_maximum_fusion.2
  56.7 7.6 %copy.253 = bf16[2,3,8,176,512]{4,3,1,0,2:T(8,128)(2,1)} copy(bf16[2,3,8,176,512]{4,3,2,1,0:T(8,128)(2,1)} %bitcast.235) | data formatting | bytes 17301504 | tf_op jit(solution)/shard_map/reshape | solution.py:61
  64.3 5.1 %all-to-all-start.1 = ((bf16[8,2,3,176,512]{4,3,2,1,0:T(8,128)(2,1)}), bf16[8,2,3,176,512]{4,3,2,1,0:T(8,128)(2,1)}, u32[]{:S(2)}, u32[]{:S(2)}) async-start(bf16[8,2,3,176,512]{4,3,2,1,0:T(8,128)(2,1)} %bitcast.234), calls=%async_computation.1 | async-start | bytes 17301504 | tf_op jit(solution)/shard_map/all_to_all | solution.py:63
  85.6 2.6 fusion.92
  88.2 1.5 reshape.370
  94.8 2.6 scatter_custom_fusion
  98.6 2.1 gather_fusion
  105.0 1.6 fusion.5
  106.6 1.9 fusion.91
  116.2 1.4 convolution_bitcast_fusion.3
  121.6 1.6 convolution_multiply_fusion
  124.9 11.6 %all-gather = f32[128,2,514]{2,0,1:T(8,128)S(1)} all-gather(f32[32,2,514]{2,0,1:T(8,128)S(1)} %pad_maximum_fusion.3), channel_id=2, replica_groups=mesh['dp'=4,'expert'=8] {'dp'}, dimensions={0}, use_global_device_ids=true | all-gather | bytes 657920 | tf_op jit(solution)/shard_map/all_gather | solution.py:224
  138.0 2.5 copy.222
  140.5 1.5 fusion.84
  142.7 3.0 multiply_reduce_fusion
  147.4 2.4 fusion.25
  159.2 1.8 fusion.7
  160.9 98.0 %all-to-all-done.1 = bf16[8,2,3,176,512]{4,3,2,1,0:T(8,128)(2,1)} async-done(((bf16[8,2,3,176,512]{4,3,2,1,0:T(8,128)(2,1)}), bf16[8,2,3,176,512]{4,3,2,1,0:T(8,128)(2,1)}, u32[]{:S(2)}, u32[]{:S(2)}) %all-to-all-start.1) | async-done | bytes 8650784 | tf_op jit(solution)/shard_map/all_to_all | solution.py:63
  258.9 15.1 %all-gather.1 = f32[64,2048]{1,0:T(8,128)S(1)} all-gather(f32[8,2048]{1,0:T(8,128)S(1)} %fusion.7), channel_id=3, replica_groups=mesh['dp'=4,'expert'=8] {'expert'}, dimensions={0}, use_global_device_ids=true | all-gather | bytes 589824 | tf_op jit(solution)/shard_map/all_gather | solution.py:258
  274.2 1.9 dynamic-slice_dynamic-update-slice_fusion.15
  276.1 1.9 dynamic-slice_dynamic-update-slice_fusion.14
  278.0 1.9 dynamic-slice_dynamic-update-slice_fusion.13
  279.9 1.9 dynamic-slice_dynamic-update-slice_fusion.12
  281.8 1.9 dynamic-slice_dynamic-update-slice_fusion.11
  283.7 1.9 dynamic-slice_dynamic-update-slice_fusion.10
  285.6 1.9 dynamic-slice_dynamic-update-slice_fusion.9
  287.4 1.9 dynamic-slice_dynamic-update-slice_fusion.8
  290.2 4.6 %all-to-all-start.2 = ((bf16[8,3,176,512]{3,2,1,0:T(8,128)(2,1)}), bf16[8,3,176,512]{3,2,1,0:T(8,128)(2,1)}, u32[]{:S(2)}, u32[]{:S(2)}) async-start(bf16[8,3,176,512]{3,2,1,0:T(8,128)(2,1)} %get-tuple-element.199), calls=%async_computation.2 | async-start | bytes 8650752 | tf_op jit(solution)/shard_map/all_to_all | solution.py:135
  296.8 4.5 %compare_select_fusion.3 = (s32[192,1]{0,1:T(1,128)S(1)}, s32[192,1]{0,1:T(1,128)S(1)}) fusion(s32[]{:T(128)} %bitcast.65, s32[]{:T(128)} %bitcast.66, s32[]{:T(128)} %bitcast.67, s32[]{:T(128)} %bitcast.68, s32[]{:T(128)} %bitcast.69, s32[]{:T(128)} %bitcast.71, s32[]{:T(128)} %bitcast.70, s32[192,1]{0,1:T(1,128)S(1)} %copy-done.20), kind=kLoop, calls=%fused_computation.196 | loop fusion | flops 2880 | bytes 2332 | tf_op jit(solution)/shard_map/gather | solution.py:294
  301.4 10.7 %select_subtract_fusion = s32[192]{0:T(256)S(1)} fusion(pred[192]{0:T(512)(128)(4,1)S(1)} %get-tuple-element.118, pred[192]{0:T(512)(128)(4,1)S(1)} %get-tuple-element.117, pred[192]{0:T(512)(128)(4,1)S(1)} %get-tuple-element.116, pred[192]{0:T(512)(128)(4,1)S(1)} %get-tuple-element.115, pred[192]{0:T(512)(128)(4,1)S(1)} %get-tuple-element.114, ...), kind=kLoop, calls=%fused_computation.224 | loop fusion | flops 3456 | bytes 4872 | tf_op jit(solution)/shard_map/sub | solution.py:296
  314.3 8.4 %all_gather.39 = bf16[32,2048]{1,0:T(8,128)(2,1)S(1)} all-gather(bf16[8,2048]{1,0:T(8,128)(2,1)S(1)} %multiply_convert_fusion), channel_id=1, replica_groups=mesh['dp'=4,'expert'=8] {'dp'}, dimensions={0}, use_global_device_ids=true | all-gather | bytes 163840 | tf_op jit(solution)/shard_map/all_gather | solution.py:268
  322.8 6.9 %convolution_bitcast_fusion.1 = f32[4,2,16,1408]{3,2,1,0:T(8,128)} fusion(bf16[4,2,1408,512]{3,2,1,0:T(8,128)(2,1)} %param.34, bf16[32,512,1]{1,0,2:T(8,128)(2,1)S(1)} %reshape.543, bf16[32,4,16]{0,2,1:T(8,128)(2,1)S(1)} %get-tuple-element.100), kind=kOutput, calls=%fused_computation.31 | convolution fusion | flops 186679296 | bytes 12292096 | tf_op jit(solution)/shard_map/scd,sgfd->sgcf/dot_general | solution.py:309
  332.8 4.2 %convolution_bitcast_fusion = f32[2,4,2816]{2,1,0:T(4,128)S(1)} fusion(bf16[2,2816,512]{2,1,0:T(8,128)(2,1)} %param.36, bf16[4,1,1,512]{3,1,0,2:T(2,128)(2,1)S(1)} %constant_dynamic-slice_fusion.6), kind=kOutput, calls=%fused_computation.27 | convolution fusion | flops 23068672 | bytes 5861376 | tf_op jit(solution)/shard_map/td,gfd->gtf/dot_general | solution.py:312
  337.0 11.4 %all-gather.3 = f32[8,4,2816]{2,1,0:T(4,128)S(1)} all-gather(f32[2,4,2816]{2,1,0:T(4,128)S(1)} %convolution_bitcast_fusion), channel_id=5, replica_groups=mesh['dp'=4,'expert'=8] {'dp'}, dimensions={0}, use_global_device_ids=true | all-gather | bytes 450560 | tf_op jit(solution)/shard_map/all_gather | solution.py:76
  349.1 5.5 %broadcast_multiply_fusion.1 = bf16[4,1408,512]{2,1,0:T(8,128)(2,1)} fusion(bf16[4,1408,512]{2,1,0:T(8,128)(2,1)} %param.35, bf16[]{:T(256)} %bitcast.102), kind=kLoop, calls=%fused_computation.29 | loop fusion | flops 2883584 | bytes 11534338 | tf_op jit(solution)/shard_map/mul | solution.py:271
  354.7 9.9 %broadcast_multiply_fusion = bf16[4,2,1408,512]{3,2,1,0:T(8,128)(2,1)} fusion(bf16[4,2,1408,512]{3,2,1,0:T(8,128)(2,1)} %param.34, bf16[]{:T(256)} %bitcast.102), kind=kLoop, calls=%fused_computation.26 | loop fusion | flops 5767168 | bytes 23068674 | tf_op jit(solution)/shard_map/mul | solution.py:270
  364.6 9.9 %all-gather.7.cloned.1.call-done = f32[16,2,16,1408]{3,2,1,0:T(8,128)} async-done(((f32[4,2,16,1408]{3,2,1,0:T(8,128)}), f32[16,2,16,1408]{3,2,1,0:T(8,128)}) %all-gather.7.cloned.1.call-update) | async-done | bytes 2883600 | tf_op jit(solution)/shard_map/all_gather | solution.py:76
  374.5 2.9 reduce_sum.137
  377.4 3.7 fusion.17
  381.4 10.2 %all-to-all-done.2 = bf16[8,3,176,512]{3,2,1,0:T(8,128)(2,1)} async-done(((bf16[8,3,176,512]{3,2,1,0:T(8,128)(2,1)}), bf16[8,3,176,512]{3,2,1,0:T(8,128)(2,1)}, u32[]{:S(2)}, u32[]{:S(2)}) %all-to-all-start.2) | async-done | bytes 4325408 | tf_op jit(solution)/shard_map/all_to_all | solution.py:135
  391.6 4.6 %copy.207 = bf16[1,3,8,176,512]{4,3,2,1,0:T(8,128)(2,1)} copy(bf16[1,3,8,176,512]{4,3,1,2,0:T(8,128)(2,1)} %bitcast.94) | data formatting | bytes 8650752 | tf_op jit(solution)/shard_map/all_to_all | solution.py:135
  397.4 2.6 all-to-all-start.3
  400.0 3.6 slice_dynamic-update-slice_fusion
  403.6 2.6 bitcast_dynamic-update-slice_fusion
  (200 shorter events, 58.3 us)
Async XLA Ops:
  7.2 389.0 %copy-start = (bf16[2816,512]{1,0:T(8,128)(2,1)S(1)}, bf16[2816,512]{1,0:T(8,128)(2,1)}, u32[]{:S(2)}) copy-start(bf16[2816,512]{1,0:T(8,128)(2,1)} %param.37) | copy-start | bytes 8650756
  8.2 4.3 %copy-start.18 = (s32[32]{0:T(128)}, s32[32]{0:T(128)S(1)}, u32[]{:S(2)}) copy-start(s32[32]{0:T(128)S(1)} %eq.139) | copy-start | bytes 388
  9.4 6.9 %copy-start.27 = (s32[8]{0:T(128)}, s32[8]{0:T(128)S(1)}, u32[]{:S(2)}) copy-start(s32[8]{0:T(128)S(1)} %get-tuple-element.42) | copy-start | bytes 100
  18.3 0.6 copy-start.12
  64.2 18.2 %copy-start.21 = (s32[32,6]{0,1:T(8,128)S(1)}, s32[32,6]{0,1:T(8,128)}, u32[]{:S(2)}) copy-start(s32[32,6]{0,1:T(8,128)} %param.30) | copy-start | bytes 2308
  64.2 20.5 %copy-start.15 = (f32[2048]{0:T(1024)S(1)}, f32[2048]{0:T(1024)}, u32[]{:S(2)}) copy-start(f32[2048]{0:T(1024)} %param.21) | copy-start | bytes 24580
  64.3 194.6 %all-to-all-start.1 = ((bf16[8,2,3,176,512]{4,3,2,1,0:T(8,128)(2,1)}), bf16[8,2,3,176,512]{4,3,2,1,0:T(8,128)(2,1)}, u32[]{:S(2)}, u32[]{:S(2)}) async-start(bf16[8,2,3,176,512]{4,3,2,1,0:T(8,128)(2,1)} %bitcast.234), calls=%async_computation.1 | async-start | bytes 17301504 | tf_op jit(solution)/shard_map/all_to_all | solution.py:63
  71.4 11.1 %copy-start.24 = (s32[8]{0:T(128)}, s32[8]{0:T(128)S(1)}, u32[]{:S(2)}) copy-start(s32[8]{0:T(128)S(1)} %gather_fusion.3) | copy-start | bytes 100
  84.6 55.8 %copy-start.2 = (bf16[512,512]{0,1:T(8,128)(2,1)}, bf16[512,512]{0,1:T(8,128)(2,1)S(1)}, u32[]{:S(2)}) copy-start(bf16[512,512]{0,1:T(8,128)(2,1)S(1)} %copy.187) | copy-start | bytes 1572868
  84.9 0.6 copy-start.4
  90.7 0.6 copy-start.5
  98.0 0.6 copy-start.14
  98.6 4.4 %copy-start.17 = (s32[1024]{0:T(1024)}, s32[1024]{0:T(1024)S(1)}, u32[]{:S(2)}) copy-start(s32[1024]{0:T(1024)S(1)} %pad_clamp_fusion.1) | copy-start | bytes 12292
  100.7 0.8 copy-start.23
  101.4 0.6 copy-start.26
  102.9 0.6 copy-start.7
  103.0 0.6 copy-start.9
  108.5 0.6 copy-start.6
  136.5 0.8 copy-start.3
  136.5 14.2 %copy-start.8 = (bf16[32,2,32]{2,1,0:T(2,128)(2,1)S(1)}, bf16[32,2,32]{2,1,0:T(2,128)(2,1)}, u32[]{:S(2)}) copy-start(bf16[32,2,32]{2,1,0:T(2,128)(2,1)} %copy-done.7) | copy-start | bytes 12292
  142.0 0.6 copy-start.11
  142.1 0.6 copy-start.10
  274.2 15.2 %copy-start.13 = (s32[1,4]{0,1:T(4,128)S(1)}, s32[1,4]{0,1:T(4,128)}, u32[]{:S(2)}) copy-start(s32[1,4]{0,1:T(4,128)} %copy-done.12) | copy-start | bytes 52
  274.2 15.2 %copy-start.25 = (s32[8]{0:T(128)S(1)}, s32[8]{0:T(128)}, u32[]{:S(2)}) copy-start(s32[8]{0:T(128)} %copy-done.24) | copy-start | bytes 100
  274.2 15.2 %copy-start.29 = (s32[8]{0:T(128)S(1)}, s32[8]{0:T(128)}, u32[]{:S(2)}) copy-start(s32[8]{0:T(128)} %get-tuple-element.120) | copy-start | bytes 100
  289.4 0.7 copy-start.16
  290.1 4.6 %copy-start.19 = (s32[32]{0:T(128)S(1)}, s32[32]{0:T(128)}, u32[]{:S(2)}) copy-start(s32[32]{0:T(128)} %copy-done.18) | copy-start | bytes 388
  290.2 6.7 %copy-start.20 = (s32[192,1]{0,1:T(1,128)S(1)}, s32[192,1]{0,1:T(1,128)}, u32[]{:S(2)}) copy-start(s32[192,1]{0,1:T(1,128)} %reshape_reshape.3) | copy-start | bytes 2308
  290.2 23.8 %copy-start.22 = (f32[32,6]{0,1:T(8,128)S(1)}, f32[32,6]{0,1:T(8,128)}, u32[]{:S(2)}) copy-start(f32[32,6]{0,1:T(8,128)} %param.31) | copy-start | bytes 2308
  290.2 101.4 %all-to-all-start.2 = ((bf16[8,3,176,512]{3,2,1,0:T(8,128)(2,1)}), bf16[8,3,176,512]{3,2,1,0:T(8,128)(2,1)}, u32[]{:S(2)}, u32[]{:S(2)}) async-start(bf16[8,3,176,512]{3,2,1,0:T(8,128)(2,1)} %get-tuple-element.199), calls=%async_computation.2 | async-start | bytes 8650752 | tf_op jit(solution)/shard_map/all_to_all | solution.py:135
  294.7 79.7 %all-gather.7.cloned.1.call-start = ((), (), s32[]{:S(2)}) async-start(), calls=%async_computation.4 | async-start | bytes 3604480 | tf_op jit(solution)/shard_map/all_gather | solution.py:76
  322.8 6.9 %copy-start.28 = (s32[8]{0:T(128)S(1)}, s32[8]{0:T(128)}, u32[]{:S(2)}) copy-start(s32[8]{0:T(128)} %copy-done.27) | copy-start | bytes 100
  397.4 10.0 %all-to-all-start.3 = ((f32[32,1,512]{2,1,0:T(1,128)}), f32[32,1,512]{2,1,0:T(1,128)S(1)}, u32[]{:S(2)}, u32[]{:S(2)}) async-start(f32[32,1,512]{2,1,0:T(1,128)} %copy.209), calls=%async_computation.3 | async-start | bytes 131072 | tf_op jit(solution)/shard_map/all_to_all | solution.py:329
Sparse Core Ops, SparseCore 0:
  329.9 44.5 all-gather.6

commit v3 on v2

--- a/solution.py
+++ b/solution.py
@@ -52,16 +52,26 @@
     return jnp.stack([lax.dynamic_index_in_dim(table, rows[k], 0, False) for k in range(rows.shape[0])])
 
 
-def pick_slots(gate_up, down, picks):
-    return jnp.concatenate([pick_rows(gate_up, picks), pick_rows(down, picks)[:, None]], axis=1)
-
-
-def spread_slots(chosen, ex_count):
-    count, parts, ff_width, col_width = chosen.shape
-    pieces = chosen.reshape(count, parts, ex_count, ff_width // ex_count, col_width)
-    pieces = pieces.transpose(2, 0, 1, 3, 4)
+def pick_slots(gate_up, down, picks, ex_count):
+    slots, parts, ff_width, col_width = gate_up.shape
+    rows = ff_width // ex_count
+    gate_up_blocks = gate_up.reshape(slots, parts, ex_count, rows, col_width)
+    down_blocks = down.reshape(slots, ex_count, rows, col_width)
+    chunks = []
+    for c in range(ex_count):
+        held = []
+        for k in range(picks.shape[0]):
+            pair = lax.dynamic_index_in_dim(gate_up_blocks[:, :, c], picks[k], 0, False)
+            single = lax.dynamic_index_in_dim(down_blocks[:, c], picks[k], 0, False)
+            held.append(jnp.concatenate([pair, single[None]], axis=0))
+        chunks.append(jnp.stack(held))
+    return jnp.stack(chunks)
+
+
+def spread_slots(pieces):
+    ex_count, count, parts, rows, col_width = pieces.shape
     spread = lax.all_to_all(pieces, "expert", split_axis=0, concat_axis=0, tiled=True)
-    return spread.reshape(ex_count * count, parts, ff_width // ex_count, col_width)
+    return spread.reshape(ex_count * count, parts, rows, col_width)
 
 
 def scatter_sum(values, axis):
@@ -109,7 +119,7 @@
     src_dev = source // slots_local
     src_rank = rank.reshape(-1)[source]
     fast = min(2, slots_local)
-    chosen = pick_slots(expert_gate_up, expert_down, my_picks[:fast])
+    chosen = pick_slots(expert_gate_up, expert_down, my_picks[:fast], ex_count)
     return chosen, (my_picks, src_dev, src_rank, load, moved_slot[ex_index])
 
 
@@ -118,13 +128,13 @@
     ex_count = src_dev.shape[0]
     slots_local = expert_gate_up.shape[0]
     fast = spread.shape[0] // ex_count
-    out_a = pick_rows(spread, src_dev * fast + jnp.minimum(src_rank, fast - 1))
+    out_a = jnp.take(spread, src_dev * fast + jnp.minimum(src_rank, fast - 1), axis=0)
     if slots_local > fast:
         rest = slots_local - fast
 
         def extra():
-            spread_b = spread_slots(pick_slots(expert_gate_up, expert_down, my_picks[fast:]), ex_count)
-            out_b = pick_rows(spread_b, src_dev * rest + jnp.clip(src_rank - fast, 0, rest - 1))
+            spread_b = spread_slots(pick_slots(expert_gate_up, expert_down, my_picks[fast:], ex_count))
+            out_b = jnp.take(spread_b, src_dev * rest + jnp.clip(src_rank - fast, 0, rest - 1), axis=0)
             return jnp.where((src_rank < fast)[:, None, None, None], out_a, out_b)
 
         out_a = lax.cond(load > fast, extra, lambda: out_a)
@@ -168,7 +178,7 @@
     chosen, plan = migrate_start(expert_gate_up, expert_down, old_place, new_place, ex_index)
     everyone = gather_rows(hidden)
     everyone, chosen = lax.optimization_barrier((everyone, chosen))
-    spread = spread_slots(chosen, ex_count)
+    spread = spread_slots(chosen)
     normed = rms_norm(everyone.astype(jnp.float32), attn_gain).astype(jnp.bfloat16)
     queries = jnp.einsum(
         "td,qd->tq", normed, query_weight, preferred_element_type=jnp.float32

time: 418 us -> 426 us (1.019)
  waiting for transfers between devices: 119 us -> 152 us
  between operations: 38.1 us -> 23.8 us
  local copies, waits for them, and re-layouts: 79.3 us -> 66.2 us
  other arithmetic: 64.1 us -> 69.8 us
    all_to_all x1, waiting for transfers between devices: 98 us -> 131 us  [spread_slots(): lax.all_to_all(pieces, 'expert', split_axis=0, concat_axis=0, tiled=True)]
    unnamed x75 -> x84, local copies, waits for them, and re-layouts: 25.9 us -> 15.2 us
    slice x4 -> x5, local copies, waits for them, and re-layouts: 1.36 us -> 10.8 us  [the longest x1 5.72 us: pick_slots(): single = lax.dynamic_index_in_dim(down_blocks[:, c], picks[k], 0, False)]
    reshape x1 -> x0, local copies, waits for them, and re-layouts: 7.57 us -> none  [spread_slots(): chosen.reshape(count, parts, ex_count, ff_width // ex_count, col_width)]
    unnamed x1 -> x8, other arithmetic: 0.07 us -> 7.43 us
    gather x0 -> x1, local copies, waits for them, and re-layouts: none -> 6.46 us  [migrate_route(): jnp.take(spread, src_dev * fast + jnp.minimum(src_rank, fast - 1), axis=0)]
    select_n x0 -> x1, other arithmetic: none -> 4.72 us  [migrate_route(): jnp.take(spread, src_dev * fast + jnp.minimum(src_rank, fast - 1), axis=0)]
  transfers between devices with their start and end apart: 4 -> 4, of which waited for: 4 -> 4; matrix products, arithmetic and copies ran while one was open for 29% -> 24% of each run, Pallas kernels for 0% -> 0%
where the time goes in v3:
time: 426 us; the launch traced here: 424 us
  waiting for transfers between devices  152 us (36%)
  blocking collectives  71.1 us (17%)
  other arithmetic  69.8 us (16%)
  local copies, waits for them, and re-layouts  66.2 us (16%)
  matrix products  28.5 us (7%)
  between operations  23.8 us (6%)
  starting transfers between devices  12.3 us (3%)
    all_to_all x1, waiting for transfers between devices, spread_slots(): lax.all_to_all(pieces, 'expert', split_axis=0, concat_axis=0, tiled=True)  131 us
    all_gather x1, blocking collectives, gather_rows(): by_expert = lax.all_gather(rows, 'expert', axis=0, tiled=True)  15.9 us
    unnamed x84, local copies, waits for them, and re-layouts  15.2 us
    all_gather x1, blocking collectives, local(): lax.all_gather(partial_value, 'expert', axis=0, tiled=False)  14.9 us
    all_gather x1, blocking collectives, local(): gathered = lax.all_gather(packed, 'dp', axis=0, tiled=False)  11.7 us
    all_gather x1, blocking collectives, sum_over(): return jnp.sum(lax.all_gather(values, axis, axis=0, tiled=False), axis=0)  11.6 us
    sub x1, other arithmetic, local(): local_slot = slot_of - ex_index * slots_local  10.7 us
    all_gather x1, waiting for transfers between devices, sum_over(): return jnp.sum(lax.all_gather(values, axis, axis=0, tiled=False), axis=0)  10.1 us
  transfers between devices with their start and end apart: 4, of which 4 were waited for; matrix products, arithmetic and copies ran while one was open for 24% of the time, Pallas kernels for 0%

profile of v3, /device:TPU:0, one launch (start us, length us, event | category | flops | bytes accessed | tf_op | source)
XLA Modules:
  0.0 423.8 jit_solution(13777116319564910718)
XLA Ops:
  8.1 1.2 iota_reduce_fusion.7
  9.4 1.3 gather_fusion.5
  21.9 15.9 %all-gather.4 = bf16[8,1,2048]{2,1,0:T(2,128)(2,1)S(1)} all-gather(bf16[1,1,2048]{2,1,0:T(2,128)(2,1)} %bitcast.488), channel_id=1, replica_groups=mesh['dp'=4,'expert'=8] {'expert'}, dimensions={0}, use_global_device_ids=true | all-gather | bytes 36864 | tf_op jit(solution)/shard_map/all_gather | solution.py:47
  37.8 8.5 %all_gather.34 = bf16[32,2048]{1,0:T(8,128)(2,1)S(1)} all-gather(bf16[8,2048]{1,0:T(8,128)(2,1)S(1)} %bitcast.481), channel_id=1, replica_groups=mesh['dp'=4,'expert'=8] {'dp'}, dimensions={0}, use_global_device_ids=true | all-gather | bytes 163840 | tf_op jit(solution)/shard_map/all_gather | solution.py:48
  46.2 5.7 %fusion.107 = (bf16[4,1,176,512]{3,2,1,0:T(8,128)(2,1)}, bf16[4,1,176,512]{3,2,1,0:T(8,128)(2,1)}, bf16[4,1,176,512]{3,2,1,0:T(8,128)(2,1)}, bf16[4,1,176,512]{3...) fusion(bf16[4,8,176,512]{3,2,1,0:T(8,128)(2,1)} %bitcast.469), kind=kLoop, calls=%fused_computation.359 | loop fusion | bytes 11534336 | tf_op jit(solution)/shard_map/slice | solution.py:65
  52.0 2.3 copy-done.1
  54.3 4.4 %fusion.106 = (bf16[4,2,1,176,512]{4,3,2,1,0:T(8,128)(2,1)}, bf16[4,2,1,176,512]{4,3,2,1,0:T(8,128)(2,1)}, bf16[4,2,1,176,512]{4,3,2,1,0:T(8,128)(2,1)}, bf16[4,...) fusion(bf16[4,2,8,176,512]{4,3,2,1,0:T(8,128)(2,1)S(1)} %bitcas, ...), kind=kLoop, calls=%fused_computation.358 | loop fusion | bytes 23068672 | tf_op jit(solution)/shard_map/slice | solution.py:64
  60.0 1.4 dynamic-slice_bitcast_fusion.49
  61.4 1.4 dynamic-slice_bitcast_fusion.53
  77.4 5.1 %all-to-all-start.1 = ((bf16[8,2,3,176,512]{4,3,2,1,0:T(8,128)(2,1)}), bf16[8,2,3,176,512]{4,3,2,1,0:T(8,128)(2,1)}, u32[]{:S(2)}, u32[]{:S(2)}) async-start(bf16[8,2,3,176,512]{4,3,2,1,0:T(8,128)(2,1)} %fusion.19), calls=%async_computation.1 | async-start | bytes 17301504 | tf_op jit(solution)/shard_map/all_to_all | solution.py:73
  85.6 1.3 copy.160
  88.5 2.6 fusion.112
  91.1 1.5 reshape.478
  92.6 1.4 slice.398
  94.7 2.4 fusion.41
  101.6 1.4 fusion.98
  106.0 2.6 scatter_custom_fusion
  108.7 1.2 compare_and_fusion.1
  112.7 1.6 fusion.21
  114.3 1.3 fusion.111
  117.2 1.6 convolution_multiply_fusion
  119.0 11.7 %all-gather = f32[128,2,514]{2,0,1:T(8,128)S(1)} all-gather(f32[32,2,514]{2,0,1:T(8,128)S(1)} %pad_maximum_fusion), channel_id=2, replica_groups=mesh['dp'=4,'expert'=8] {'dp'}, dimensions={0}, use_global_device_ids=true | all-gather | bytes 657920 | tf_op jit(solution)/shard_map/all_gather | solution.py:234
  132.8 1.7 copy.194
  134.5 3.0 multiply_reduce_fusion
  139.0 1.8 fusion.23
  140.8 131.2 %all-to-all-done.1 = bf16[8,2,3,176,512]{4,3,2,1,0:T(8,128)(2,1)} async-done(((bf16[8,2,3,176,512]{4,3,2,1,0:T(8,128)(2,1)}), bf16[8,2,3,176,512]{4,3,2,1,0:T(8,128)(2,1)}, u32[]{:S(2)}, u32[]{:S(2)}) %all-to-all-start.1) | async-done | bytes 8650784 | tf_op jit(solution)/shard_map/all_to_all | solution.py:73
  272.0 14.9 %all-gather.1 = f32[64,2048]{1,0:T(8,128)S(1)} all-gather(f32[8,2048]{1,0:T(8,128)S(1)} %fusion.23), channel_id=3, replica_groups=mesh['dp'=4,'expert'=8] {'expert'}, dimensions={0}, use_global_device_ids=true | all-gather | bytes 589824 | tf_op jit(solution)/shard_map/all_gather | solution.py:268
  287.1 6.5 %gather_fusion.6 = bf16[8,3,176,512]{3,2,1,0:T(8,128)(2,1)} fusion(bf16[16,3,176,512]{3,2,1,0:T(8,128)(2,1)} %bitcast.146, s32[1024]{0:T(1024)} %get-tuple-element.306), kind=kCustom, calls=%fused_computation.1.clone | custom fusion | bytes 8650784 | tf_op jit(solution)/shard_map/jit(_take)/gather | solution.py:131
  293.6 4.7 %broadcast_select_fusion = bf16[8,3,176,512]{3,2,1,0:T(8,128)(2,1)} fusion(bf16[8,3,176,512]{3,2,1,0:T(8,128)(2,1)} %gather_fusion.6, pred[8]{0:T(512)(128)(4,1)S(1)} %copy-done.46), kind=kLoop, calls=%fused_computation.78 | loop fusion | flops 2162688 | bytes 8650760 | tf_op jit(solution)/shard_map/jit(_take)/select_n | solution.py:131
  299.1 4.6 %all-to-all-start.2 = ((bf16[8,3,176,512]{3,2,1,0:T(8,128)(2,1)}), bf16[8,3,176,512]{3,2,1,0:T(8,128)(2,1)}, u32[]{:S(2)}, u32[]{:S(2)}) async-start(bf16[8,3,176,512]{3,2,1,0:T(8,128)(2,1)} %get-tuple-element.308), calls=%async_computation.2 | async-start | bytes 8650752 | tf_op jit(solution)/shard_map/all_to_all | solution.py:145
  305.8 4.5 %compare_select_fusion.4 = (s32[192,1]{0,1:T(1,128)S(1)}, s32[192,1]{0,1:T(1,128)S(1)}) fusion(s32[]{:T(128)} %bitcast.166, s32[]{:T(128)} %bitcast.167, s32[]{:T(128)} %bitcast.168, s32[]{:T(128)} %bitcast.169, s32[]{:T(128)} %bitcast.170, s32[]{:T(128)} %bitcast.172, s32[]{:T(128)} %bitcast.171, s32[192,1]{0,1:T(1,128)S(1)} %copy-done.43), kind=kLoop, calls=%fused_computation.303 | loop fusion | flops 2880 | bytes 2332 | tf_op jit(solution)/shard_map/gather | solution.py:304
  310.3 10.7 %select_subtract_fusion = s32[192]{0:T(256)S(1)} fusion(pred[192]{0:T(512)(128)(4,1)S(1)} %get-tuple-element.119, pred[192]{0:T(512)(128)(4,1)S(1)} %get-tuple-element.118, pred[192]{0:T(512)(128)(4,1)S(1)} %get-tuple-element.117, pred[192]{0:T(512)(128)(4,1)S(1)} %get-tuple-element.116, pred[192]{0:T(512)(128)(4,1)S(1)} %get-tuple-element.115, ...), kind=kLoop, calls=%fused_computation.333 | loop fusion | flops 3456 | bytes 4872 | tf_op jit(solution)/shard_map/sub | solution.py:306
  321.1 1.2 reduce-window.6
  323.3 8.4 %all_gather.39 = bf16[32,2048]{1,0:T(8,128)(2,1)S(1)} all-gather(bf16[8,2048]{1,0:T(8,128)(2,1)S(1)} %multiply_convert_fusion), channel_id=1, replica_groups=mesh['dp'=4,'expert'=8] {'dp'}, dimensions={0}, use_global_device_ids=true | all-gather | bytes 163840 | tf_op jit(solution)/shard_map/all_gather | solution.py:278
  331.8 6.9 %convolution_bitcast_fusion.1 = f32[4,2,16,1408]{3,2,1,0:T(8,128)} fusion(bf16[4,2,1408,512]{3,2,1,0:T(8,128)(2,1)} %param.36, bf16[32,512,1]{1,0,2:T(8,128)(2,1)S(1)} %reshape.672, bf16[32,4,16]{0,2,1:T(8,128)(2,1)S(1)} %get-tuple-element.101), kind=kOutput, calls=%fused_computation.82 | convolution fusion | flops 186679296 | bytes 12292096 | tf_op jit(solution)/shard_map/scd,sgfd->sgcf/dot_general | solution.py:319
  342.4 4.2 convolution_bitcast_fusion
  346.6 11.6 %all-gather.3 = f32[8,4,2816]{2,1,0:T(4,128)S(1)} all-gather(f32[2,4,2816]{2,1,0:T(4,128)S(1)} %convolution_bitcast_fusion), channel_id=5, replica_groups=mesh['dp'=4,'expert'=8] {'dp'}, dimensions={0}, use_global_device_ids=true | all-gather | bytes 450560 | tf_op jit(solution)/shard_map/all_gather | solution.py:86
  358.3 5.5 %broadcast_multiply_fusion.1 = bf16[4,1408,512]{2,1,0:T(8,128)(2,1)} fusion(bf16[4,1408,512]{2,1,0:T(8,128)(2,1)} %param.37, bf16[]{:T(256)} %bitcast.195), kind=kLoop, calls=%fused_computation.80 | loop fusion | flops 2883584 | bytes 11534338 | tf_op jit(solution)/shard_map/mul | solution.py:281
  363.9 9.9 %broadcast_multiply_fusion = bf16[4,2,1408,512]{3,2,1,0:T(8,128)(2,1)} fusion(bf16[4,2,1408,512]{3,2,1,0:T(8,128)(2,1)} %param.36, bf16[]{:T(256)} %bitcast.195), kind=kLoop, calls=%fused_computation.77 | loop fusion | flops 5767168 | bytes 23068674 | tf_op jit(solution)/shard_map/mul | solution.py:280
  373.8 10.1 %all-gather.7.cloned.1.call-done = f32[16,2,16,1408]{3,2,1,0:T(8,128)} async-done(((f32[4,2,16,1408]{3,2,1,0:T(8,128)}), f32[16,2,16,1408]{3,2,1,0:T(8,128)}) %all-gather.7.cloned.1.call-update) | async-done | bytes 2883600 | tf_op jit(solution)/shard_map/all_gather | solution.py:86
  383.9 2.9 reduce_sum.137
  386.8 3.7 fusion.33
  390.8 9.7 %all-to-all-done.2 = bf16[8,3,176,512]{3,2,1,0:T(8,128)(2,1)} async-done(((bf16[8,3,176,512]{3,2,1,0:T(8,128)(2,1)}), bf16[8,3,176,512]{3,2,1,0:T(8,128)(2,1)}, u32[]{:S(2)}, u32[]{:S(2)}) %all-to-all-start.2) | async-done | bytes 4325408 | tf_op jit(solution)/shard_map/all_to_all | solution.py:145
  400.5 4.6 %copy.179 = bf16[1,3,8,176,512]{4,3,2,1,0:T(8,128)(2,1)} copy(bf16[1,3,8,176,512]{4,3,1,2,0:T(8,128)(2,1)} %bitcast.187) | data formatting | bytes 8650752 | tf_op jit(solution)/shard_map/all_to_all | solution.py:145
  406.4 2.6 all-to-all-start.3
  408.9 3.6 slice_dynamic-update-slice_fusion
  412.5 2.6 bitcast_dynamic-update-slice_fusion
  415.1 1.2 all-to-all-done.3
  (239 shorter events, 50.0 us)
Async XLA Ops:
  7.2 397.9 %copy-start = (bf16[2816,512]{1,0:T(8,128)(2,1)S(1)}, bf16[2816,512]{1,0:T(8,128)(2,1)}, u32[]{:S(2)}) copy-start(bf16[2816,512]{1,0:T(8,128)(2,1)} %param.39) | copy-start | bytes 8650756
  9.3 7.5 %copy-start.48 = (s32[8]{0:T(128)}, s32[8]{0:T(128)S(1)}, u32[]{:S(2)}) copy-start(s32[8]{0:T(128)S(1)} %get-tuple-element.43) | copy-start | bytes 100
  10.8 1.7 copy-start.37
  11.6 1.3 copy-start.39
  12.3 0.6 copy-start.40
  46.2 8.0 %copy-start.1 = (bf16[4,2,1408,512]{3,2,1,0:T(8,128)(2,1)S(1)}, bf16[4,2,1408,512]{3,2,1,0:T(8,128)(2,1)}, u32[]{:S(2)}) copy-start(bf16[4,2,1408,512]{3,2,1,0:T(8,128)(2,1)} %param.36) | copy-start | bytes 34603012
  59.9 2.8 copy-start.24
  59.9 2.8 copy-start.25
  59.9 2.9 copy-start.20
  59.9 2.9 copy-start.21
  61.3 1.8 copy-start.15
  61.4 2.3 copy-start.16
  63.7 1.4 copy-start.11
  63.7 1.8 copy-start.12
  65.6 1.4 copy-start.7
  65.7 1.8 copy-start.8
  65.8 2.1 copy-start.3
  65.9 2.5 copy-start.4
  77.4 6.5 %copy-start.44 = (s32[32,6]{0,1:T(8,128)S(1)}, s32[32,6]{0,1:T(8,128)}, u32[]{:S(2)}) copy-start(s32[32,6]{0,1:T(8,128)} %param.32) | copy-start | bytes 2308
  77.4 7.4 %copy-start.35 = (s32[32,16]{0,1:T(8,128)S(1)}, s32[32,16]{0,1:T(8,128)}, u32[]{:S(2)}) copy-start(s32[32,16]{0,1:T(8,128)} %param.29) | copy-start | bytes 6148
  77.4 194.6 %all-to-all-start.1 = ((bf16[8,2,3,176,512]{4,3,2,1,0:T(8,128)(2,1)}), bf16[8,2,3,176,512]{4,3,2,1,0:T(8,128)(2,1)}, u32[]{:S(2)}, u32[]{:S(2)}) async-start(bf16[8,2,3,176,512]{4,3,2,1,0:T(8,128)(2,1)} %fusion.19), calls=%async_computation.1 | async-start | bytes 17301504 | tf_op jit(solution)/shard_map/all_to_all | solution.py:73
  86.8 12.3 %copy-start.19 = (bf16[512,512]{0,1:T(8,128)(2,1)}, bf16[512,512]{0,1:T(8,128)(2,1)S(1)}, u32[]{:S(2)}) copy-start(bf16[512,512]{0,1:T(8,128)(2,1)S(1)} %copy.160) | copy-start | bytes 1572868
  87.8 0.7 copy-start.29
  93.9 3.5 copy-start.30
  97.1 0.6 copy-start.32
  97.7 0.6 copy-start.33
  97.7 0.6 copy-start.34
  100.1 0.6 copy-start.31
  106.0 4.0 copy-start.41
  130.8 0.8 copy-start.28
  287.1 6.5 %copy-start.46 = (pred[8]{0:T(512)(128)(4,1)S(1)}, pred[8]{0:T(512)(128)(4,1)}, u32[]{:S(2)}) copy-start(pred[8]{0:T(512)(128)(4,1)} %get-tuple-element.122) | copy-start | bytes 28
  293.6 4.7 %copy-start.42 = (s32[8]{0:T(128)S(1)}, s32[8]{0:T(128)}, u32[]{:S(2)}) copy-start(s32[8]{0:T(128)} %copy-done.41) | copy-start | bytes 100
  293.6 4.7 %copy-start.47 = (s32[8]{0:T(128)S(1)}, s32[8]{0:T(128)}, u32[]{:S(2)}) copy-start(s32[8]{0:T(128)} %get-tuple-element.124) | copy-start | bytes 100
  298.3 0.7 copy-start.36
  299.1 4.6 %copy-start.38 = (s32[32]{0:T(128)S(1)}, s32[32]{0:T(128)}, u32[]{:S(2)}) copy-start(s32[32]{0:T(128)} %copy-done.37) | copy-start | bytes 388
  299.1 6.7 %copy-start.43 = (s32[192,1]{0,1:T(1,128)S(1)}, s32[192,1]{0,1:T(1,128)}, u32[]{:S(2)}) copy-start(s32[192,1]{0,1:T(1,128)} %reshape_reshape.3) | copy-start | bytes 2308
  299.1 23.6 %copy-start.45 = (f32[32,6]{0,1:T(8,128)S(1)}, f32[32,6]{0,1:T(8,128)}, u32[]{:S(2)}) copy-start(f32[32,6]{0,1:T(8,128)} %param.33) | copy-start | bytes 2308
  299.1 101.4 %all-to-all-start.2 = ((bf16[8,3,176,512]{3,2,1,0:T(8,128)(2,1)}), bf16[8,3,176,512]{3,2,1,0:T(8,128)(2,1)}, u32[]{:S(2)}, u32[]{:S(2)}) async-start(bf16[8,3,176,512]{3,2,1,0:T(8,128)(2,1)} %get-tuple-element.308), calls=%async_computation.2 | async-start | bytes 8650752 | tf_op jit(solution)/shard_map/all_to_all | solution.py:145
  303.7 80.2 %all-gather.7.cloned.1.call-start = ((), (), s32[]{:S(2)}) async-start(), calls=%async_computation.4 | async-start | bytes 3604480 | tf_op jit(solution)/shard_map/all_gather | solution.py:86
  331.8 6.9 %copy-start.49 = (s32[8]{0:T(128)S(1)}, s32[8]{0:T(128)}, u32[]{:S(2)}) copy-start(s32[8]{0:T(128)} %copy-done.48) | copy-start | bytes 100
  406.4 10.0 %all-to-all-start.3 = ((f32[32,1,512]{2,1,0:T(1,128)}), f32[32,1,512]{2,1,0:T(1,128)S(1)}, u32[]{:S(2)}, u32[]{:S(2)}) async-start(f32[32,1,512]{2,1,0:T(1,128)} %copy.181), calls=%async_computation.3 | async-start | bytes 131072 | tf_op jit(solution)/shard_map/all_to_all | solution.py:339
Sparse Core Ops, SparseCore 0:
  338.8 45.0 all-gather.6

commit v4 on v2

--- a/solution.py
+++ b/solution.py
@@ -118,13 +118,13 @@
     ex_count = src_dev.shape[0]
     slots_local = expert_gate_up.shape[0]
     fast = spread.shape[0] // ex_count
-    out_a = pick_rows(spread, src_dev * fast + jnp.minimum(src_rank, fast - 1))
+    out_a = jnp.take(spread, src_dev * fast + jnp.minimum(src_rank, fast - 1), axis=0, mode="clip")
     if slots_local > fast:
         rest = slots_local - fast
 
         def extra():
             spread_b = spread_slots(pick_slots(expert_gate_up, expert_down, my_picks[fast:]), ex_count)
-            out_b = pick_rows(spread_b, src_dev * rest + jnp.clip(src_rank - fast, 0, rest - 1))
+            out_b = jnp.take(spread_b, src_dev * rest + jnp.clip(src_rank - fast, 0, rest - 1), axis=0, mode="clip")
             return jnp.where((src_rank < fast)[:, None, None, None], out_a, out_b)
 
         out_a = lax.cond(load > fast, extra, lambda: out_a)

time: 418 us -> 409 us (0.978)
  waiting for transfers between devices: 119 us -> 136 us
  between operations: 38.1 us -> 23.5 us
  local copies, waits for them, and re-layouts: 79.3 us -> 69.8 us
    all_to_all x1, waiting for transfers between devices: 98 us -> 115 us  [spread_slots(): lax.all_to_all(pieces, 'expert', split_axis=0, concat_axis=0, tiled=True)]
    unnamed x75 -> x66, local copies, waits for them, and re-layouts: 25.9 us -> 12.6 us
    transpose x0 -> x1, local copies, waits for them, and re-layouts: none -> 7.57 us  [spread_slots(): pieces = pieces.transpose(2, 0, 1, 3, 4)]
    reshape x1 -> x0, local copies, waits for them, and re-layouts: 7.57 us -> none  [spread_slots(): chosen.reshape(count, parts, ex_count, ff_width // ex_count, col_width)]
    gather x0 -> x1, local copies, waits for them, and re-layouts: none -> 6.3 us  [migrate_route(): jnp.take(spread, src_dev * fast + jnp.minimum(src_rank, fast - 1), axis=0...]
where the time goes in v4:
time: 409 us; the launch traced here: 407 us
  waiting for transfers between devices  136 us (33%)
  blocking collectives  70.8 us (17%)
  local copies, waits for them, and re-layouts  69.8 us (17%)
  other arithmetic  63.6 us (16%)
  matrix products  31 us (8%)
  between operations  23.5 us (6%)
  starting transfers between devices  12.3 us (3%)
    all_to_all x1, waiting for transfers between devices, spread_slots(): lax.all_to_all(pieces, 'expert', split_axis=0, concat_axis=0, tiled=True)  115 us
    all_gather x1, blocking collectives, gather_rows(): by_expert = lax.all_gather(rows, 'expert', axis=0, tiled=True)  15.9 us
    all_gather x1, blocking collectives, local(): lax.all_gather(partial_value, 'expert', axis=0, tiled=False)  15.1 us
    unnamed x66, local copies, waits for them, and re-layouts  12.6 us
    all_gather x1, blocking collectives, local(): gathered = lax.all_gather(packed, 'dp', axis=0, tiled=False)  11.5 us
    all_gather x1, blocking collectives, sum_over(): return jnp.sum(lax.all_gather(values, axis, axis=0, tiled=False), axis=0)  11.4 us
    sub x1, other arithmetic, local(): local_slot = slot_of - ex_index * slots_local  10.7 us
    all_to_all x1, waiting for transfers between devices, deliver(): lax.all_to_all(outgoing, 'expert', split_axis=0, concat_axis=2, tiled=True)  10.2 us
  transfers between devices with their start and end apart: 4, of which 4 were waited for; matrix products, arithmetic and copies ran while one was open for 29% of the time, Pallas kernels for 0%

profile of v4, /device:TPU:0, one launch (start us, length us, event | category | flops | bytes accessed | tf_op | source)
XLA Modules:
  0.0 406.8 jit_solution(16729001158379053923)
XLA Ops:
  9.5 1.3 gather_fusion.6
  22.5 15.9 %all-gather.4 = bf16[8,1,2048]{2,1,0:T(2,128)(2,1)S(1)} all-gather(bf16[1,1,2048]{2,1,0:T(2,128)(2,1)} %bitcast.237), channel_id=1, replica_groups=mesh['dp'=4,'expert'=8] {'expert'}, dimensions={0}, use_global_device_ids=true | all-gather | bytes 36864 | tf_op jit(solution)/shard_map/all_gather | solution.py:47
  38.3 8.5 %all_gather.34 = bf16[32,2048]{1,0:T(8,128)(2,1)S(1)} all-gather(bf16[8,2048]{1,0:T(8,128)(2,1)S(1)} %bitcast.230), channel_id=1, replica_groups=mesh['dp'=4,'expert'=8] {'dp'}, dimensions={0}, use_global_device_ids=true | all-gather | bytes 163840 | tf_op jit(solution)/shard_map/all_gather | solution.py:48
  48.1 2.1 constant_dynamic-slice_fusion.9
  50.2 3.1 constant_dynamic-slice_fusion.11
  53.6 3.9 pad_maximum_fusion.2
  57.5 7.6 %copy.188 = bf16[8,2,3,176,512]{4,3,2,1,0:T(8,128)(2,1)} copy(bf16[8,2,3,176,512]{4,3,0,2,1:T(8,128)(2,1)} %bitcast.217) | data formatting | bytes 17301504 | tf_op jit(solution)/shard_map/transpose | solution.py:62
  65.0 5.1 %all-to-all-start.1 = ((bf16[8,2,3,176,512]{4,3,2,1,0:T(8,128)(2,1)}), bf16[8,2,3,176,512]{4,3,2,1,0:T(8,128)(2,1)}, u32[]{:S(2)}, u32[]{:S(2)}) async-start(bf16[8,2,3,176,512]{4,3,2,1,0:T(8,128)(2,1)} %copy.188), calls=%async_computation.1 | async-start | bytes 17301504 | tf_op jit(solution)/shard_map/all_to_all | solution.py:63
  74.5 2.6 fusion.90
  77.1 1.5 reshape.370
  83.7 2.6 scatter_custom_fusion
  87.5 2.1 gather_fusion.1
  92.6 1.3 gather_fusion.2
  93.9 1.6 fusion.5
  95.5 1.9 fusion.89
  100.0 1.3 select_reduce_fusion.1
  102.1 1.3 gather_fusion.3
  105.1 1.4 convolution_bitcast_fusion.3
  106.6 1.4 copy.184
  107.9 1.3 copy.183
  109.3 1.3 dynamic_slice.75
  110.6 1.6 convolution_multiply_fusion
  113.9 11.5 %all-gather = f32[128,2,514]{2,0,1:T(8,128)S(1)} all-gather(f32[32,2,514]{2,0,1:T(8,128)S(1)} %pad_maximum_fusion.3), channel_id=2, replica_groups=mesh['dp'=4,'expert'=8] {'dp'}, dimensions={0}, use_global_device_ids=true | all-gather | bytes 657920 | tf_op jit(solution)/shard_map/all_gather | solution.py:224
  127.0 2.5 copy.212
  129.5 1.5 fusion.84
  131.1 3.0 multiply_reduce_fusion
  135.8 2.4 fusion.25
  143.4 1.8 fusion.7
  145.1 114.5 %all-to-all-done.1 = bf16[8,2,3,176,512]{4,3,2,1,0:T(8,128)(2,1)} async-done(((bf16[8,2,3,176,512]{4,3,2,1,0:T(8,128)(2,1)}), bf16[8,2,3,176,512]{4,3,2,1,0:T(8,128)(2,1)}, u32[]{:S(2)}, u32[]{:S(2)}) %all-to-all-start.1) | async-done | bytes 8650784 | tf_op jit(solution)/shard_map/all_to_all | solution.py:63
  259.7 15.1 %all-gather.1 = f32[64,2048]{1,0:T(8,128)S(1)} all-gather(f32[8,2048]{1,0:T(8,128)S(1)} %fusion.7), channel_id=3, replica_groups=mesh['dp'=4,'expert'=8] {'expert'}, dimensions={0}, use_global_device_ids=true | all-gather | bytes 589824 | tf_op jit(solution)/shard_map/all_gather | solution.py:258
  275.0 6.3 %gather_fusion.5 = bf16[8,3,176,512]{3,2,1,0:T(8,128)(2,1)} fusion(bf16[16,3,176,512]{3,2,1,0:T(8,128)(2,1)} %bitcast.37, s32[1024]{0:T(1024)S(1)} %pad_clamp_fusion.1), kind=kCustom, calls=%fused_computation.5 | custom fusion | bytes 8650784 | tf_op jit(solution)/shard_map/jit(_take)/gather | solution.py:121
  282.1 4.6 %all-to-all-start.2 = ((bf16[8,3,176,512]{3,2,1,0:T(8,128)(2,1)}), bf16[8,3,176,512]{3,2,1,0:T(8,128)(2,1)}, u32[]{:S(2)}, u32[]{:S(2)}) async-start(bf16[8,3,176,512]{3,2,1,0:T(8,128)(2,1)} %get-tuple-element.183), calls=%async_computation.2 | async-start | bytes 8650752 | tf_op jit(solution)/shard_map/all_to_all | solution.py:135
  288.7 4.5 %compare_select_fusion.3 = (s32[192,1]{0,1:T(1,128)S(1)}, s32[192,1]{0,1:T(1,128)S(1)}) fusion(s32[]{:T(128)} %bitcast.57, s32[]{:T(128)} %bitcast.58, s32[]{:T(128)} %bitcast.59, s32[]{:T(128)} %bitcast.60, s32[]{:T(128)} %bitcast.61, s32[]{:T(128)} %bitcast.63, s32[]{:T(128)} %bitcast.62, s32[192,1]{0,1:T(1,128)S(1)} %copy-done.21), kind=kLoop, calls=%fused_computation.183 | loop fusion | flops 2880 | bytes 2332 | tf_op jit(solution)/shard_map/gather | solution.py:294
  293.3 10.7 %select_subtract_fusion = s32[192]{0:T(256)S(1)} fusion(pred[192]{0:T(512)(128)(4,1)S(1)} %get-tuple-element.118, pred[192]{0:T(512)(128)(4,1)S(1)} %get-tuple-element.117, pred[192]{0:T(512)(128)(4,1)S(1)} %get-tuple-element.116, pred[192]{0:T(512)(128)(4,1)S(1)} %get-tuple-element.115, pred[192]{0:T(512)(128)(4,1)S(1)} %get-tuple-element.114, ...), kind=kLoop, calls=%fused_computation.211 | loop fusion | flops 3456 | bytes 4872 | tf_op jit(solution)/shard_map/sub | solution.py:296
  306.2 8.4 %all_gather.39 = bf16[32,2048]{1,0:T(8,128)(2,1)S(1)} all-gather(bf16[8,2048]{1,0:T(8,128)(2,1)S(1)} %multiply_convert_fusion), channel_id=1, replica_groups=mesh['dp'=4,'expert'=8] {'dp'}, dimensions={0}, use_global_device_ids=true | all-gather | bytes 163840 | tf_op jit(solution)/shard_map/all_gather | solution.py:268
  314.8 6.9 %convolution_bitcast_fusion.1 = f32[4,2,16,1408]{3,2,1,0:T(8,128)} fusion(bf16[4,2,1408,512]{3,2,1,0:T(8,128)(2,1)} %param.34, bf16[32,512,1]{1,0,2:T(8,128)(2,1)S(1)} %reshape.561, bf16[32,4,16]{0,2,1:T(8,128)(2,1)S(1)} %get-tuple-element.100), kind=kOutput, calls=%fused_computation.25 | convolution fusion | flops 186679296 | bytes 12292096 | tf_op jit(solution)/shard_map/scd,sgfd->sgcf/dot_general | solution.py:309
  324.7 4.2 %convolution_bitcast_fusion = f32[2,4,2816]{2,1,0:T(4,128)S(1)} fusion(bf16[2,2816,512]{2,1,0:T(8,128)(2,1)} %param.36, bf16[4,1,1,512]{3,1,0,2:T(2,128)(2,1)S(1)} %constant_dynamic-slice_fusion.6), kind=kOutput, calls=%fused_computation.21 | convolution fusion | flops 23068672 | bytes 5861376 | tf_op jit(solution)/shard_map/td,gfd->gtf/dot_general | solution.py:312
  328.9 11.4 %all-gather.3 = f32[8,4,2816]{2,1,0:T(4,128)S(1)} all-gather(f32[2,4,2816]{2,1,0:T(4,128)S(1)} %convolution_bitcast_fusion), channel_id=5, replica_groups=mesh['dp'=4,'expert'=8] {'dp'}, dimensions={0}, use_global_device_ids=true | all-gather | bytes 450560 | tf_op jit(solution)/shard_map/all_gather | solution.py:76
  341.0 5.5 %broadcast_multiply_fusion.1 = bf16[4,1408,512]{2,1,0:T(8,128)(2,1)} fusion(bf16[4,1408,512]{2,1,0:T(8,128)(2,1)} %param.35, bf16[]{:T(256)} %bitcast.86), kind=kLoop, calls=%fused_computation.23 | loop fusion | flops 2883584 | bytes 11534338 | tf_op jit(solution)/shard_map/mul | solution.py:271
  346.6 9.9 %broadcast_multiply_fusion = bf16[4,2,1408,512]{3,2,1,0:T(8,128)(2,1)} fusion(bf16[4,2,1408,512]{3,2,1,0:T(8,128)(2,1)} %param.34, bf16[]{:T(256)} %bitcast.86), kind=kLoop, calls=%fused_computation.20 | loop fusion | flops 5767168 | bytes 23068674 | tf_op jit(solution)/shard_map/mul | solution.py:270
  356.5 9.9 %all-gather.7.cloned.1.call-done = f32[16,2,16,1408]{3,2,1,0:T(8,128)} async-done(((f32[4,2,16,1408]{3,2,1,0:T(8,128)}), f32[16,2,16,1408]{3,2,1,0:T(8,128)}) %all-gather.7.cloned.1.call-update) | async-done | bytes 2883600 | tf_op jit(solution)/shard_map/all_gather | solution.py:76
  366.4 2.9 reduce_sum.137
  369.3 3.7 fusion.17
  373.3 10.2 %all-to-all-done.2 = bf16[8,3,176,512]{3,2,1,0:T(8,128)(2,1)} async-done(((bf16[8,3,176,512]{3,2,1,0:T(8,128)(2,1)}), bf16[8,3,176,512]{3,2,1,0:T(8,128)(2,1)}, u32[]{:S(2)}, u32[]{:S(2)}) %all-to-all-start.2) | async-done | bytes 4325408 | tf_op jit(solution)/shard_map/all_to_all | solution.py:135
  383.4 4.6 %copy.197 = bf16[1,3,8,176,512]{4,3,2,1,0:T(8,128)(2,1)} copy(bf16[1,3,8,176,512]{4,3,1,2,0:T(8,128)(2,1)} %bitcast.78) | data formatting | bytes 8650752 | tf_op jit(solution)/shard_map/all_to_all | solution.py:135
  389.3 2.6 all-to-all-start.3
  391.9 3.6 slice_dynamic-update-slice_fusion
  395.5 2.6 bitcast_dynamic-update-slice_fusion
  (191 shorter events, 47.7 us)
Async XLA Ops:
  7.2 380.9 %copy-start = (bf16[2816,512]{1,0:T(8,128)(2,1)S(1)}, bf16[2816,512]{1,0:T(8,128)(2,1)}, u32[]{:S(2)}) copy-start(bf16[2816,512]{1,0:T(8,128)(2,1)} %param.37) | copy-start | bytes 8650756
  8.2 4.8 %copy-start.18 = (s32[32]{0:T(128)}, s32[32]{0:T(128)S(1)}, u32[]{:S(2)}) copy-start(s32[32]{0:T(128)S(1)} %eq.139) | copy-start | bytes 388
  9.4 1.5 copy-start.26
  11.6 0.8 copy-start.14
  12.3 0.6 copy-start.20
  16.1 37.2 %copy-start.5 = (s32[8,4]{1,0:T(8,128)}, s32[8,4]{1,0:T(8,128)S(1)}, u32[]{:S(2)}) copy-start(s32[8,4]{1,0:T(8,128)S(1)} %reduce_window_sum.26) | copy-start | bytes 388
  18.7 0.6 copy-start.10
  65.0 6.4 %copy-start.22 = (s32[32,6]{0,1:T(8,128)S(1)}, s32[32,6]{0,1:T(8,128)}, u32[]{:S(2)}) copy-start(s32[32,6]{0,1:T(8,128)} %param.30) | copy-start | bytes 2308
  65.0 8.7 %copy-start.13 = (f32[2048]{0:T(1024)S(1)}, f32[2048]{0:T(1024)}, u32[]{:S(2)}) copy-start(f32[2048]{0:T(1024)} %param.21) | copy-start | bytes 24580
  65.0 194.6 %all-to-all-start.1 = ((bf16[8,2,3,176,512]{4,3,2,1,0:T(8,128)(2,1)}), bf16[8,2,3,176,512]{4,3,2,1,0:T(8,128)(2,1)}, u32[]{:S(2)}, u32[]{:S(2)}) async-start(bf16[8,2,3,176,512]{4,3,2,1,0:T(8,128)(2,1)} %copy.188), calls=%async_computation.1 | async-start | bytes 17301504 | tf_op jit(solution)/shard_map/all_to_all | solution.py:63
  73.6 55.9 %copy-start.1 = (bf16[512,512]{0,1:T(8,128)(2,1)}, bf16[512,512]{0,1:T(8,128)(2,1)S(1)}, u32[]{:S(2)}) copy-start(bf16[512,512]{0,1:T(8,128)(2,1)S(1)} %copy.177) | copy-start | bytes 1572868
  73.8 0.6 copy-start.3
  79.6 0.6 copy-start.4
  86.9 0.6 copy-start.12
  87.5 4.4 %copy-start.17 = (s32[1024]{0:T(1024)}, s32[1024]{0:T(1024)S(1)}, u32[]{:S(2)}) copy-start(s32[1024]{0:T(1024)S(1)} %pad_clamp_fusion.3) | copy-start | bytes 12292
  89.7 0.8 copy-start.24
  90.3 0.6 copy-start.25
  91.9 0.6 copy-start.8
  91.9 0.6 copy-start.9
  97.4 0.6 copy-start.7
  125.4 0.8 copy-start.2
  126.3 14.9 %copy-start.6 = (s32[8,4]{1,0:T(8,128)S(1)}, s32[8,4]{1,0:T(8,128)}, u32[]{:S(2)}) copy-start(s32[8,4]{1,0:T(8,128)} %copy-done.5) | copy-start | bytes 388
  126.3 15.0 %copy-start.15 = (s32[8]{0:T(128)S(1)}, s32[8]{0:T(128)}, u32[]{:S(2)}) copy-start(s32[8]{0:T(128)} %copy-done.14) | copy-start | bytes 100
  274.9 6.3 %copy-start.11 = (s32[1,4]{0,1:T(4,128)S(1)}, s32[1,4]{0,1:T(4,128)}, u32[]{:S(2)}) copy-start(s32[1,4]{0,1:T(4,128)} %copy-done.10) | copy-start | bytes 52
  281.3 0.7 copy-start.16
  282.0 4.6 %copy-start.19 = (s32[32]{0:T(128)S(1)}, s32[32]{0:T(128)}, u32[]{:S(2)}) copy-start(s32[32]{0:T(128)} %copy-done.18) | copy-start | bytes 388
  282.0 6.7 %copy-start.21 = (s32[192,1]{0,1:T(1,128)S(1)}, s32[192,1]{0,1:T(1,128)}, u32[]{:S(2)}) copy-start(s32[192,1]{0,1:T(1,128)} %reshape_reshape.3) | copy-start | bytes 2308
  282.0 23.9 %copy-start.23 = (f32[32,6]{0,1:T(8,128)S(1)}, f32[32,6]{0,1:T(8,128)}, u32[]{:S(2)}) copy-start(f32[32,6]{0,1:T(8,128)} %param.31) | copy-start | bytes 2308
  282.1 101.4 %all-to-all-start.2 = ((bf16[8,3,176,512]{3,2,1,0:T(8,128)(2,1)}), bf16[8,3,176,512]{3,2,1,0:T(8,128)(2,1)}, u32[]{:S(2)}, u32[]{:S(2)}) async-start(bf16[8,3,176,512]{3,2,1,0:T(8,128)(2,1)} %get-tuple-element.183), calls=%async_computation.2 | async-start | bytes 8650752 | tf_op jit(solution)/shard_map/all_to_all | solution.py:135
  286.6 79.8 %all-gather.7.cloned.1.call-start = ((), (), s32[]{:S(2)}) async-start(), calls=%async_computation.4 | async-start | bytes 3604480 | tf_op jit(solution)/shard_map/all_gather | solution.py:76
  314.8 6.9 %copy-start.27 = (s32[8]{0:T(128)S(1)}, s32[8]{0:T(128)}, u32[]{:S(2)}) copy-start(s32[8]{0:T(128)} %copy-done.26) | copy-start | bytes 100
  389.3 10.0 %all-to-all-start.3 = ((f32[32,1,512]{2,1,0:T(1,128)}), f32[32,1,512]{2,1,0:T(1,128)S(1)}, u32[]{:S(2)}, u32[]{:S(2)}) async-start(f32[32,1,512]{2,1,0:T(1,128)} %copy.199), calls=%async_computation.3 | async-start | bytes 131072 | tf_op jit(solution)/shard_map/all_to_all | solution.py:329
Sparse Core Ops, SparseCore 0:
  321.8 44.5 all-gather.6

commit v5 on v4

--- a/solution.py
+++ b/solution.py
@@ -81,36 +81,33 @@
     slots = rows * slots_local
     ex_count = rows
     ff_width = expert_gate_up.shape[2]
+    local_ids = jnp.arange(slots_local, dtype=jnp.int32)
+    slot_ids = jnp.arange(slots, dtype=jnp.int32)
     changed = old_place != new_place
-    moved_slot = jnp.argmax(changed, axis=1)
-    wanted = jnp.take_along_axis(new_place, moved_slot[:, None], axis=1)[:, 0]
+    moved_slot = jnp.min(jnp.where(changed, local_ids[None, :], slots_local), axis=1)
+    wanted = jnp.sum(jnp.where(local_ids[None, :] == moved_slot[:, None], new_place, 0), axis=1)
     hit = old_place.reshape(-1)[None, :] == wanted[:, None]
-    first = jnp.argmax(hit, axis=1).astype(jnp.int32)
-    last = (slots - 1 - jnp.argmax(hit[:, ::-1], axis=1)).astype(jnp.int32)
-    slot_ids = jnp.arange(slots, dtype=jnp.int32)
-
-    def needed_of(src):
-        needed = jnp.any(src[:, None] == slot_ids[None, :], axis=0).reshape(rows, slots_local)
-        return needed, jnp.max(jnp.sum(needed.astype(jnp.int32), axis=1))
-
-    need_first, load_first = needed_of(first)
-    need_last, load_last = needed_of(last)
-    use_last = load_last < load_first
+    first = jnp.min(jnp.where(hit, slot_ids[None, :], slots), axis=1)
+    last = jnp.max(jnp.where(hit, slot_ids[None, :], -1), axis=1)
+    both = jnp.stack([first, last])
+    needed_both = jnp.any(both[:, :, None] == slot_ids[None, None, :], axis=1)
+    needed_both = needed_both.reshape(2, rows, slots_local)
+    loads = jnp.max(jnp.sum(needed_both.astype(jnp.int32), axis=2), axis=1)
+    use_last = loads[1] < loads[0]
     source = jnp.where(use_last, last, first)
-    needed = jnp.where(use_last, need_last, need_first)
-    load = jnp.minimum(load_first, load_last)
-    rank = jnp.cumsum(needed.astype(jnp.int32), axis=1) - 1
-    local_ids = jnp.arange(slots_local, dtype=jnp.int32)
-    picks = jnp.stack(
-        [jnp.argmax(needed & (rank == k), axis=1).astype(jnp.int32) for k in range(slots_local)],
-        axis=1,
-    )
-    my_picks = picks[ex_index]
+    needed = jnp.where(use_last, needed_both[1], needed_both[0]).astype(jnp.int32)
+    load = jnp.min(loads)
+    before = local_ids[None, None, :] <= local_ids[None, :, None]
+    rank = jnp.sum(jnp.where(before, needed[:, None, :], 0), axis=2) - 1
+    my_needed = lax.dynamic_index_in_dim(needed, ex_index, 0, False) > 0
+    my_rank = lax.dynamic_index_in_dim(rank, ex_index, 0, False)
+    at_rank = my_needed[None, :] & (my_rank[None, :] == local_ids[:, None])
+    my_picks = jnp.sum(jnp.where(at_rank, local_ids[None, :], 0), axis=1)
     src_dev = source // slots_local
-    src_rank = rank.reshape(-1)[source]
+    src_rank = jnp.sum(jnp.where(source[:, None] == slot_ids[None, :], rank.reshape(-1)[None, :], 0), axis=1)
     fast = min(2, slots_local)
     chosen = pick_slots(expert_gate_up, expert_down, my_picks[:fast])
-    return chosen, (my_picks, src_dev, src_rank, load, moved_slot[ex_index])
+    return chosen, (my_picks, src_dev, src_rank, load, lax.dynamic_index_in_dim(moved_slot, ex_index, 0, False))
 
 
 def migrate_route(spread, plan, expert_gate_up, expert_down):

time: 409 us -> 404 us (0.988)
    another operation x14 -> x6, other arithmetic: 8.26 us -> 2.97 us  [the longest x5 3.77 us: migrate_start(): moved_slot = jnp.argmax(changed, axis=1)]
    unnamed x66 -> x67, local copies, waits for them, and re-layouts: 12.6 us -> 13.6 us
  transfers between devices with their start and end apart: 4 -> 4, of which waited for: 4 -> 4; matrix products, arithmetic and copies ran while one was open for 29% -> 30% of each run, Pallas kernels for 0% -> 0%
where the time goes in v5:
time: 404 us; the launch traced here: 401 us
  waiting for transfers between devices  133 us (33%)
  local copies, waits for them, and re-layouts  70.7 us (18%)
  blocking collectives  70.6 us (17%)
  other arithmetic  60.9 us (15%)
  matrix products  30.9 us (8%)
  between operations  22.9 us (6%)
  starting transfers between devices  12.3 us (3%)
    all_to_all x1, waiting for transfers between devices, spread_slots(): lax.all_to_all(pieces, 'expert', split_axis=0, concat_axis=0, tiled=True)  112 us
    all_gather x1, blocking collectives, gather_rows(): by_expert = lax.all_gather(rows, 'expert', axis=0, tiled=True)  15.9 us
    all_gather x1, blocking collectives, local(): lax.all_gather(partial_value, 'expert', axis=0, tiled=False)  14.9 us
    unnamed x67, local copies, waits for them, and re-layouts  13.6 us
    all_gather x1, blocking collectives, local(): gathered = lax.all_gather(packed, 'dp', axis=0, tiled=False)  11.6 us
    all_gather x1, blocking collectives, sum_over(): return jnp.sum(lax.all_gather(values, axis, axis=0, tiled=False), axis=0)  11.4 us
    sub x1, other arithmetic, local(): local_slot = slot_of - ex_index * slots_local  10.7 us
    all_to_all x1, waiting for transfers between devices, deliver(): lax.all_to_all(outgoing, 'expert', split_axis=0, concat_axis=2, tiled=True)  10.2 us
  transfers between devices with their start and end apart: 4, of which 4 were waited for; matrix products, arithmetic and copies ran while one was open for 30% of the time, Pallas kernels for 0%

profile of v5, /device:TPU:0, one launch (start us, length us, event | category | flops | bytes accessed | tf_op | source)
XLA Modules:
  0.0 401.5 jit_solution(11601492270285566386)
XLA Ops:
  17.4 15.9 %all-gather.4 = bf16[8,1,2048]{2,1,0:T(2,128)(2,1)S(1)} all-gather(bf16[1,1,2048]{2,1,0:T(2,128)(2,1)} %bitcast.248), channel_id=1, replica_groups=mesh['dp'=4,'expert'=8] {'expert'}, dimensions={0}, use_global_device_ids=true | all-gather | bytes 36864 | tf_op jit(solution)/shard_map/all_gather | solution.py:47
  33.3 8.5 %all_gather.34 = bf16[32,2048]{1,0:T(8,128)(2,1)S(1)} all-gather(bf16[8,2048]{1,0:T(8,128)(2,1)S(1)} %bitcast.241), channel_id=1, replica_groups=mesh['dp'=4,'expert'=8] {'dp'}, dimensions={0}, use_global_device_ids=true | all-gather | bytes 163840 | tf_op jit(solution)/shard_map/all_gather | solution.py:48
  43.1 2.0 constant_dynamic-slice_fusion.9
  45.1 3.1 constant_dynamic-slice_fusion.11
  48.4 3.9 pad_maximum_fusion.2
  52.3 7.6 %copy.215 = bf16[8,2,3,176,512]{4,3,2,1,0:T(8,128)(2,1)} copy(bf16[8,2,3,176,512]{4,3,0,2,1:T(8,128)(2,1)} %bitcast.228) | data formatting | bytes 17301504 | tf_op jit(solution)/shard_map/transpose | solution.py:62
  59.9 5.1 %all-to-all-start.1 = ((bf16[8,2,3,176,512]{4,3,2,1,0:T(8,128)(2,1)}), bf16[8,2,3,176,512]{4,3,2,1,0:T(8,128)(2,1)}, u32[]{:S(2)}, u32[]{:S(2)}) async-start(bf16[8,2,3,176,512]{4,3,2,1,0:T(8,128)(2,1)} %copy.215), calls=%async_computation.1 | async-start | bytes 17301504 | tf_op jit(solution)/shard_map/all_to_all | solution.py:63
  68.7 2.6 fusion.95
  71.3 1.5 reshape.443
  78.0 2.6 scatter_custom_fusion
  81.8 2.1 gather_fusion.1
  86.8 1.3 gather_fusion.2
  88.2 1.6 fusion.5
  89.8 1.9 fusion.94
  94.2 1.3 select_reduce_fusion.1
  96.3 1.3 gather_fusion.3
  99.4 1.4 convolution_bitcast_fusion.3
  100.8 1.4 copy.211
  102.2 1.3 copy.210
  103.5 1.3 dynamic_slice.81
  104.8 1.6 convolution_multiply_fusion
  108.2 11.6 %all-gather = f32[128,2,514]{2,0,1:T(8,128)S(1)} all-gather(f32[32,2,514]{2,0,1:T(8,128)S(1)} %pad_maximum_fusion.3), channel_id=2, replica_groups=mesh['dp'=4,'expert'=8] {'dp'}, dimensions={0}, use_global_device_ids=true | all-gather | bytes 657920 | tf_op jit(solution)/shard_map/all_gather | solution.py:221
  121.2 2.5 copy.239
  123.7 1.5 fusion.88
  126.0 3.0 multiply_reduce_fusion
  130.7 2.4 fusion.25
  136.0 1.3 reduce_min.29
  140.9 1.8 fusion.7
  142.7 111.8 %all-to-all-done.1 = bf16[8,2,3,176,512]{4,3,2,1,0:T(8,128)(2,1)} async-done(((bf16[8,2,3,176,512]{4,3,2,1,0:T(8,128)(2,1)}), bf16[8,2,3,176,512]{4,3,2,1,0:T(8,128)(2,1)}, u32[]{:S(2)}, u32[]{:S(2)}) %all-to-all-start.1) | async-done | bytes 8650784 | tf_op jit(solution)/shard_map/all_to_all | solution.py:63
  254.5 14.9 %all-gather.1 = f32[64,2048]{1,0:T(8,128)S(1)} all-gather(f32[8,2048]{1,0:T(8,128)S(1)} %fusion.7), channel_id=3, replica_groups=mesh['dp'=4,'expert'=8] {'expert'}, dimensions={0}, use_global_device_ids=true | all-gather | bytes 589824 | tf_op jit(solution)/shard_map/all_gather | solution.py:255
  269.6 6.3 %gather_fusion.4 = bf16[8,3,176,512]{3,2,1,0:T(8,128)(2,1)} fusion(bf16[16,3,176,512]{3,2,1,0:T(8,128)(2,1)} %bitcast.34, s32[1024]{0:T(1024)S(1)} %pad_clamp_fusion.1), kind=kCustom, calls=%fused_computation.4 | custom fusion | bytes 8650784 | tf_op jit(solution)/shard_map/jit(_take)/gather | solution.py:118
  276.7 4.6 %all-to-all-start.2 = ((bf16[8,3,176,512]{3,2,1,0:T(8,128)(2,1)}), bf16[8,3,176,512]{3,2,1,0:T(8,128)(2,1)}, u32[]{:S(2)}, u32[]{:S(2)}) async-start(bf16[8,3,176,512]{3,2,1,0:T(8,128)(2,1)} %get-tuple-element.165), calls=%async_computation.2 | async-start | bytes 8650752 | tf_op jit(solution)/shard_map/all_to_all | solution.py:132
  283.4 4.5 %compare_select_fusion.5 = (s32[192,1]{0,1:T(1,128)S(1)}, s32[192,1]{0,1:T(1,128)S(1)}) fusion(s32[]{:T(128)} %bitcast.54, s32[]{:T(128)} %bitcast.55, s32[]{:T(128)} %bitcast.56, s32[]{:T(128)} %bitcast.57, s32[]{:T(128)} %bitcast.58, s32[]{:T(128)} %bitcast.60, s32[]{:T(128)} %bitcast.59, s32[192,1]{0,1:T(1,128)S(1)} %copy-done.20), kind=kLoop, calls=%fused_computation.184 | loop fusion | flops 2880 | bytes 2332 | tf_op jit(solution)/shard_map/gather | solution.py:291
  288.0 10.7 %select_subtract_fusion = s32[192]{0:T(256)S(1)} fusion(pred[192]{0:T(512)(128)(4,1)S(1)} %get-tuple-element.102, pred[192]{0:T(512)(128)(4,1)S(1)} %get-tuple-element.101, pred[192]{0:T(512)(128)(4,1)S(1)} %get-tuple-element.100, pred[192]{0:T(512)(128)(4,1)S(1)} %get-tuple-element.99, pred[192]{0:T(512)(128)(4,1)S(1)} %get-tuple-element.98, ...), kind=kLoop, calls=%fused_computation.215 | loop fusion | flops 3456 | bytes 4872 | tf_op jit(solution)/shard_map/sub | solution.py:293
  300.9 8.4 %all_gather.39 = bf16[32,2048]{1,0:T(8,128)(2,1)S(1)} all-gather(bf16[8,2048]{1,0:T(8,128)(2,1)S(1)} %multiply_convert_fusion), channel_id=1, replica_groups=mesh['dp'=4,'expert'=8] {'dp'}, dimensions={0}, use_global_device_ids=true | all-gather | bytes 163840 | tf_op jit(solution)/shard_map/all_gather | solution.py:265
  309.4 6.9 %convolution_bitcast_fusion.1 = f32[4,2,16,1408]{3,2,1,0:T(8,128)} fusion(bf16[4,2,1408,512]{3,2,1,0:T(8,128)(2,1)} %param.34, bf16[32,512,1]{1,0,2:T(8,128)(2,1)S(1)} %reshape.615, bf16[32,4,16]{0,2,1:T(8,128)(2,1)S(1)} %get-tuple-element.82), kind=kOutput, calls=%fused_computation.27 | convolution fusion | flops 186679296 | bytes 12292096 | tf_op jit(solution)/shard_map/scd,sgfd->sgcf/dot_general | solution.py:306
  319.4 4.2 %convolution_bitcast_fusion = f32[2,4,2816]{2,1,0:T(4,128)S(1)} fusion(bf16[2,2816,512]{2,1,0:T(8,128)(2,1)} %param.36, bf16[4,1,1,512]{3,1,0,2:T(2,128)(2,1)S(1)} %constant_dynamic-slice_fusion.6), kind=kOutput, calls=%fused_computation.23 | convolution fusion | flops 23068672 | bytes 5861376 | tf_op jit(solution)/shard_map/td,gfd->gtf/dot_general | solution.py:309
  323.6 11.4 %all-gather.3 = f32[8,4,2816]{2,1,0:T(4,128)S(1)} all-gather(f32[2,4,2816]{2,1,0:T(4,128)S(1)} %convolution_bitcast_fusion), channel_id=5, replica_groups=mesh['dp'=4,'expert'=8] {'dp'}, dimensions={0}, use_global_device_ids=true | all-gather | bytes 450560 | tf_op jit(solution)/shard_map/all_gather | solution.py:76
  335.7 5.5 %broadcast_multiply_fusion.1 = bf16[4,1408,512]{2,1,0:T(8,128)(2,1)} fusion(bf16[4,1408,512]{2,1,0:T(8,128)(2,1)} %param.35, bf16[]{:T(256)} %bitcast.86), kind=kLoop, calls=%fused_computation.25 | loop fusion | flops 2883584 | bytes 11534338 | tf_op jit(solution)/shard_map/mul | solution.py:268
  341.2 9.9 %broadcast_multiply_fusion = bf16[4,2,1408,512]{3,2,1,0:T(8,128)(2,1)} fusion(bf16[4,2,1408,512]{3,2,1,0:T(8,128)(2,1)} %param.34, bf16[]{:T(256)} %bitcast.86), kind=kLoop, calls=%fused_computation.22 | loop fusion | flops 5767168 | bytes 23068674 | tf_op jit(solution)/shard_map/mul | solution.py:267
  351.1 9.9 %all-gather.7.cloned.1.call-done = f32[16,2,16,1408]{3,2,1,0:T(8,128)} async-done(((f32[4,2,16,1408]{3,2,1,0:T(8,128)}), f32[16,2,16,1408]{3,2,1,0:T(8,128)}) %all-gather.7.cloned.1.call-update) | async-done | bytes 2883600 | tf_op jit(solution)/shard_map/all_gather | solution.py:76
  361.0 2.9 reduce_sum.167
  363.9 3.7 fusion.17
  367.9 10.2 %all-to-all-done.2 = bf16[8,3,176,512]{3,2,1,0:T(8,128)(2,1)} async-done(((bf16[8,3,176,512]{3,2,1,0:T(8,128)(2,1)}), bf16[8,3,176,512]{3,2,1,0:T(8,128)(2,1)}, u32[]{:S(2)}, u32[]{:S(2)}) %all-to-all-start.2) | async-done | bytes 4325408 | tf_op jit(solution)/shard_map/all_to_all | solution.py:132
  378.1 4.6 %copy.224 = bf16[1,3,8,176,512]{4,3,2,1,0:T(8,128)(2,1)} copy(bf16[1,3,8,176,512]{4,3,1,2,0:T(8,128)(2,1)} %bitcast.78) | data formatting | bytes 8650752 | tf_op jit(solution)/shard_map/all_to_all | solution.py:132
  384.0 2.6 all-to-all-start.3
  386.6 3.6 slice_dynamic-update-slice_fusion
  390.1 2.6 bitcast_dynamic-update-slice_fusion
  (181 shorter events, 46.1 us)
Async XLA Ops:
  7.2 375.6 %copy-start = (bf16[2816,512]{1,0:T(8,128)(2,1)S(1)}, bf16[2816,512]{1,0:T(8,128)(2,1)}, u32[]{:S(2)}) copy-start(bf16[2816,512]{1,0:T(8,128)(2,1)} %param.37) | copy-start | bytes 8650756
  8.2 2.3 copy-start.26
  8.9 0.6 copy-start.24
  10.4 0.6 copy-start.18
  10.4 0.6 copy-start.19
  11.3 1.9 copy-start.17
  13.8 0.5 copy-start.13
  59.9 5.8 %copy-start.21 = (s32[32,6]{0,1:T(8,128)S(1)}, s32[32,6]{0,1:T(8,128)}, u32[]{:S(2)}) copy-start(s32[32,6]{0,1:T(8,128)} %param.30) | copy-start | bytes 2308
  59.9 8.1 %copy-start.12 = (f32[2048]{0:T(1024)S(1)}, f32[2048]{0:T(1024)}, u32[]{:S(2)}) copy-start(f32[2048]{0:T(1024)} %param.21) | copy-start | bytes 24580
  59.9 194.6 %all-to-all-start.1 = ((bf16[8,2,3,176,512]{4,3,2,1,0:T(8,128)(2,1)}), bf16[8,2,3,176,512]{4,3,2,1,0:T(8,128)(2,1)}, u32[]{:S(2)}, u32[]{:S(2)}) async-start(bf16[8,2,3,176,512]{4,3,2,1,0:T(8,128)(2,1)} %copy.215), calls=%async_computation.1 | async-start | bytes 17301504 | tf_op jit(solution)/shard_map/all_to_all | solution.py:63
  67.8 55.9 %copy-start.1 = (bf16[512,512]{0,1:T(8,128)(2,1)}, bf16[512,512]{0,1:T(8,128)(2,1)S(1)}, u32[]{:S(2)}) copy-start(bf16[512,512]{0,1:T(8,128)(2,1)S(1)} %copy.204) | copy-start | bytes 1572868
  68.1 0.6 copy-start.3
  73.9 0.6 copy-start.4
  81.2 0.6 copy-start.11
  81.8 4.4 %copy-start.16 = (s32[1024]{0:T(1024)}, s32[1024]{0:T(1024)S(1)}, u32[]{:S(2)}) copy-start(s32[1024]{0:T(1024)S(1)} %pad_clamp_fusion.2) | copy-start | bytes 12292
  83.9 0.8 copy-start.23
  84.6 0.6 copy-start.28
  86.1 0.6 copy-start.6
  86.1 0.6 copy-start.8
  91.6 0.6 copy-start.5
  119.7 0.8 copy-start.2
  119.7 14.2 %copy-start.7 = (bf16[32,2,32]{2,1,0:T(2,128)(2,1)S(1)}, bf16[32,2,32]{2,1,0:T(2,128)(2,1)}, u32[]{:S(2)}) copy-start(bf16[32,2,32]{2,1,0:T(2,128)(2,1)} %copy-done.6) | copy-start | bytes 12292
  125.2 0.6 copy-start.10
  125.4 0.6 copy-start.9
  269.6 6.3 %copy-start.14 = (s32[4]{0:T(128)S(1)}, s32[4]{0:T(128)}, u32[]{:S(2)}) copy-start(s32[4]{0:T(128)} %copy-done.13) | copy-start | bytes 52
  275.9 0.7 copy-start.15
  276.7 4.6 %copy-start.27 = (s32[32]{0:T(128)S(1)}, s32[32]{0:T(128)}, u32[]{:S(2)}) copy-start(s32[32]{0:T(128)} %copy-done.26) | copy-start | bytes 388
  276.7 6.7 %copy-start.20 = (s32[192,1]{0,1:T(1,128)S(1)}, s32[192,1]{0,1:T(1,128)}, u32[]{:S(2)}) copy-start(s32[192,1]{0,1:T(1,128)} %reshape_reshape.3) | copy-start | bytes 2308
  276.7 23.8 %copy-start.22 = (f32[32,6]{0,1:T(8,128)S(1)}, f32[32,6]{0,1:T(8,128)}, u32[]{:S(2)}) copy-start(f32[32,6]{0,1:T(8,128)} %param.31) | copy-start | bytes 2308
  276.7 101.4 %all-to-all-start.2 = ((bf16[8,3,176,512]{3,2,1,0:T(8,128)(2,1)}), bf16[8,3,176,512]{3,2,1,0:T(8,128)(2,1)}, u32[]{:S(2)}, u32[]{:S(2)}) async-start(bf16[8,3,176,512]{3,2,1,0:T(8,128)(2,1)} %get-tuple-element.165), calls=%async_computation.2 | async-start | bytes 8650752 | tf_op jit(solution)/shard_map/all_to_all | solution.py:132
  281.3 79.7 %all-gather.7.cloned.1.call-start = ((), (), s32[]{:S(2)}) async-start(), calls=%async_computation.4 | async-start | bytes 3604480 | tf_op jit(solution)/shard_map/all_gather | solution.py:76
  309.4 6.9 %copy-start.25 = (s32[8]{0:T(128)S(1)}, s32[8]{0:T(128)}, u32[]{:S(2)}) copy-start(s32[8]{0:T(128)} %copy-done.24) | copy-start | bytes 100
  384.0 10.0 %all-to-all-start.3 = ((f32[32,1,512]{2,1,0:T(1,128)}), f32[32,1,512]{2,1,0:T(1,128)S(1)}, u32[]{:S(2)}, u32[]{:S(2)}) async-start(f32[32,1,512]{2,1,0:T(1,128)} %copy.226), calls=%async_computation.3 | async-start | bytes 131072 | tf_op jit(solution)/shard_map/all_to_all | solution.py:326
Sparse Core Ops, SparseCore 0:
  316.4 44.5 all-gather.6

commit v6 on v5

--- a/solution.py
+++ b/solution.py
@@ -41,11 +41,6 @@
         [first_half * cosine - second * sine_part, second * cosine + first_half * sine_part],
         axis=-1,
     )
-
-
-def gather_rows(rows):
-    by_expert = lax.all_gather(rows, "expert", axis=0, tiled=True)
-    return lax.all_gather(by_expert, "dp", axis=0, tiled=True)
 
 
 def pick_rows(table, rows):
@@ -163,9 +158,10 @@
     score_scale = (NOPE + ROPE) ** (-0.5)
     group_start = dp_index * group_rows
     chosen, plan = migrate_start(expert_gate_up, expert_down, old_place, new_place, ex_index)
-    everyone = gather_rows(hidden)
-    everyone, chosen = lax.optimization_barrier((everyone, chosen))
+    by_expert = lax.all_gather(hidden, "expert", axis=0, tiled=True)
+    by_expert, chosen = lax.optimization_barrier((by_expert, chosen))
     spread = spread_slots(chosen, ex_count)
+    everyone = lax.all_gather(by_expert, "dp", axis=0, tiled=True)
     normed = rms_norm(everyone.astype(jnp.float32), attn_gain).astype(jnp.bfloat16)
     queries = jnp.einsum(
         "td,qd->tq", normed, query_weight, preferred_element_type=jnp.float32

time: 404 us -> 397 us (0.983)
  waiting for transfers between devices: 133 us -> 124 us
    all_to_all x1, waiting for transfers between devices: 112 us -> 104 us  [spread_slots(): lax.all_to_all(pieces, 'expert', split_axis=0, concat_axis=0, tiled=True)]
  transfers between devices with their start and end apart: 4 -> 4, of which waited for: 4 -> 4; matrix products, arithmetic and copies ran while one was open for 30% -> 31% of each run, Pallas kernels for 0% -> 0%
where the time goes in v6:
time: 397 us; the launch traced here: 395 us
  waiting for transfers between devices  124 us (31%)
  local copies, waits for them, and re-layouts  71.3 us (18%)
  blocking collectives  70.9 us (18%)
  other arithmetic  61.3 us (15%)
  matrix products  30.9 us (8%)
  between operations  22.9 us (6%)
  starting transfers between devices  13.2 us (3%)
    all_to_all x1, waiting for transfers between devices, spread_slots(): lax.all_to_all(pieces, 'expert', split_axis=0, concat_axis=0, tiled=True)  104 us
    all_gather x1, blocking collectives, local(): by_expert = lax.all_gather(hidden, 'expert', axis=0, tiled=True)  15.9 us
    all_gather x1, blocking collectives, local(): lax.all_gather(partial_value, 'expert', axis=0, tiled=False)  14.9 us
    unnamed x67, local copies, waits for them, and re-layouts  14.2 us
    all_gather x1, blocking collectives, sum_over(): return jnp.sum(lax.all_gather(values, axis, axis=0, tiled=False), axis=0)  12.6 us
    sub x1, other arithmetic, local(): local_slot = slot_of - ex_index * slots_local  10.7 us
    all_gather x1, blocking collectives, local(): gathered = lax.all_gather(packed, 'dp', axis=0, tiled=False)  10.4 us
    mul x1, other arithmetic, local(): base_gate_up = expert_gate_up * unit  10.3 us
  transfers between devices with their start and end apart: 4, of which 4 were waited for; matrix products, arithmetic and copies ran while one was open for 31% of the time, Pallas kernels for 0%

profile of v6, /device:TPU:0, one launch (start us, length us, event | category | flops | bytes accessed | tf_op | source)
XLA Modules:
  0.0 394.5 jit_solution(12778731301016228053)
XLA Ops:
  17.4 15.9 %all-gather.4 = bf16[8,1,2048]{2,1,0:T(2,128)(2,1)S(1)} all-gather(bf16[1,1,2048]{2,1,0:T(2,128)(2,1)} %bitcast.248), channel_id=1, replica_groups=mesh['dp'=4,'expert'=8] {'expert'}, dimensions={0}, use_global_device_ids=true | all-gather | bytes 36864 | tf_op jit(solution)/shard_map/all_gather | solution.py:161
  35.2 2.0 constant_dynamic-slice_fusion.9
  37.2 3.1 constant_dynamic-slice_fusion.11
  40.6 3.9 pad_maximum_fusion.2
  44.5 7.6 %copy.215 = bf16[8,2,3,176,512]{4,3,2,1,0:T(8,128)(2,1)} copy(bf16[8,2,3,176,512]{4,3,0,2,1:T(8,128)(2,1)} %bitcast.228) | data formatting | bytes 17301504 | tf_op jit(solution)/shard_map/transpose | solution.py:57
  52.0 5.1 %all-to-all-start.1 = ((bf16[8,2,3,176,512]{4,3,2,1,0:T(8,128)(2,1)}), bf16[8,2,3,176,512]{4,3,2,1,0:T(8,128)(2,1)}, u32[]{:S(2)}, u32[]{:S(2)}) async-start(bf16[8,2,3,176,512]{4,3,2,1,0:T(8,128)(2,1)} %copy.215), calls=%async_computation.1 | async-start | bytes 17301504 | tf_op jit(solution)/shard_map/all_to_all | solution.py:58
  60.0 8.7 %all_gather.34 = bf16[32,2048]{1,0:T(8,128)(2,1)S(1)} all-gather(bf16[8,2048]{1,0:T(8,128)(2,1)} %bitcast.241), channel_id=1, replica_groups=mesh['dp'=4,'expert'=8] {'dp'}, dimensions={0}, use_global_device_ids=true | all-gather | bytes 163840 | tf_op jit(solution)/shard_map/all_gather | solution.py:164
  69.6 2.6 fusion.95
  72.2 1.5 reshape.443
  78.8 2.6 scatter_custom_fusion
  82.6 2.1 gather_fusion.1
  87.7 1.3 gather_fusion.2
  89.0 1.6 fusion.5
  90.6 1.9 fusion.94
  95.1 1.3 select_reduce_fusion.1
  97.1 1.3 gather_fusion.3
  100.2 1.4 convolution_bitcast_fusion.3
  101.6 1.4 copy.211
  103.0 1.3 copy.210
  104.3 1.3 dynamic_slice.81
  105.6 1.6 convolution_multiply_fusion
  109.0 10.4 %all-gather = f32[128,2,514]{2,0,1:T(8,128)S(1)} all-gather(f32[32,2,514]{2,0,1:T(8,128)S(1)} %pad_maximum_fusion.3), channel_id=2, replica_groups=mesh['dp'=4,'expert'=8] {'dp'}, dimensions={0}, use_global_device_ids=true | all-gather | bytes 657920 | tf_op jit(solution)/shard_map/all_gather | solution.py:217
  120.8 2.5 copy.239
  123.3 1.5 fusion.88
  125.6 3.0 multiply_reduce_fusion
  130.3 2.4 fusion.25
  135.6 1.3 reduce_min.29
  140.6 1.8 fusion.7
  142.3 104.3 %all-to-all-done.1 = bf16[8,2,3,176,512]{4,3,2,1,0:T(8,128)(2,1)} async-done(((bf16[8,2,3,176,512]{4,3,2,1,0:T(8,128)(2,1)}), bf16[8,2,3,176,512]{4,3,2,1,0:T(8,128)(2,1)}, u32[]{:S(2)}, u32[]{:S(2)}) %all-to-all-start.1) | async-done | bytes 8650784 | tf_op jit(solution)/shard_map/all_to_all | solution.py:58
  246.6 14.9 %all-gather.1 = f32[64,2048]{1,0:T(8,128)S(1)} all-gather(f32[8,2048]{1,0:T(8,128)S(1)} %fusion.7), channel_id=3, replica_groups=mesh['dp'=4,'expert'=8] {'expert'}, dimensions={0}, use_global_device_ids=true | all-gather | bytes 589824 | tf_op jit(solution)/shard_map/all_gather | solution.py:251
  261.8 6.3 %gather_fusion.4 = bf16[8,3,176,512]{3,2,1,0:T(8,128)(2,1)} fusion(bf16[16,3,176,512]{3,2,1,0:T(8,128)(2,1)} %bitcast.34, s32[1024]{0:T(1024)S(1)} %pad_clamp_fusion.1), kind=kCustom, calls=%fused_computation.4 | custom fusion | bytes 8650784 | tf_op jit(solution)/shard_map/jit(_take)/gather | solution.py:113
  268.9 4.6 %all-to-all-start.2 = ((bf16[8,3,176,512]{3,2,1,0:T(8,128)(2,1)}), bf16[8,3,176,512]{3,2,1,0:T(8,128)(2,1)}, u32[]{:S(2)}, u32[]{:S(2)}) async-start(bf16[8,3,176,512]{3,2,1,0:T(8,128)(2,1)} %get-tuple-element.165), calls=%async_computation.2 | async-start | bytes 8650752 | tf_op jit(solution)/shard_map/all_to_all | solution.py:127
  275.6 4.5 %compare_select_fusion.5 = (s32[192,1]{0,1:T(1,128)S(1)}, s32[192,1]{0,1:T(1,128)S(1)}) fusion(s32[]{:T(128)} %bitcast.54, s32[]{:T(128)} %bitcast.55, s32[]{:T(128)} %bitcast.56, s32[]{:T(128)} %bitcast.57, s32[]{:T(128)} %bitcast.58, s32[]{:T(128)} %bitcast.60, s32[]{:T(128)} %bitcast.59, s32[192,1]{0,1:T(1,128)S(1)} %copy-done.20), kind=kLoop, calls=%fused_computation.184 | loop fusion | flops 2880 | bytes 2332 | tf_op jit(solution)/shard_map/gather | solution.py:287
  280.1 10.7 %select_subtract_fusion = s32[192]{0:T(256)S(1)} fusion(pred[192]{0:T(512)(128)(4,1)S(1)} %get-tuple-element.102, pred[192]{0:T(512)(128)(4,1)S(1)} %get-tuple-element.101, pred[192]{0:T(512)(128)(4,1)S(1)} %get-tuple-element.100, pred[192]{0:T(512)(128)(4,1)S(1)} %get-tuple-element.99, pred[192]{0:T(512)(128)(4,1)S(1)} %get-tuple-element.98, ...), kind=kLoop, calls=%fused_computation.215 | loop fusion | flops 3456 | bytes 4872 | tf_op jit(solution)/shard_map/sub | solution.py:289
  293.0 8.5 %all_gather.39 = bf16[32,2048]{1,0:T(8,128)(2,1)S(1)} all-gather(bf16[8,2048]{1,0:T(8,128)(2,1)S(1)} %multiply_convert_fusion), channel_id=1, replica_groups=mesh['dp'=4,'expert'=8] {'dp'}, dimensions={0}, use_global_device_ids=true | all-gather | bytes 163840 | tf_op jit(solution)/shard_map/all_gather | solution.py:261
  301.6 6.9 %convolution_bitcast_fusion.1 = f32[4,2,16,1408]{3,2,1,0:T(8,128)} fusion(bf16[4,2,1408,512]{3,2,1,0:T(8,128)(2,1)} %param.34, bf16[32,512,1]{1,0,2:T(8,128)(2,1)S(1)} %reshape.615, bf16[32,4,16]{0,2,1:T(8,128)(2,1)S(1)} %get-tuple-element.82), kind=kOutput, calls=%fused_computation.27 | convolution fusion | flops 186679296 | bytes 12292096 | tf_op jit(solution)/shard_map/scd,sgfd->sgcf/dot_general | solution.py:302
  311.5 4.2 %convolution_bitcast_fusion = f32[2,4,2816]{2,1,0:T(4,128)S(1)} fusion(bf16[2,2816,512]{2,1,0:T(8,128)(2,1)} %param.36, bf16[4,1,1,512]{3,1,0,2:T(2,128)(2,1)S(1)} %constant_dynamic-slice_fusion.6), kind=kOutput, calls=%fused_computation.23 | convolution fusion | flops 23068672 | bytes 5861376 | tf_op jit(solution)/shard_map/td,gfd->gtf/dot_general | solution.py:305
  315.8 12.6 %all-gather.3 = f32[8,4,2816]{2,1,0:T(4,128)S(1)} all-gather(f32[2,4,2816]{2,1,0:T(4,128)S(1)} %convolution_bitcast_fusion), channel_id=5, replica_groups=mesh['dp'=4,'expert'=8] {'dp'}, dimensions={0}, use_global_device_ids=true | all-gather | bytes 450560 | tf_op jit(solution)/shard_map/all_gather | solution.py:71
  329.1 5.5 %broadcast_multiply_fusion.1 = bf16[4,1408,512]{2,1,0:T(8,128)(2,1)} fusion(bf16[4,1408,512]{2,1,0:T(8,128)(2,1)} %param.35, bf16[]{:T(256)} %bitcast.86), kind=kLoop, calls=%fused_computation.25 | loop fusion | flops 2883584 | bytes 11534338 | tf_op jit(solution)/shard_map/mul | solution.py:264
  334.6 10.3 %broadcast_multiply_fusion = bf16[4,2,1408,512]{3,2,1,0:T(8,128)(2,1)} fusion(bf16[4,2,1408,512]{3,2,1,0:T(8,128)(2,1)} %param.34, bf16[]{:T(256)} %bitcast.86), kind=kLoop, calls=%fused_computation.22 | loop fusion | flops 5767168 | bytes 23068674 | tf_op jit(solution)/shard_map/mul | solution.py:263
  345.0 8.2 %all-gather.7.cloned.1.call-done = f32[16,2,16,1408]{3,2,1,0:T(8,128)} async-done(((f32[4,2,16,1408]{3,2,1,0:T(8,128)}), f32[16,2,16,1408]{3,2,1,0:T(8,128)}) %all-gather.7.cloned.1.call-update) | async-done | bytes 2883600 | tf_op jit(solution)/shard_map/all_gather | solution.py:71
  353.2 2.9 reduce_sum.167
  356.1 3.7 fusion.17
  360.1 10.1 %all-to-all-done.2 = bf16[8,3,176,512]{3,2,1,0:T(8,128)(2,1)} async-done(((bf16[8,3,176,512]{3,2,1,0:T(8,128)(2,1)}), bf16[8,3,176,512]{3,2,1,0:T(8,128)(2,1)}, u32[]{:S(2)}, u32[]{:S(2)}) %all-to-all-start.2) | async-done | bytes 4325408 | tf_op jit(solution)/shard_map/all_to_all | solution.py:127
  370.3 4.6 %copy.224 = bf16[1,3,8,176,512]{4,3,2,1,0:T(8,128)(2,1)} copy(bf16[1,3,8,176,512]{4,3,1,2,0:T(8,128)(2,1)} %bitcast.78) | data formatting | bytes 8650752 | tf_op jit(solution)/shard_map/all_to_all | solution.py:127
  376.1 3.5 all-to-all-start.3
  379.6 3.6 slice_dynamic-update-slice_fusion
  383.2 2.6 bitcast_dynamic-update-slice_fusion
  (181 shorter events, 46.7 us)
Async XLA Ops:
  7.2 367.7 %copy-start = (bf16[2816,512]{1,0:T(8,128)(2,1)S(1)}, bf16[2816,512]{1,0:T(8,128)(2,1)}, u32[]{:S(2)}) copy-start(bf16[2816,512]{1,0:T(8,128)(2,1)} %param.37) | copy-start | bytes 8650756
  8.2 2.3 copy-start.26
  8.9 0.6 copy-start.24
  10.4 0.6 copy-start.18
  10.4 0.6 copy-start.19
  11.3 1.9 copy-start.17
  13.8 0.5 copy-start.13
  52.0 5.8 %copy-start.21 = (s32[32,6]{0,1:T(8,128)S(1)}, s32[32,6]{0,1:T(8,128)}, u32[]{:S(2)}) copy-start(s32[32,6]{0,1:T(8,128)} %param.30) | copy-start | bytes 2308
  52.0 16.8 %copy-start.12 = (f32[2048]{0:T(1024)S(1)}, f32[2048]{0:T(1024)}, u32[]{:S(2)}) copy-start(f32[2048]{0:T(1024)} %param.21) | copy-start | bytes 24580
  52.0 194.6 %all-to-all-start.1 = ((bf16[8,2,3,176,512]{4,3,2,1,0:T(8,128)(2,1)}), bf16[8,2,3,176,512]{4,3,2,1,0:T(8,128)(2,1)}, u32[]{:S(2)}, u32[]{:S(2)}) async-start(bf16[8,2,3,176,512]{4,3,2,1,0:T(8,128)(2,1)} %copy.215), calls=%async_computation.1 | async-start | bytes 17301504 | tf_op jit(solution)/shard_map/all_to_all | solution.py:58
  60.0 60.9 %copy-start.1 = (bf16[512,512]{0,1:T(8,128)(2,1)}, bf16[512,512]{0,1:T(8,128)(2,1)S(1)}, u32[]{:S(2)}) copy-start(bf16[512,512]{0,1:T(8,128)(2,1)S(1)} %copy.204) | copy-start | bytes 1572868
  68.9 0.6 copy-start.3
  74.7 0.6 copy-start.4
  82.0 0.6 copy-start.11
  82.6 4.4 %copy-start.16 = (s32[1024]{0:T(1024)}, s32[1024]{0:T(1024)S(1)}, u32[]{:S(2)}) copy-start(s32[1024]{0:T(1024)S(1)} %pad_clamp_fusion.2) | copy-start | bytes 12292
  84.7 0.8 copy-start.23
  85.4 0.6 copy-start.28
  86.9 0.6 copy-start.6
  87.0 0.6 copy-start.8
  92.5 0.6 copy-start.5
  119.3 0.8 copy-start.2
  119.3 14.2 %copy-start.7 = (bf16[32,2,32]{2,1,0:T(2,128)(2,1)S(1)}, bf16[32,2,32]{2,1,0:T(2,128)(2,1)}, u32[]{:S(2)}) copy-start(bf16[32,2,32]{2,1,0:T(2,128)(2,1)} %copy-done.6) | copy-start | bytes 12292
  124.9 0.6 copy-start.10
  125.0 0.6 copy-start.9
  261.8 6.3 %copy-start.14 = (s32[4]{0:T(128)S(1)}, s32[4]{0:T(128)}, u32[]{:S(2)}) copy-start(s32[4]{0:T(128)} %copy-done.13) | copy-start | bytes 52
  268.1 0.7 copy-start.15
  268.9 4.6 %copy-start.27 = (s32[32]{0:T(128)S(1)}, s32[32]{0:T(128)}, u32[]{:S(2)}) copy-start(s32[32]{0:T(128)} %copy-done.26) | copy-start | bytes 388
  268.9 6.7 %copy-start.20 = (s32[192,1]{0,1:T(1,128)S(1)}, s32[192,1]{0,1:T(1,128)}, u32[]{:S(2)}) copy-start(s32[192,1]{0,1:T(1,128)} %reshape_reshape.3) | copy-start | bytes 2308
  268.9 23.8 %copy-start.22 = (f32[32,6]{0,1:T(8,128)S(1)}, f32[32,6]{0,1:T(8,128)}, u32[]{:S(2)}) copy-start(f32[32,6]{0,1:T(8,128)} %param.31) | copy-start | bytes 2308
  268.9 101.4 %all-to-all-start.2 = ((bf16[8,3,176,512]{3,2,1,0:T(8,128)(2,1)}), bf16[8,3,176,512]{3,2,1,0:T(8,128)(2,1)}, u32[]{:S(2)}, u32[]{:S(2)}) async-start(bf16[8,3,176,512]{3,2,1,0:T(8,128)(2,1)} %get-tuple-element.165), calls=%async_computation.2 | async-start | bytes 8650752 | tf_op jit(solution)/shard_map/all_to_all | solution.py:127
  273.4 79.8 %all-gather.7.cloned.1.call-start = ((), (), s32[]{:S(2)}) async-start(), calls=%async_computation.4 | async-start | bytes 3604480 | tf_op jit(solution)/shard_map/all_gather | solution.py:71
  301.6 6.9 %copy-start.25 = (s32[8]{0:T(128)S(1)}, s32[8]{0:T(128)}, u32[]{:S(2)}) copy-start(s32[8]{0:T(128)} %copy-done.24) | copy-start | bytes 100
  376.1 10.9 %all-to-all-start.3 = ((f32[32,1,512]{2,1,0:T(1,128)}), f32[32,1,512]{2,1,0:T(1,128)S(1)}, u32[]{:S(2)}, u32[]{:S(2)}) async-start(f32[32,1,512]{2,1,0:T(1,128)} %copy.226), calls=%async_computation.3 | async-start | bytes 131072 | tf_op jit(solution)/shard_map/all_to_all | solution.py:322
Sparse Core Ops, SparseCore 0:
  308.6 44.5 all-gather.6

commit v7 on v6

--- a/solution.py
+++ b/solution.py
@@ -124,7 +124,7 @@
 
 
 def deliver(outgoing):
-    return lax.all_to_all(outgoing, "expert", split_axis=0, concat_axis=2, tiled=True)
+    return lax.all_to_all(outgoing, "expert", split_axis=0, concat_axis=0, tiled=True)
 
 
 def local(
@@ -324,8 +324,16 @@
     moe_part = moe_cols.transpose(1, 0, 2).reshape(req_local, dp_count * col_width)
     layer_out = (residual + moe_part).astype(jnp.bfloat16)
     my_moved = plan[-1]
-    moved_gate_up = lax.dynamic_update_index_in_dim(base_gate_up, arrived[0, :2], my_moved, 0)
-    moved_down = lax.dynamic_update_index_in_dim(base_down, arrived[0, 2], my_moved, 0)
+    chunk_rows = arrived.shape[2]
+    slot_shape = (slots_local, 2, ex_count, chunk_rows, col_width)
+    new_pair = arrived[:, :2].transpose(1, 0, 2, 3)[None]
+    moved_gate_up = lax.dynamic_update_slice(
+        base_gate_up.reshape(slot_shape), new_pair, (my_moved, 0, 0, 0, 0)
+    ).reshape(base_gate_up.shape)
+    new_single = arrived[:, 2][None]
+    moved_down = lax.dynamic_update_slice(
+        base_down.reshape(slots_local, ex_count, chunk_rows, col_width), new_single, (my_moved, 0, 0, 0)
+    ).reshape(base_down.shape)
     return (layer_out, moved_gate_up, moved_down)
 
 

time: 397 us -> 393 us (0.990)
  local copies, waits for them, and re-layouts: 71.3 us -> 66.9 us
    all_to_all x1 -> x0, local copies, waits for them, and re-layouts: 4.6 us -> none  [deliver(): lax.all_to_all(outgoing, 'expert', split_axis=0, concat_axis=2, tiled=True)]
where the time goes in v7:
time: 393 us; the launch traced here: 390 us
  waiting for transfers between devices  124 us (32%)
  blocking collectives  70.9 us (18%)
  local copies, waits for them, and re-layouts  66.9 us (17%)
  other arithmetic  61.3 us (16%)
  matrix products  30.9 us (8%)
  between operations  22.9 us (6%)
  starting transfers between devices  13.2 us (3%)
    all_to_all x1, waiting for transfers between devices, spread_slots(): lax.all_to_all(pieces, 'expert', split_axis=0, concat_axis=0, tiled=True)  104 us
    all_gather x1, blocking collectives, local(): by_expert = lax.all_gather(hidden, 'expert', axis=0, tiled=True)  15.9 us
    all_gather x1, blocking collectives, local(): lax.all_gather(partial_value, 'expert', axis=0, tiled=False)  14.9 us
    unnamed x67, local copies, waits for them, and re-layouts  14.2 us
    all_gather x1, blocking collectives, sum_over(): return jnp.sum(lax.all_gather(values, axis, axis=0, tiled=False), axis=0)  12.6 us
    sub x1, other arithmetic, local(): local_slot = slot_of - ex_index * slots_local  10.7 us
    all_gather x1, blocking collectives, local(): gathered = lax.all_gather(packed, 'dp', axis=0, tiled=False)  10.4 us
    mul x1, other arithmetic, local(): base_gate_up = expert_gate_up * unit  10.3 us
  transfers between devices with their start and end apart: 4, of which 4 were waited for; matrix products, arithmetic and copies ran while one was open for 31% of the time, Pallas kernels for 0%

profile of v7, /device:TPU:0, one launch (start us, length us, event | category | flops | bytes accessed | tf_op | source)
XLA Modules:
  0.0 390.0 jit_solution(13043371215482769581)
XLA Ops:
  17.4 15.9 %all-gather.4 = bf16[8,1,2048]{2,1,0:T(2,128)(2,1)S(1)} all-gather(bf16[1,1,2048]{2,1,0:T(2,128)(2,1)} %bitcast.255), channel_id=1, replica_groups=mesh['dp'=4,'expert'=8] {'expert'}, dimensions={0}, use_global_device_ids=true | all-gather | bytes 36864 | tf_op jit(solution)/shard_map/all_gather | solution.py:161
  35.2 2.1 constant_dynamic-slice_fusion.9
  37.4 3.1 constant_dynamic-slice_fusion.11
  40.7 3.9 pad_maximum_fusion.2
  44.6 7.6 %copy.215 = bf16[8,2,3,176,512]{4,3,2,1,0:T(8,128)(2,1)} copy(bf16[8,2,3,176,512]{4,3,0,2,1:T(8,128)(2,1)} %bitcast.233) | data formatting | bytes 17301504 | tf_op jit(solution)/shard_map/transpose | solution.py:57
  52.2 5.1 %all-to-all-start.1 = ((bf16[8,2,3,176,512]{4,3,2,1,0:T(8,128)(2,1)}), bf16[8,2,3,176,512]{4,3,2,1,0:T(8,128)(2,1)}, u32[]{:S(2)}, u32[]{:S(2)}) async-start(bf16[8,2,3,176,512]{4,3,2,1,0:T(8,128)(2,1)} %copy.215), calls=%async_computation.1 | async-start | bytes 17301504 | tf_op jit(solution)/shard_map/all_to_all | solution.py:58
  58.8 1.3 copy.204
  60.1 8.7 %all_gather.34 = bf16[32,2048]{1,0:T(8,128)(2,1)S(1)} all-gather(bf16[8,2048]{1,0:T(8,128)(2,1)} %bitcast.248), channel_id=1, replica_groups=mesh['dp'=4,'expert'=8] {'dp'}, dimensions={0}, use_global_device_ids=true | all-gather | bytes 163840 | tf_op jit(solution)/shard_map/all_gather | solution.py:164
  69.7 2.6 fusion.95
  72.3 1.5 reshape.454
  78.9 2.6 scatter_custom_fusion
  82.7 2.1 gather_fusion.1
  87.8 1.3 gather_fusion.2
  89.1 1.6 fusion.5
  90.7 1.9 fusion.94
  95.2 1.3 select_reduce_fusion.1
  97.3 1.3 gather_fusion.3
  100.3 1.4 convolution_bitcast_fusion.3
  101.8 1.4 copy.211
  103.1 1.3 copy.210
  104.5 1.3 dynamic_slice.81
  105.8 1.6 convolution_multiply_fusion
  109.1 10.4 %all-gather = f32[128,2,514]{2,0,1:T(8,128)S(1)} all-gather(f32[32,2,514]{2,0,1:T(8,128)S(1)} %pad_maximum_fusion.3), channel_id=2, replica_groups=mesh['dp'=4,'expert'=8] {'dp'}, dimensions={0}, use_global_device_ids=true | all-gather | bytes 657920 | tf_op jit(solution)/shard_map/all_gather | solution.py:217
  121.0 2.5 copy.239
  123.5 1.5 fusion.88
  125.7 3.0 multiply_reduce_fusion
  130.4 2.4 fusion.25
  135.8 1.3 reduce_min.29
  140.7 1.8 fusion.7
  142.5 104.3 %all-to-all-done.1 = bf16[8,2,3,176,512]{4,3,2,1,0:T(8,128)(2,1)} async-done(((bf16[8,2,3,176,512]{4,3,2,1,0:T(8,128)(2,1)}), bf16[8,2,3,176,512]{4,3,2,1,0:T(8,128)(2,1)}, u32[]{:S(2)}, u32[]{:S(2)}) %all-to-all-start.1) | async-done | bytes 8650784 | tf_op jit(solution)/shard_map/all_to_all | solution.py:58
  246.8 14.9 %all-gather.1 = f32[64,2048]{1,0:T(8,128)S(1)} all-gather(f32[8,2048]{1,0:T(8,128)S(1)} %fusion.7), channel_id=3, replica_groups=mesh['dp'=4,'expert'=8] {'expert'}, dimensions={0}, use_global_device_ids=true | all-gather | bytes 589824 | tf_op jit(solution)/shard_map/all_gather | solution.py:251
  261.9 6.3 %gather_fusion.4 = bf16[8,3,176,512]{3,2,1,0:T(8,128)(2,1)} fusion(bf16[16,3,176,512]{3,2,1,0:T(8,128)(2,1)} %bitcast.34, s32[1024]{0:T(1024)S(1)} %pad_clamp_fusion.1), kind=kCustom, calls=%fused_computation.4 | custom fusion | bytes 8650784 | tf_op jit(solution)/shard_map/jit(_take)/gather | solution.py:113
  269.0 4.6 %all-to-all-start.2 = ((bf16[8,3,176,512]{3,2,1,0:T(8,128)(2,1)}), bf16[8,3,176,512]{3,2,1,0:T(8,128)(2,1)}, u32[]{:S(2)}, u32[]{:S(2)}) async-start(bf16[8,3,176,512]{3,2,1,0:T(8,128)(2,1)} %get-tuple-element.165), calls=%async_computation.2 | async-start | bytes 8650752 | tf_op jit(solution)/shard_map/all_to_all | solution.py:127
  275.7 4.5 %compare_select_fusion.5 = (s32[192,1]{0,1:T(1,128)S(1)}, s32[192,1]{0,1:T(1,128)S(1)}) fusion(s32[]{:T(128)} %bitcast.54, s32[]{:T(128)} %bitcast.55, s32[]{:T(128)} %bitcast.56, s32[]{:T(128)} %bitcast.57, s32[]{:T(128)} %bitcast.58, s32[]{:T(128)} %bitcast.60, s32[]{:T(128)} %bitcast.59, s32[192,1]{0,1:T(1,128)S(1)} %copy-done.20), kind=kLoop, calls=%fused_computation.185 | loop fusion | flops 2880 | bytes 2332 | tf_op jit(solution)/shard_map/gather | solution.py:287
  280.2 10.7 %select_subtract_fusion = s32[192]{0:T(256)S(1)} fusion(pred[192]{0:T(512)(128)(4,1)S(1)} %get-tuple-element.102, pred[192]{0:T(512)(128)(4,1)S(1)} %get-tuple-element.101, pred[192]{0:T(512)(128)(4,1)S(1)} %get-tuple-element.100, pred[192]{0:T(512)(128)(4,1)S(1)} %get-tuple-element.99, pred[192]{0:T(512)(128)(4,1)S(1)} %get-tuple-element.98, ...), kind=kLoop, calls=%fused_computation.216 | loop fusion | flops 3456 | bytes 4872 | tf_op jit(solution)/shard_map/sub | solution.py:289
  293.2 8.5 %all_gather.39 = bf16[32,2048]{1,0:T(8,128)(2,1)S(1)} all-gather(bf16[8,2048]{1,0:T(8,128)(2,1)S(1)} %multiply_convert_fusion), channel_id=1, replica_groups=mesh['dp'=4,'expert'=8] {'dp'}, dimensions={0}, use_global_device_ids=true | all-gather | bytes 163840 | tf_op jit(solution)/shard_map/all_gather | solution.py:261
  301.7 6.9 %convolution_bitcast_fusion.1 = f32[4,2,16,1408]{3,2,1,0:T(8,128)} fusion(bf16[4,2,1408,512]{3,2,1,0:T(8,128)(2,1)} %param.34, bf16[32,512,1]{1,0,2:T(8,128)(2,1)S(1)} %reshape.630, bf16[32,4,16]{0,2,1:T(8,128)(2,1)S(1)} %get-tuple-element.82), kind=kOutput, calls=%fused_computation.28 | convolution fusion | flops 186679296 | bytes 12292096 | tf_op jit(solution)/shard_map/scd,sgfd->sgcf/dot_general | solution.py:302
  311.7 4.2 %convolution_bitcast_fusion = f32[2,4,2816]{2,1,0:T(4,128)S(1)} fusion(bf16[2,2816,512]{2,1,0:T(8,128)(2,1)} %param.36, bf16[4,1,1,512]{3,1,0,2:T(2,128)(2,1)S(1)} %constant_dynamic-slice_fusion.6), kind=kOutput, calls=%fused_computation.23 | convolution fusion | flops 23068672 | bytes 5861376 | tf_op jit(solution)/shard_map/td,gfd->gtf/dot_general | solution.py:305
  315.9 12.6 %all-gather.3 = f32[8,4,2816]{2,1,0:T(4,128)S(1)} all-gather(f32[2,4,2816]{2,1,0:T(4,128)S(1)} %convolution_bitcast_fusion), channel_id=5, replica_groups=mesh['dp'=4,'expert'=8] {'dp'}, dimensions={0}, use_global_device_ids=true | all-gather | bytes 450560 | tf_op jit(solution)/shard_map/all_gather | solution.py:71
  329.2 5.5 %broadcast_multiply_fusion.1 = bf16[4,1408,512]{2,1,0:T(8,128)(2,1)} fusion(bf16[4,1408,512]{2,1,0:T(8,128)(2,1)} %param.35, bf16[]{:T(256)} %bitcast.83), kind=kLoop, calls=%fused_computation.26 | loop fusion | flops 2883584 | bytes 11534338 | tf_op jit(solution)/shard_map/mul | solution.py:264
  334.8 10.3 %broadcast_multiply_fusion = bf16[4,2,1408,512]{3,2,1,0:T(8,128)(2,1)} fusion(bf16[4,2,1408,512]{3,2,1,0:T(8,128)(2,1)} %param.34, bf16[]{:T(256)} %bitcast.83), kind=kLoop, calls=%fused_computation.22 | loop fusion | flops 5767168 | bytes 23068674 | tf_op jit(solution)/shard_map/mul | solution.py:263
  345.1 8.2 %all-gather.7.cloned.1.call-done = f32[16,2,16,1408]{3,2,1,0:T(8,128)} async-done(((f32[4,2,16,1408]{3,2,1,0:T(8,128)}), f32[16,2,16,1408]{3,2,1,0:T(8,128)}) %all-gather.7.cloned.1.call-update) | async-done | bytes 2883600 | tf_op jit(solution)/shard_map/all_gather | solution.py:71
  353.3 2.9 reduce_sum.167
  356.3 3.7 fusion.17
  360.3 10.1 %all-to-all-done.2 = bf16[8,3,176,512]{3,2,1,0:T(8,128)(2,1)} async-done(((bf16[8,3,176,512]{3,2,1,0:T(8,128)(2,1)}), bf16[8,3,176,512]{3,2,1,0:T(8,128)(2,1)}, u32[]{:S(2)}, u32[]{:S(2)}) %all-to-all-start.2) | async-done | bytes 4325408 | tf_op jit(solution)/shard_map/all_to_all | solution.py:127
  371.6 3.5 all-to-all-start.3
  375.1 3.6 copy_dynamic-update-slice_fusion
  378.8 2.6 bitcast_dynamic-update-slice_fusion
  (180 shorter events, 45.4 us)
Async XLA Ops:
  7.2 363.2 %copy-start = (bf16[2816,512]{1,0:T(8,128)(2,1)S(1)}, bf16[2816,512]{1,0:T(8,128)(2,1)}, u32[]{:S(2)}) copy-start(bf16[2816,512]{1,0:T(8,128)(2,1)} %param.37) | copy-start | bytes 8650756
  8.2 2.3 copy-start.26
  8.9 0.6 copy-start.24
  10.4 0.6 copy-start.18
  10.4 0.6 copy-start.19
  11.3 1.9 copy-start.17
  13.8 0.5 copy-start.13
  52.2 5.8 %copy-start.21 = (s32[32,6]{0,1:T(8,128)S(1)}, s32[32,6]{0,1:T(8,128)}, u32[]{:S(2)}) copy-start(s32[32,6]{0,1:T(8,128)} %param.30) | copy-start | bytes 2308
  52.2 16.8 %copy-start.12 = (f32[2048]{0:T(1024)S(1)}, f32[2048]{0:T(1024)}, u32[]{:S(2)}) copy-start(f32[2048]{0:T(1024)} %param.21) | copy-start | bytes 24580
  52.2 194.6 %all-to-all-start.1 = ((bf16[8,2,3,176,512]{4,3,2,1,0:T(8,128)(2,1)}), bf16[8,2,3,176,512]{4,3,2,1,0:T(8,128)(2,1)}, u32[]{:S(2)}, u32[]{:S(2)}) async-start(bf16[8,2,3,176,512]{4,3,2,1,0:T(8,128)(2,1)} %copy.215), calls=%async_computation.1 | async-start | bytes 17301504 | tf_op jit(solution)/shard_map/all_to_all | solution.py:58
  60.1 60.9 %copy-start.1 = (bf16[512,512]{0,1:T(8,128)(2,1)}, bf16[512,512]{0,1:T(8,128)(2,1)S(1)}, u32[]{:S(2)}) copy-start(bf16[512,512]{0,1:T(8,128)(2,1)S(1)} %copy.204) | copy-start | bytes 1572868
  69.0 0.6 copy-start.3
  74.8 0.6 copy-start.4
  82.1 0.6 copy-start.11
  82.7 4.4 %copy-start.16 = (s32[1024]{0:T(1024)}, s32[1024]{0:T(1024)S(1)}, u32[]{:S(2)}) copy-start(s32[1024]{0:T(1024)S(1)} %pad_clamp_fusion.2) | copy-start | bytes 12292
  84.9 0.8 copy-start.23
  85.5 0.6 copy-start.28
  87.1 0.6 copy-start.6
  87.1 0.6 copy-start.8
  92.6 0.6 copy-start.5
  119.5 0.8 copy-start.2
  119.5 14.2 %copy-start.7 = (bf16[32,2,32]{2,1,0:T(2,128)(2,1)S(1)}, bf16[32,2,32]{2,1,0:T(2,128)(2,1)}, u32[]{:S(2)}) copy-start(bf16[32,2,32]{2,1,0:T(2,128)(2,1)} %copy-done.6) | copy-start | bytes 12292
  125.0 0.6 copy-start.10
  125.1 0.6 copy-start.9
  261.9 6.3 %copy-start.14 = (s32[4]{0:T(128)S(1)}, s32[4]{0:T(128)}, u32[]{:S(2)}) copy-start(s32[4]{0:T(128)} %copy-done.13) | copy-start | bytes 52
  268.2 0.7 copy-start.15
  269.0 4.6 %copy-start.27 = (s32[32]{0:T(128)S(1)}, s32[32]{0:T(128)}, u32[]{:S(2)}) copy-start(s32[32]{0:T(128)} %copy-done.26) | copy-start | bytes 388
  269.0 6.7 %copy-start.20 = (s32[192,1]{0,1:T(1,128)S(1)}, s32[192,1]{0,1:T(1,128)}, u32[]{:S(2)}) copy-start(s32[192,1]{0,1:T(1,128)} %reshape_reshape.3) | copy-start | bytes 2308
  269.0 23.8 %copy-start.22 = (f32[32,6]{0,1:T(8,128)S(1)}, f32[32,6]{0,1:T(8,128)}, u32[]{:S(2)}) copy-start(f32[32,6]{0,1:T(8,128)} %param.31) | copy-start | bytes 2308
  269.0 101.4 %all-to-all-start.2 = ((bf16[8,3,176,512]{3,2,1,0:T(8,128)(2,1)}), bf16[8,3,176,512]{3,2,1,0:T(8,128)(2,1)}, u32[]{:S(2)}, u32[]{:S(2)}) async-start(bf16[8,3,176,512]{3,2,1,0:T(8,128)(2,1)} %get-tuple-element.165), calls=%async_computation.2 | async-start | bytes 8650752 | tf_op jit(solution)/shard_map/all_to_all | solution.py:127
  273.6 79.8 %all-gather.7.cloned.1.call-start = ((), (), s32[]{:S(2)}) async-start(), calls=%async_computation.4 | async-start | bytes 3604480 | tf_op jit(solution)/shard_map/all_gather | solution.py:71
  301.7 6.9 %copy-start.25 = (s32[8]{0:T(128)S(1)}, s32[8]{0:T(128)}, u32[]{:S(2)}) copy-start(s32[8]{0:T(128)} %copy-done.24) | copy-start | bytes 100
  371.6 10.9 %all-to-all-start.3 = ((f32[32,1,512]{2,1,0:T(1,128)}), f32[32,1,512]{2,1,0:T(1,128)S(1)}, u32[]{:S(2)}, u32[]{:S(2)}) async-start(f32[32,1,512]{2,1,0:T(1,128)} %copy.225), calls=%async_computation.3 | async-start | bytes 131072 | tf_op jit(solution)/shard_map/all_to_all | solution.py:322
Sparse Core Ops, SparseCore 0:
  308.7 44.5 all-gather.6

commit v8 on v7

--- a/solution.py
+++ b/solution.py
@@ -158,7 +158,9 @@
     score_scale = (NOPE + ROPE) ** (-0.5)
     group_start = dp_index * group_rows
     chosen, plan = migrate_start(expert_gate_up, expert_down, old_place, new_place, ex_index)
-    by_expert = lax.all_gather(hidden, "expert", axis=0, tiled=True)
+    copies = jnp.broadcast_to(hidden[None], (ex_count,) + hidden.shape)
+    by_expert = lax.all_to_all(copies, "expert", split_axis=0, concat_axis=0, tiled=True)
+    by_expert = by_expert.reshape(ex_count * req_local, hidden.shape[1])
     by_expert, chosen = lax.optimization_barrier((by_expert, chosen))
     spread = spread_slots(chosen, ex_count)
     everyone = lax.all_gather(by_expert, "dp", axis=0, tiled=True)

time: 393 us -> 385 us (0.980)
  blocking collectives: 70.9 us -> 55 us
  starting transfers between devices: 13.2 us -> 19.6 us
  local copies, waits for them, and re-layouts: 66.9 us -> 61.9 us
  waiting for transfers between devices: 124 us -> 129 us
    all_gather x1 -> x0, blocking collectives: 15.9 us -> none  [local(): by_expert = lax.all_gather(hidden, 'expert', axis=0, tiled=True)]
    all_to_all x0 -> x1, starting transfers between devices: none -> 6.33 us  [local(): lax.all_to_all(copies, 'expert', split_axis=0, concat_axis=0, tiled=True)]
    all_to_all x1, waiting for transfers between devices: 104 us -> 110 us  [spread_slots(): lax.all_to_all(pieces, 'expert', split_axis=0, concat_axis=0, tiled=True)]
    unnamed x67 -> x69, local copies, waits for them, and re-layouts: 14.2 us -> 11.8 us
  transfers between devices with their start and end apart: 4 -> 5, of which waited for: 4 -> 4; matrix products, arithmetic and copies ran while one was open for 31% -> 34% of each run, Pallas kernels for 0% -> 0%
where the time goes in v8:
time: 385 us; the launch traced here: 383 us
  waiting for transfers between devices  129 us (34%)
  other arithmetic  62.8 us (16%)
  local copies, waits for them, and re-layouts  61.9 us (16%)
  blocking collectives  55 us (14%)
  matrix products  31 us (8%)
  between operations  23 us (6%)
  starting transfers between devices  19.6 us (5%)
    all_to_all x1, waiting for transfers between devices, spread_slots(): lax.all_to_all(pieces, 'expert', split_axis=0, concat_axis=0, tiled=True)  110 us
    all_gather x1, blocking collectives, local(): lax.all_gather(partial_value, 'expert', axis=0, tiled=False)  15 us
    all_gather x1, blocking collectives, sum_over(): return jnp.sum(lax.all_gather(values, axis, axis=0, tiled=False), axis=0)  12.6 us
    unnamed x69, local copies, waits for them, and re-layouts  11.8 us
    sub x1, other arithmetic, local(): local_slot = slot_of - ex_index * slots_local  10.7 us
    all_gather x1, blocking collectives, local(): gathered = lax.all_gather(packed, 'dp', axis=0, tiled=False)  10.3 us
    mul x1, other arithmetic, local(): base_gate_up = expert_gate_up * unit  10.3 us
    all_to_all x1, waiting for transfers between devices, deliver(): lax.all_to_all(outgoing, 'expert', split_axis=0, concat_axis=0, tiled=True)  10.1 us
  transfers between devices with their start and end apart: 5, of which 4 were waited for; matrix products, arithmetic and copies ran while one was open for 34% of the time, Pallas kernels for 0%

profile of v8, /device:TPU:0, one launch (start us, length us, event | category | flops | bytes accessed | tf_op | source)
XLA Modules:
  0.0 382.7 jit_solution(3039016485924183188)
XLA Ops:
  10.1 6.3 %all-to-all-start.1 = ((bf16[8,2,1024]{2,1,0:T(2,128)(2,1)}), bf16[8,2,1024]{2,1,0:T(2,128)(2,1)S(1)}, u32[]{:S(2)}, u32[]{:S(2)}) async-start(bf16[8,2,1024]{2,1,0:T(2,128)(2,1)} %reshape.669), calls=%async_computation.1 | async-start | bytes 65536 | tf_op jit(solution)/shard_map/all_to_all | solution.py:162
  26.8 2.1 constant_dynamic-slice_fusion.9
  28.9 3.1 constant_dynamic-slice_fusion.11
  32.3 3.9 %pad_maximum_fusion.2 = bf16[2,3,1408,512]{3,2,1,0:T(8,128)(2,1)} fusion(bf16[2,1,1408,512]{3,2,1,0:T(8,128)(2,1)S(1)} %maximum_bitcast_fusion.1, bf16[1,2,1408,512]{3,2,1,0:T(8,128)(2,1)S(1)} %get-tuple-element.121, bf16[1,2,1408,512]{3,2,1,0:T(8,128)(2,1)S(1)} %get-tuple-element.120), kind=kLoop, calls=%fused_computation.21 | loop fusion | flops 8650752 | bytes 17301504 | tf_op jit(solution)/shard_map/concatenate | solution.py:51
  36.8 7.6 %copy.215 = bf16[8,2,3,176,512]{4,3,2,1,0:T(8,128)(2,1)} copy(bf16[8,2,3,176,512]{4,3,0,2,1:T(8,128)(2,1)} %bitcast.232) | data formatting | bytes 17301504 | tf_op jit(solution)/shard_map/transpose | solution.py:57
  44.4 5.2 %all-to-all-start.2 = ((bf16[8,2,3,176,512]{4,3,2,1,0:T(8,128)(2,1)}), bf16[8,2,3,176,512]{4,3,2,1,0:T(8,128)(2,1)}, u32[]{:S(2)}, u32[]{:S(2)}) async-start(bf16[8,2,3,176,512]{4,3,2,1,0:T(8,128)(2,1)} %copy.215), calls=%async_computation.2 | async-start | bytes 17301504 | tf_op jit(solution)/shard_map/all_to_all | solution.py:58
  50.6 1.3 copy.204
  54.1 2.4 scatter_custom_fusion
  59.9 8.7 %all_gather.30 = bf16[32,2048]{1,0:T(8,128)(2,1)S(1)} all-gather(bf16[8,2048]{1,0:T(8,128)(2,1)} %bitcast.247), channel_id=1, replica_groups=mesh['dp'=4,'expert'=8] {'dp'}, dimensions={0}, use_global_device_ids=true | all-gather | bytes 163840 | tf_op jit(solution)/shard_map/all_gather | solution.py:166
  70.1 2.6 fusion.95
  72.7 1.5 reshape.461
  76.6 2.3 gather_fusion.1
  80.5 1.3 gather_fusion.2
  81.8 1.6 fusion.5
  83.4 1.9 fusion.94
  87.2 1.4 select_reduce_fusion.1
  89.3 1.3 gather_fusion.3
  92.3 1.4 convolution_bitcast_fusion.3
  93.8 1.4 copy.211
  95.2 1.3 copy.210
  96.5 1.6 convolution_multiply_fusion
  99.9 10.3 %all-gather = f32[128,2,514]{2,0,1:T(8,128)S(1)} all-gather(f32[32,2,514]{2,0,1:T(8,128)S(1)} %pad_maximum_fusion.3), channel_id=2, replica_groups=mesh['dp'=4,'expert'=8] {'dp'}, dimensions={0}, use_global_device_ids=true | all-gather | bytes 657920 | tf_op jit(solution)/shard_map/all_gather | solution.py:219
  111.7 2.5 copy.239
  114.2 1.5 fusion.88
  116.5 3.0 multiply_reduce_fusion
  121.2 2.4 fusion.25
  128.0 1.8 fusion.7
  129.7 109.5 %all-to-all-done.2 = bf16[8,2,3,176,512]{4,3,2,1,0:T(8,128)(2,1)} async-done(((bf16[8,2,3,176,512]{4,3,2,1,0:T(8,128)(2,1)}), bf16[8,2,3,176,512]{4,3,2,1,0:T(8,128)(2,1)}, u32[]{:S(2)}, u32[]{:S(2)}) %all-to-all-start.2) | async-done | bytes 8650784 | tf_op jit(solution)/shard_map/all_to_all | solution.py:58
  239.3 15.0 %all-gather.1 = f32[64,2048]{1,0:T(8,128)S(1)} all-gather(f32[8,2048]{1,0:T(8,128)S(1)} %fusion.7), channel_id=3, replica_groups=mesh['dp'=4,'expert'=8] {'expert'}, dimensions={0}, use_global_device_ids=true | all-gather | bytes 589824 | tf_op jit(solution)/shard_map/all_gather | solution.py:253
  254.4 6.4 %gather_fusion.4 = bf16[8,3,176,512]{3,2,1,0:T(8,128)(2,1)} fusion(bf16[16,3,176,512]{3,2,1,0:T(8,128)(2,1)} %bitcast.33, s32[1024]{0:T(1024)} %pad_clamp_fusion.1), kind=kCustom, calls=%fused_computation.4 | custom fusion | bytes 8650784 | tf_op jit(solution)/shard_map/jit(_take)/gather | solution.py:113
  261.7 4.6 %all-to-all-start.3 = ((bf16[8,3,176,512]{3,2,1,0:T(8,128)(2,1)}), bf16[8,3,176,512]{3,2,1,0:T(8,128)(2,1)}, u32[]{:S(2)}, u32[]{:S(2)}) async-start(bf16[8,3,176,512]{3,2,1,0:T(8,128)(2,1)} %get-tuple-element.165), calls=%async_computation.3 | async-start | bytes 8650752 | tf_op jit(solution)/shard_map/all_to_all | solution.py:127
  268.3 4.5 %compare_select_fusion.5 = (s32[192,1]{0,1:T(1,128)S(1)}, s32[192,1]{0,1:T(1,128)S(1)}) fusion(s32[]{:T(128)} %bitcast.53, s32[]{:T(128)} %bitcast.54, s32[]{:T(128)} %bitcast.55, s32[]{:T(128)} %bitcast.56, s32[]{:T(128)} %bitcast.57, s32[]{:T(128)} %bitcast.59, s32[]{:T(128)} %bitcast.58, s32[192,1]{0,1:T(1,128)S(1)} %copy-done.18), kind=kLoop, calls=%fused_computation.185 | loop fusion | flops 2880 | bytes 2332 | tf_op jit(solution)/shard_map/gather | solution.py:289
  272.9 10.7 %select_subtract_fusion = s32[192]{0:T(256)S(1)} fusion(pred[192]{0:T(512)(128)(4,1)S(1)} %get-tuple-element.102, pred[192]{0:T(512)(128)(4,1)S(1)} %get-tuple-element.101, pred[192]{0:T(512)(128)(4,1)S(1)} %get-tuple-element.100, pred[192]{0:T(512)(128)(4,1)S(1)} %get-tuple-element.99, pred[192]{0:T(512)(128)(4,1)S(1)} %get-tuple-element.98, ...), kind=kLoop, calls=%fused_computation.216 | loop fusion | flops 3456 | bytes 4872 | tf_op jit(solution)/shard_map/sub | solution.py:291
  283.7 1.2 reduce-window.6
  285.8 8.5 %all_gather.35 = bf16[32,2048]{1,0:T(8,128)(2,1)S(1)} all-gather(bf16[8,2048]{1,0:T(8,128)(2,1)S(1)} %multiply_convert_fusion), channel_id=1, replica_groups=mesh['dp'=4,'expert'=8] {'dp'}, dimensions={0}, use_global_device_ids=true | all-gather | bytes 163840 | tf_op jit(solution)/shard_map/all_gather | solution.py:263
  294.4 6.9 %convolution_bitcast_fusion.1 = f32[4,2,16,1408]{3,2,1,0:T(8,128)} fusion(bf16[4,2,1408,512]{3,2,1,0:T(8,128)(2,1)} %param.34, bf16[32,512,1]{1,0,2:T(8,128)(2,1)S(1)} %reshape.635, bf16[32,4,16]{0,2,1:T(8,128)(2,1)S(1)} %get-tuple-element.82), kind=kOutput, calls=%fused_computation.28 | convolution fusion | flops 186679296 | bytes 12292096 | tf_op jit(solution)/shard_map/scd,sgfd->sgcf/dot_general | solution.py:304
  304.3 4.2 %convolution_bitcast_fusion = f32[2,4,2816]{2,1,0:T(4,128)S(1)} fusion(bf16[2,2816,512]{2,1,0:T(8,128)(2,1)} %param.36, bf16[4,1,1,512]{3,1,0,2:T(2,128)(2,1)S(1)} %constant_dynamic-slice_fusion.6), kind=kOutput, calls=%fused_computation.23 | convolution fusion | flops 23068672 | bytes 5861376 | tf_op jit(solution)/shard_map/td,gfd->gtf/dot_general | solution.py:307
  308.6 12.6 %all-gather.3 = f32[8,4,2816]{2,1,0:T(4,128)S(1)} all-gather(f32[2,4,2816]{2,1,0:T(4,128)S(1)} %convolution_bitcast_fusion), channel_id=5, replica_groups=mesh['dp'=4,'expert'=8] {'dp'}, dimensions={0}, use_global_device_ids=true | all-gather | bytes 450560 | tf_op jit(solution)/shard_map/all_gather | solution.py:71
  321.9 5.5 %broadcast_multiply_fusion.1 = bf16[4,1408,512]{2,1,0:T(8,128)(2,1)} fusion(bf16[4,1408,512]{2,1,0:T(8,128)(2,1)} %param.35, bf16[]{:T(256)} %bitcast.82), kind=kLoop, calls=%fused_computation.26 | loop fusion | flops 2883584 | bytes 11534338 | tf_op jit(solution)/shard_map/mul | solution.py:266
  327.5 10.3 %broadcast_multiply_fusion = bf16[4,2,1408,512]{3,2,1,0:T(8,128)(2,1)} fusion(bf16[4,2,1408,512]{3,2,1,0:T(8,128)(2,1)} %param.34, bf16[]{:T(256)} %bitcast.82), kind=kLoop, calls=%fused_computation.22 | loop fusion | flops 5767168 | bytes 23068674 | tf_op jit(solution)/shard_map/mul | solution.py:265
  337.8 8.2 %all-gather.6.cloned.1.call-done = f32[16,2,16,1408]{3,2,1,0:T(8,128)} async-done(((f32[4,2,16,1408]{3,2,1,0:T(8,128)}), f32[16,2,16,1408]{3,2,1,0:T(8,128)}) %all-gather.6.cloned.1.call-update) | async-done | bytes 2883600 | tf_op jit(solution)/shard_map/all_gather | solution.py:71
  346.0 2.9 reduce_sum.167
  348.9 3.7 fusion.17
  352.9 10.1 %all-to-all-done.3 = bf16[8,3,176,512]{3,2,1,0:T(8,128)(2,1)} async-done(((bf16[8,3,176,512]{3,2,1,0:T(8,128)(2,1)}), bf16[8,3,176,512]{3,2,1,0:T(8,128)(2,1)}, u32[]{:S(2)}, u32[]{:S(2)}) %all-to-all-start.3) | async-done | bytes 4325408 | tf_op jit(solution)/shard_map/all_to_all | solution.py:127
  364.3 3.5 all-to-all-start.4
  367.8 3.6 copy_dynamic-update-slice_fusion
  371.4 2.6 bitcast_dynamic-update-slice_fusion
  374.0 1.2 all-to-all-done.4
  (187 shorter events, 42.2 us)
Async XLA Ops:
  7.2 355.9 %copy-start = (bf16[2816,512]{1,0:T(8,128)(2,1)S(1)}, bf16[2816,512]{1,0:T(8,128)(2,1)}, u32[]{:S(2)}) copy-start(bf16[2816,512]{1,0:T(8,128)(2,1)} %param.37) | copy-start | bytes 8650756
  10.1 26.1 %all-to-all-start.1 = ((bf16[8,2,1024]{2,1,0:T(2,128)(2,1)}), bf16[8,2,1024]{2,1,0:T(2,128)(2,1)S(1)}, u32[]{:S(2)}, u32[]{:S(2)}) async-start(bf16[8,2,1024]{2,1,0:T(2,128)(2,1)} %reshape.669), calls=%async_computation.1 | async-start | bytes 65536 | tf_op jit(solution)/shard_map/all_to_all | solution.py:162
  17.3 1.7 copy-start.24
  18.0 1.0 copy-start.22
  21.8 0.5 copy-start.13
  44.4 5.3 %copy-start.19 = (s32[32,6]{0,1:T(8,128)S(1)}, s32[32,6]{0,1:T(8,128)}, u32[]{:S(2)}) copy-start(s32[32,6]{0,1:T(8,128)} %param.30) | copy-start | bytes 2308
  44.4 7.4 %copy-start.12 = (s32[32,16]{0,1:T(8,128)S(1)}, s32[32,16]{0,1:T(8,128)}, u32[]{:S(2)}) copy-start(s32[32,16]{0,1:T(8,128)} %param.27) | copy-start | bytes 6148
  44.4 9.1 %copy-start.28 = (s32[32]{0:T(128)S(1)}, s32[32]{0:T(128)}, u32[]{:S(2)}) copy-start(s32[32]{0:T(128)} %param.28) | copy-start | bytes 388
  44.4 194.8 %all-to-all-start.2 = ((bf16[8,2,3,176,512]{4,3,2,1,0:T(8,128)(2,1)}), bf16[8,2,3,176,512]{4,3,2,1,0:T(8,128)(2,1)}, u32[]{:S(2)}, u32[]{:S(2)}) async-start(bf16[8,2,3,176,512]{4,3,2,1,0:T(8,128)(2,1)} %copy.215), calls=%async_computation.2 | async-start | bytes 17301504 | tf_op jit(solution)/shard_map/all_to_all | solution.py:58
  51.9 59.9 %copy-start.1 = (bf16[512,512]{0,1:T(8,128)(2,1)}, bf16[512,512]{0,1:T(8,128)(2,1)S(1)}, u32[]{:S(2)}) copy-start(bf16[512,512]{0,1:T(8,128)(2,1)S(1)} %copy.204) | copy-start | bytes 1572868
  56.5 2.6 copy-start.21
  57.1 11.6 %copy-start.11 = (s32[32]{0:T(128)}, s32[32]{0:T(128)S(1)}, u32[]{:S(2)}) copy-start(s32[32]{0:T(128)S(1)} %get-tuple-element.111) | copy-start | bytes 388
  57.7 11.0 %copy-start.16 = (s32[8]{0:T(128)}, s32[8]{0:T(128)S(1)}, u32[]{:S(2)}) copy-start(s32[8]{0:T(128)S(1)} %broadcast_select_fusion.2) | copy-start | bytes 100
  57.9 10.6 %copy-start.26 = (s32[8]{0:T(128)}, s32[8]{0:T(128)S(1)}, u32[]{:S(2)}) copy-start(s32[8]{0:T(128)S(1)} %select_reduce_fusion.3) | copy-start | bytes 100
  69.5 0.6 copy-start.3
  75.2 0.6 copy-start.4
  79.8 0.6 copy-start.6
  79.8 0.6 copy-start.8
  85.3 0.6 copy-start.5
  110.2 0.8 copy-start.2
  110.2 14.2 %copy-start.7 = (bf16[32,2,32]{2,1,0:T(2,128)(2,1)S(1)}, bf16[32,2,32]{2,1,0:T(2,128)(2,1)}, u32[]{:S(2)}) copy-start(bf16[32,2,32]{2,1,0:T(2,128)(2,1)} %copy-done.6) | copy-start | bytes 12292
  115.7 0.6 copy-start.10
  115.8 0.6 copy-start.9
  254.4 6.5 %copy-start.14 = (s32[4]{0:T(128)S(1)}, s32[4]{0:T(128)}, u32[]{:S(2)}) copy-start(s32[4]{0:T(128)} %copy-done.13) | copy-start | bytes 52
  254.4 6.4 %copy-start.17 = (s32[8]{0:T(128)S(1)}, s32[8]{0:T(128)}, u32[]{:S(2)}) copy-start(s32[8]{0:T(128)} %copy-done.16) | copy-start | bytes 100
  254.4 6.4 %copy-start.27 = (s32[8]{0:T(128)S(1)}, s32[8]{0:T(128)}, u32[]{:S(2)}) copy-start(s32[8]{0:T(128)} %copy-done.26) | copy-start | bytes 100
  260.8 0.7 copy-start.15
  261.6 4.6 %copy-start.25 = (s32[32]{0:T(128)S(1)}, s32[32]{0:T(128)}, u32[]{:S(2)}) copy-start(s32[32]{0:T(128)} %copy-done.24) | copy-start | bytes 388
  261.6 6.7 %copy-start.18 = (s32[192,1]{0,1:T(1,128)S(1)}, s32[192,1]{0,1:T(1,128)}, u32[]{:S(2)}) copy-start(s32[192,1]{0,1:T(1,128)} %reshape_reshape.3) | copy-start | bytes 2308
  261.6 23.9 %copy-start.20 = (f32[32,6]{0,1:T(8,128)S(1)}, f32[32,6]{0,1:T(8,128)}, u32[]{:S(2)}) copy-start(f32[32,6]{0,1:T(8,128)} %param.31) | copy-start | bytes 2308
  261.7 101.4 %all-to-all-start.3 = ((bf16[8,3,176,512]{3,2,1,0:T(8,128)(2,1)}), bf16[8,3,176,512]{3,2,1,0:T(8,128)(2,1)}, u32[]{:S(2)}, u32[]{:S(2)}) async-start(bf16[8,3,176,512]{3,2,1,0:T(8,128)(2,1)} %get-tuple-element.165), calls=%async_computation.3 | async-start | bytes 8650752 | tf_op jit(solution)/shard_map/all_to_all | solution.py:127
  266.2 79.8 %all-gather.6.cloned.1.call-start = ((), (), s32[]{:S(2)}) async-start(), calls=%async_computation.5 | async-start | bytes 3604480 | tf_op jit(solution)/shard_map/all_gather | solution.py:71
  294.4 6.9 %copy-start.23 = (s32[8]{0:T(128)S(1)}, s32[8]{0:T(128)}, u32[]{:S(2)}) copy-start(s32[8]{0:T(128)} %copy-done.22) | copy-start | bytes 100
  364.3 10.9 %all-to-all-start.4 = ((f32[32,1,512]{2,1,0:T(1,128)}), f32[32,1,512]{2,1,0:T(1,128)S(1)}, u32[]{:S(2)}, u32[]{:S(2)}) async-start(f32[32,1,512]{2,1,0:T(1,128)} %copy.225), calls=%async_computation.4 | async-start | bytes 131072 | tf_op jit(solution)/shard_map/all_to_all | solution.py:324
Sparse Core Ops, SparseCore 0:
  301.4 44.5 all-gather.5

commit v9 on v8

--- a/solution.py
+++ b/solution.py
@@ -312,15 +312,19 @@
     slot_out = jnp.einsum(
         "scf,sfd->scd", activated, expert_down, preferred_element_type=jnp.float32
     )
-    routed = jnp.einsum("tsc,scd->td", combine, slot_out, precision=HIGHEST)
+    combine_tok = combine.reshape((ex_count, dp_count, req_local) + combine.shape[1:])
+    combine_tok = combine_tok.transpose(1, 0, 2, 3, 4).reshape(combine.shape)
+    routed = jnp.einsum("tsc,scd->td", combine_tok, slot_out, precision=HIGHEST)
     shared_act = (jax.nn.silu(shared_sum[0]) * shared_sum[1]).astype(jnp.bfloat16)
     shared_term = jnp.dot(shared_act, shared_down, preferred_element_type=jnp.float32)
     routed, arrived = lax.optimization_barrier((routed, arrived))
-    shared_at = ex_index * dp_count * req_local
-    own_block = lax.dynamic_slice_in_dim(routed, shared_at, dp_count * req_local, 0) + shared_term
-    routed = lax.dynamic_update_slice_in_dim(routed, own_block, shared_at, 0)
-    by_token = routed.reshape(ex_count, dp_count, req_local, col_width).transpose(1, 0, 2, 3)
-    by_token = by_token.reshape(requests, col_width)
+    token_ids = jnp.arange(requests, dtype=jnp.int32)
+    token_ex = (token_ids // req_local) % ex_count
+    token_slot = (token_ids // (req_local * ex_count)) * req_local + token_ids % req_local
+    owns = (token_ex == ex_index)[:, None] & (
+        token_slot[:, None] == jnp.arange(dp_count * req_local, dtype=jnp.int32)[None, :]
+    )
+    by_token = routed + jnp.dot(owns.astype(jnp.float32), shared_term, precision=HIGHEST)
     received = lax.all_to_all(by_token, ("dp", "expert"), split_axis=0, concat_axis=0, tiled=True)
     moe_cols = jnp.sum(received.reshape(dp_count, ex_count, req_local, col_width), axis=1)
     moe_part = moe_cols.transpose(1, 0, 2).reshape(req_local, dp_count * col_width)

time: 385 us -> 385 us (level)
    unnamed x69 -> x73, local copies, waits for them, and re-layouts: 11.8 us -> 11.8 us
  transfers between devices with their start and end apart: 5 -> 5, of which waited for: 4 -> 4; matrix products, arithmetic and copies ran while one was open for 34% -> 35% of each run, Pallas kernels for 0% -> 0%
where the time goes in v9:
time: 385 us; the launch traced here: 382 us
  waiting for transfers between devices  128 us (33%)
  other arithmetic  63 us (16%)
  local copies, waits for them, and re-layouts  62.6 us (16%)
  blocking collectives  55 us (14%)
  matrix products  31.2 us (8%)
  between operations  23 us (6%)
  starting transfers between devices  19.5 us (5%)
    all_to_all x1, waiting for transfers between devices, spread_slots(): lax.all_to_all(pieces, 'expert', split_axis=0, concat_axis=0, tiled=True)  108 us
    all_gather x1, blocking collectives, local(): lax.all_gather(partial_value, 'expert', axis=0, tiled=False)  15 us
    all_gather x1, blocking collectives, sum_over(): return jnp.sum(lax.all_gather(values, axis, axis=0, tiled=False), axis=0)  12.6 us
    unnamed x73, local copies, waits for them, and re-layouts  11.8 us
    sub x1, other arithmetic, local(): local_slot = slot_of - ex_index * slots_local  10.7 us
    all_to_all x1, waiting for transfers between devices, deliver(): lax.all_to_all(outgoing, 'expert', split_axis=0, concat_axis=0, tiled=True)  10.4 us
    all_gather x1, blocking collectives, local(): gathered = lax.all_gather(packed, 'dp', axis=0, tiled=False)  10.3 us
    mul x1, other arithmetic, local(): base_gate_up = expert_gate_up * unit  10.1 us
  transfers between devices with their start and end apart: 5, of which 4 were waited for; matrix products, arithmetic and copies ran while one was open for 35% of the time, Pallas kernels for 0%

profile of v9, /device:TPU:0, one launch (start us, length us, event | category | flops | bytes accessed | tf_op | source)
XLA Modules:
  0.0 382.2 jit_solution(17064032614242339189)
XLA Ops:
  10.1 6.3 %all-to-all-start.1 = ((bf16[8,2,1024]{2,1,0:T(2,128)(2,1)}), bf16[8,2,1024]{2,1,0:T(2,128)(2,1)S(1)}, u32[]{:S(2)}, u32[]{:S(2)}) async-start(bf16[8,2,1024]{2,1,0:T(2,128)(2,1)} %reshape.695), calls=%async_computation.1 | async-start | bytes 65536 | tf_op jit(solution)/shard_map/all_to_all | solution.py:162
  26.8 2.1 constant_dynamic-slice_fusion.9
  29.0 3.1 constant_dynamic-slice_fusion.11
  32.3 3.9 %pad_maximum_fusion.2 = bf16[2,3,1408,512]{3,2,1,0:T(8,128)(2,1)} fusion(bf16[2,1,1408,512]{3,2,1,0:T(8,128)(2,1)S(1)} %maximum_bitcast_fusion.1, bf16[1,2,1408,512]{3,2,1,0:T(8,128)(2,1)S(1)} %get-tuple-element.121, bf16[1,2,1408,512]{3,2,1,0:T(8,128)(2,1)S(1)} %get-tuple-element.120), kind=kLoop, calls=%fused_computation.21 | loop fusion | flops 8650752 | bytes 17301504 | tf_op jit(solution)/shard_map/concatenate | solution.py:51
  36.9 7.6 %copy.223 = bf16[8,2,3,176,512]{4,3,2,1,0:T(8,128)(2,1)} copy(bf16[8,2,3,176,512]{4,3,0,2,1:T(8,128)(2,1)} %bitcast.235) | data formatting | bytes 17301504 | tf_op jit(solution)/shard_map/transpose | solution.py:57
  44.4 5.1 %all-to-all-start.2 = ((bf16[8,2,3,176,512]{4,3,2,1,0:T(8,128)(2,1)}), bf16[8,2,3,176,512]{4,3,2,1,0:T(8,128)(2,1)}, u32[]{:S(2)}, u32[]{:S(2)}) async-start(bf16[8,2,3,176,512]{4,3,2,1,0:T(8,128)(2,1)} %copy.223), calls=%async_computation.2 | async-start | bytes 17301504 | tf_op jit(solution)/shard_map/all_to_all | solution.py:58
  49.6 1.3 copy.212
  54.9 2.4 scatter_custom_fusion
  61.3 8.7 %all_gather.30 = bf16[32,2048]{1,0:T(8,128)(2,1)S(1)} all-gather(bf16[8,2048]{1,0:T(8,128)(2,1)} %bitcast.250), channel_id=1, replica_groups=mesh['dp'=4,'expert'=8] {'dp'}, dimensions={0}, use_global_device_ids=true | all-gather | bytes 163840 | tf_op jit(solution)/shard_map/all_gather | solution.py:166
  71.5 2.6 fusion.103
  74.1 1.5 reshape.486
  78.0 2.3 gather_fusion.1
  81.9 1.3 gather_fusion.2
  83.2 1.6 fusion.5
  84.8 1.9 fusion.102
  88.6 1.4 select_reduce_fusion.1
  90.7 1.3 gather_fusion.3
  93.7 1.4 convolution_bitcast_fusion.3
  95.2 1.4 copy.219
  96.6 1.3 copy.218
  97.9 1.6 convolution_multiply_fusion
  101.3 10.3 %all-gather = f32[128,2,514]{2,0,1:T(8,128)S(1)} all-gather(f32[32,2,514]{2,0,1:T(8,128)S(1)} %pad_maximum_fusion.3), channel_id=2, replica_groups=mesh['dp'=4,'expert'=8] {'dp'}, dimensions={0}, use_global_device_ids=true | all-gather | bytes 657920 | tf_op jit(solution)/shard_map/all_gather | solution.py:219
  113.1 2.5 copy.250
  115.6 1.5 fusion.96
  117.8 3.0 multiply_reduce_fusion
  122.6 2.4 fusion.27
  129.4 1.8 fusion.7
  131.1 108.0 %all-to-all-done.2 = bf16[8,2,3,176,512]{4,3,2,1,0:T(8,128)(2,1)} async-done(((bf16[8,2,3,176,512]{4,3,2,1,0:T(8,128)(2,1)}), bf16[8,2,3,176,512]{4,3,2,1,0:T(8,128)(2,1)}, u32[]{:S(2)}, u32[]{:S(2)}) %all-to-all-start.2) | async-done | bytes 8650784 | tf_op jit(solution)/shard_map/all_to_all | solution.py:58
  239.1 15.0 %all-gather.1 = f32[64,2048]{1,0:T(8,128)S(1)} all-gather(f32[8,2048]{1,0:T(8,128)S(1)} %fusion.7), channel_id=3, replica_groups=mesh['dp'=4,'expert'=8] {'expert'}, dimensions={0}, use_global_device_ids=true | all-gather | bytes 589824 | tf_op jit(solution)/shard_map/all_gather | solution.py:253
  254.3 6.4 %gather_fusion.4 = bf16[8,3,176,512]{3,2,1,0:T(8,128)(2,1)} fusion(bf16[16,3,176,512]{3,2,1,0:T(8,128)(2,1)} %bitcast.33, s32[1024]{0:T(1024)} %pad_clamp_fusion.1), kind=kCustom, calls=%fused_computation.4 | custom fusion | bytes 8650784 | tf_op jit(solution)/shard_map/jit(_take)/gather | solution.py:113
  261.5 4.6 %all-to-all-start.3 = ((bf16[8,3,176,512]{3,2,1,0:T(8,128)(2,1)}), bf16[8,3,176,512]{3,2,1,0:T(8,128)(2,1)}, u32[]{:S(2)}, u32[]{:S(2)}) async-start(bf16[8,3,176,512]{3,2,1,0:T(8,128)(2,1)} %get-tuple-element.167), calls=%async_computation.3 | async-start | bytes 8650752 | tf_op jit(solution)/shard_map/all_to_all | solution.py:127
  268.2 4.5 %compare_select_fusion.5 = (s32[192,1]{0,1:T(1,128)S(1)}, s32[192,1]{0,1:T(1,128)S(1)}) fusion(s32[]{:T(128)} %bitcast.53, s32[]{:T(128)} %bitcast.54, s32[]{:T(128)} %bitcast.55, s32[]{:T(128)} %bitcast.56, s32[]{:T(128)} %bitcast.57, s32[]{:T(128)} %bitcast.59, s32[]{:T(128)} %bitcast.58, s32[192,1]{0,1:T(1,128)S(1)} %copy-done.19), kind=kLoop, calls=%fused_computation.191 | loop fusion | flops 2880 | bytes 2332 | tf_op jit(solution)/shard_map/gather | solution.py:289
  272.7 10.7 %select_subtract_fusion = s32[192]{0:T(256)S(1)} fusion(pred[192]{0:T(512)(128)(4,1)S(1)} %get-tuple-element.100, pred[192]{0:T(512)(128)(4,1)S(1)} %get-tuple-element.99, pred[192]{0:T(512)(128)(4,1)S(1)} %get-tuple-element.98, pred[192]{0:T(512)(128)(4,1)S(1)} %get-tuple-element.97, pred[192]{0:T(512)(128)(4,1)S(1)} %get-tuple-element.96, ...), kind=kLoop, calls=%fused_computation.224 | loop fusion | flops 3456 | bytes 4872 | tf_op jit(solution)/shard_map/sub | solution.py:291
  283.5 1.2 reduce-window.6
  285.4 8.5 %all_gather.35 = bf16[32,2048]{1,0:T(8,128)(2,1)S(1)} all-gather(bf16[8,2048]{1,0:T(8,128)(2,1)S(1)} %multiply_convert_fusion), channel_id=1, replica_groups=mesh['dp'=4,'expert'=8] {'dp'}, dimensions={0}, use_global_device_ids=true | all-gather | bytes 163840 | tf_op jit(solution)/shard_map/all_gather | solution.py:263
  293.9 6.9 %convolution_bitcast_fusion.1 = f32[4,2,16,1408]{3,2,1,0:T(8,128)} fusion(bf16[4,2,1408,512]{3,2,1,0:T(8,128)(2,1)} %param.34, bf16[32,512,1]{1,0,2:T(8,128)(2,1)S(1)} %reshape.661, bf16[32,4,16]{0,2,1:T(8,128)(2,1)S(1)} %get-tuple-element.83), kind=kOutput, calls=%fused_computation.28 | convolution fusion | flops 186679296 | bytes 12292096 | tf_op jit(solution)/shard_map/scd,sgfd->sgcf/dot_general | solution.py:304
  304.0 4.2 %convolution_bitcast_fusion = f32[2,4,2816]{2,1,0:T(4,128)S(1)} fusion(bf16[2,2816,512]{2,1,0:T(8,128)(2,1)} %param.36, bf16[4,1,1,512]{3,1,0,2:T(2,128)(2,1)S(1)} %constant_dynamic-slice_fusion.6), kind=kOutput, calls=%fused_computation.23 | convolution fusion | flops 23068672 | bytes 5861376 | tf_op jit(solution)/shard_map/td,gfd->gtf/dot_general | solution.py:307
  308.2 12.6 %all-gather.3 = f32[8,4,2816]{2,1,0:T(4,128)S(1)} all-gather(f32[2,4,2816]{2,1,0:T(4,128)S(1)} %convolution_bitcast_fusion), channel_id=5, replica_groups=mesh['dp'=4,'expert'=8] {'dp'}, dimensions={0}, use_global_device_ids=true | all-gather | bytes 450560 | tf_op jit(solution)/shard_map/all_gather | solution.py:71
  322.0 5.6 %broadcast_multiply_fusion.1 = bf16[4,1408,512]{2,1,0:T(8,128)(2,1)} fusion(bf16[4,1408,512]{2,1,0:T(8,128)(2,1)} %param.35, bf16[]{:T(256)} %bitcast.84), kind=kLoop, calls=%fused_computation.26 | loop fusion | flops 2883584 | bytes 11534338 | tf_op jit(solution)/shard_map/mul | solution.py:266
  327.5 10.1 %broadcast_multiply_fusion = bf16[4,2,1408,512]{3,2,1,0:T(8,128)(2,1)} fusion(bf16[4,2,1408,512]{3,2,1,0:T(8,128)(2,1)} %param.34, bf16[]{:T(256)} %bitcast.84), kind=kLoop, calls=%fused_computation.22 | loop fusion | flops 5767168 | bytes 23068674 | tf_op jit(solution)/shard_map/mul | solution.py:265
  337.6 8.0 %all-gather.6.cloned.1.call-done = f32[16,2,16,1408]{3,2,1,0:T(8,128)} async-done(((f32[4,2,16,1408]{3,2,1,0:T(8,128)}), f32[16,2,16,1408]{3,2,1,0:T(8,128)}) %all-gather.6.cloned.1.call-update) | async-done | bytes 2883600 | tf_op jit(solution)/shard_map/all_gather | solution.py:71
  345.6 2.9 reduce_sum.167
  348.5 3.7 fusion.17
  352.5 10.4 %all-to-all-done.3 = bf16[8,3,176,512]{3,2,1,0:T(8,128)(2,1)} async-done(((bf16[8,3,176,512]{3,2,1,0:T(8,128)(2,1)}), bf16[8,3,176,512]{3,2,1,0:T(8,128)(2,1)}, u32[]{:S(2)}, u32[]{:S(2)}) %all-to-all-start.3) | async-done | bytes 4325408 | tf_op jit(solution)/shard_map/all_to_all | solution.py:127
  363.8 3.5 all-to-all-start.4
  367.3 3.6 copy_dynamic-update-slice_fusion
  371.0 2.6 bitcast_dynamic-update-slice_fusion
  373.5 1.2 all-to-all-done.4
  (192 shorter events, 43.7 us)
Async XLA Ops:
  7.2 314.3 %copy-start = (bf16[2816,512]{1,0:T(8,128)(2,1)S(1)}, bf16[2816,512]{1,0:T(8,128)(2,1)}, u32[]{:S(2)}) copy-start(bf16[2816,512]{1,0:T(8,128)(2,1)} %param.37) | copy-start | bytes 8650756
  10.1 26.1 %all-to-all-start.1 = ((bf16[8,2,1024]{2,1,0:T(2,128)(2,1)}), bf16[8,2,1024]{2,1,0:T(2,128)(2,1)S(1)}, u32[]{:S(2)}, u32[]{:S(2)}) async-start(bf16[8,2,1024]{2,1,0:T(2,128)(2,1)} %reshape.695), calls=%async_computation.1 | async-start | bytes 65536 | tf_op jit(solution)/shard_map/all_to_all | solution.py:162
  17.3 1.7 copy-start.25
  18.0 1.0 copy-start.23
  21.8 0.5 copy-start.14
  44.4 6.5 %copy-start.13 = (s32[32,16]{0,1:T(8,128)S(1)}, s32[32,16]{0,1:T(8,128)}, u32[]{:S(2)}) copy-start(s32[32,16]{0,1:T(8,128)} %param.27) | copy-start | bytes 6148
  44.4 8.1 %copy-start.20 = (f32[32,6]{0,1:T(8,128)S(1)}, f32[32,6]{0,1:T(8,128)}, u32[]{:S(2)}) copy-start(f32[32,6]{0,1:T(8,128)} %param.31) | copy-start | bytes 2308
  44.4 9.0 %copy-start.21 = (s32[32,6]{0,1:T(8,128)S(1)}, s32[32,6]{0,1:T(8,128)}, u32[]{:S(2)}) copy-start(s32[32,6]{0,1:T(8,128)} %param.30) | copy-start | bytes 2308
  44.4 9.9 %copy-start.30 = (s32[32]{0:T(128)S(1)}, s32[32]{0:T(128)}, u32[]{:S(2)}) copy-start(s32[32]{0:T(128)} %param.28) | copy-start | bytes 388
  44.4 194.7 %all-to-all-start.2 = ((bf16[8,2,3,176,512]{4,3,2,1,0:T(8,128)(2,1)}), bf16[8,2,3,176,512]{4,3,2,1,0:T(8,128)(2,1)}, u32[]{:S(2)}, u32[]{:S(2)}) async-start(bf16[8,2,3,176,512]{4,3,2,1,0:T(8,128)(2,1)} %copy.223), calls=%async_computation.2 | async-start | bytes 17301504 | tf_op jit(solution)/shard_map/all_to_all | solution.py:58
  50.9 62.2 %copy-start.1 = (bf16[512,512]{0,1:T(8,128)(2,1)}, bf16[512,512]{0,1:T(8,128)(2,1)S(1)}, u32[]{:S(2)}) copy-start(bf16[512,512]{0,1:T(8,128)(2,1)S(1)} %copy.212) | copy-start | bytes 1572868
  57.3 3.2 copy-start.22
  57.9 12.1 %copy-start.12 = (s32[32]{0:T(128)}, s32[32]{0:T(128)S(1)}, u32[]{:S(2)}) copy-start(s32[32]{0:T(128)S(1)} %get-tuple-element.113) | copy-start | bytes 388
  59.1 10.9 %copy-start.17 = (s32[8]{0:T(128)}, s32[8]{0:T(128)S(1)}, u32[]{:S(2)}) copy-start(s32[8]{0:T(128)S(1)} %broadcast_select_fusion.2) | copy-start | bytes 100
  59.3 1.2 copy-start.28
  70.9 0.6 copy-start.3
  76.6 0.6 copy-start.4
  81.2 0.6 copy-start.6
  81.2 0.6 copy-start.8
  86.7 0.6 copy-start.5
  111.6 0.8 copy-start.2
  111.6 14.2 %copy-start.7 = (bf16[32,2,32]{2,1,0:T(2,128)(2,1)S(1)}, bf16[32,2,32]{2,1,0:T(2,128)(2,1)}, u32[]{:S(2)}) copy-start(bf16[32,2,32]{2,1,0:T(2,128)(2,1)} %copy-done.6) | copy-start | bytes 12292
  117.1 0.6 copy-start.10
  117.2 0.6 copy-start.9
  254.3 6.5 %copy-start.15 = (s32[4]{0:T(128)S(1)}, s32[4]{0:T(128)}, u32[]{:S(2)}) copy-start(s32[4]{0:T(128)} %copy-done.14) | copy-start | bytes 52
  254.3 6.4 %copy-start.18 = (s32[8]{0:T(128)S(1)}, s32[8]{0:T(128)}, u32[]{:S(2)}) copy-start(s32[8]{0:T(128)} %copy-done.17) | copy-start | bytes 100
  254.3 6.4 %copy-start.29 = (s32[8]{0:T(128)S(1)}, s32[8]{0:T(128)}, u32[]{:S(2)}) copy-start(s32[8]{0:T(128)} %copy-done.28) | copy-start | bytes 100
  260.7 0.7 copy-start.16
  261.5 4.6 %copy-start.26 = (s32[32]{0:T(128)S(1)}, s32[32]{0:T(128)}, u32[]{:S(2)}) copy-start(s32[32]{0:T(128)} %copy-done.25) | copy-start | bytes 388
  261.5 6.7 %copy-start.19 = (s32[192,1]{0,1:T(1,128)S(1)}, s32[192,1]{0,1:T(1,128)}, u32[]{:S(2)}) copy-start(s32[192,1]{0,1:T(1,128)} %reshape_reshape.3) | copy-start | bytes 2308
  261.5 23.8 %copy-start.11 = (f32[32,6]{0,1:T(8,128)S(1)}, f32[32,6]{0,1:T(8,128)}, u32[]{:S(2)}) copy-start(f32[32,6]{0,1:T(8,128)} %mul.322) | copy-start | bytes 2308
  261.5 101.4 %all-to-all-start.3 = ((bf16[8,3,176,512]{3,2,1,0:T(8,128)(2,1)}), bf16[8,3,176,512]{3,2,1,0:T(8,128)(2,1)}, u32[]{:S(2)}, u32[]{:S(2)}) async-start(bf16[8,3,176,512]{3,2,1,0:T(8,128)(2,1)} %get-tuple-element.167), calls=%async_computation.3 | async-start | bytes 8650752 | tf_op jit(solution)/shard_map/all_to_all | solution.py:127
  266.1 79.4 %all-gather.6.cloned.1.call-start = ((), (), s32[]{:S(2)}) async-start(), calls=%async_computation.5 | async-start | bytes 3604480 | tf_op jit(solution)/shard_map/all_gather | solution.py:71
  293.9 6.9 %copy-start.24 = (s32[8]{0:T(128)S(1)}, s32[8]{0:T(128)}, u32[]{:S(2)}) copy-start(s32[8]{0:T(128)} %copy-done.23) | copy-start | bytes 100
  348.5 14.5 %copy-start.27 = (s32[32]{0:T(128)S(1)}, s32[32]{0:T(128)}, u32[]{:S(2)}) copy-start(s32[32]{0:T(128)} %get-tuple-element.165) | copy-start | bytes 388
  363.8 10.9 %all-to-all-start.4 = ((f32[32,1,512]{2,1,0:T(1,128)}), f32[32,1,512]{2,1,0:T(1,128)S(1)}, u32[]{:S(2)}, u32[]{:S(2)}) async-start(f32[32,1,512]{2,1,0:T(1,128)} %copy.235), calls=%async_computation.4 | async-start | bytes 131072 | tf_op jit(solution)/shard_map/all_to_all | solution.py:328
Sparse Core Ops, SparseCore 0:
  300.9 44.5 all-gather.5
